TPU v7x, 512 devices: a whole 4x8x8 slice. The times are simulated.
512 devices in a mesh: atoms: 32 (over x_hi, z, core), loops: 16 (over x_lo, y).
Axes of the slice: x: 4 (x_hi: 2, x_lo: 2; x = x_hi * 2 + x_lo), y: 8, z: 8, core: 2. Of those that a mesh axis runs over, the one named last changes fastest.
Arguments:
- atom_site: int32 [131072], P('atoms'), may hold values from 0 to 262143, as said below
- loop_cells: int32 [3, 4096], P(None, 'loops'), may hold values from -200 to 199
- loop_burgers: int32 [4096], P('loops'), may hold values from 0 to 3
- loop_habit: int32 [4096], P('loops'), may hold values from 0 to 5
- loop_radius: float32 [4096], P('loops'), may hold values from 10 to 40
Outputs:
- log_intensity: float32 [64, 128, 128], P('loops', 'atoms')
Inputs may be any that keep to these rules, and one draw needn't show every extreme that they name: `atom_site`: site numbers are distinct; the first and the last site of the window are always occupied.
All inputs are finite; a program needn't handle non-finite values.
Results may differ from a plain program's by a relative error of at most 0.0003.
Values sent between devices are 32-bit elements; how exact they have to be, the bound alone decides.
No kernel may reach another device: no remote copies, remote signals or barrier semaphores. Data moves between devices by JAX's collectives and lax.ppermute only.
A program may use at most 64 MiB of HBM per device.

v0:
```python
import math

import jax
import jax.numpy as jnp
import numpy as np
from jax import lax
from jax.sharding import PartitionSpec as P

WIN_X = 32
WIN_Y = 32
QX = 128
QY = 128
QZ = 64


LATTICE = 2.8665
POISSON = 0.29
TWO_PI = 2.0 * math.pi
BURGERS_TABLE = np.array(
    [[1.0, 1.0, 1.0], [-1.0, 1.0, 1.0], [1.0, -1.0, 1.0], [1.0, 1.0, -1.0]]
) * (0.5 * LATTICE)
NORMAL_TABLE = (
    np.array(
        [
            [1.0, 1.0, 0.0],
            [1.0, -1.0, 0.0],
            [1.0, 0.0, 1.0],
            [1.0, 0.0, -1.0],
            [0.0, 1.0, 1.0],
            [0.0, 1.0, -1.0],
        ]
    )
    * 0.70710678
)


def lookup(index, table):
    columns = []
    for column in range(3):
        total = jnp.zeros(index.shape, jnp.float32)
        for entry in range(table.shape[0]):
            total = total + jnp.where(
                index == entry, jnp.float32(table[entry, column]), jnp.float32(0.0)
            )
        columns.append(total)
    return jnp.stack(columns)


def site_anchor(site):
    basis = site % 2
    cell = site // 2
    first = cell % WIN_X
    second = cell // WIN_X % WIN_Y
    third = cell // (WIN_X * WIN_Y)
    cells = jnp.stack([first, second, third]).astype(jnp.float32)
    return LATTICE * (cells + 0.5 * basis.astype(jnp.float32)[None, :])


def loop_centre(cells):
    return LATTICE * (cells.astype(jnp.float32) + 0.25)


def loop_field(anchor, centre, burgers, normal, radius):
    offset = anchor[:, None, :] - centre[:, :, None]
    radius_sq = (radius * radius)[:, None]
    distance_sq = jnp.sum(offset * offset, axis=0) + radius_sq
    unit_dir = offset * lax.rsqrt(distance_sq)[None]
    along_b = jnp.sum(burgers[:, :, None] * unit_dir, axis=0)
    along_n = jnp.sum(normal[:, :, None] * unit_dir, axis=0)
    burgers_normal = jnp.sum(burgers * normal, axis=0)[:, None]
    strength = radius_sq / (8.0 * (1.0 - POISSON) * distance_sq)
    field = (1.0 - 2.0 * POISSON) * (
        burgers[:, :, None] * along_n[None] + normal[:, :, None] * along_b[None]
    )
    field = field - burgers_normal[None] * unit_dir + 3.0 * unit_dir * (along_b * along_n)[None]
    return jnp.sum(strength[None] * field, axis=1)


def waves(first, count, total, centre):
    steps = first + jnp.arange(count, dtype=jnp.float32)
    return TWO_PI / LATTICE * (centre + (steps - total * 0.5 + 0.5) / QX)


def factor_block(xcosines, xsines, zcosines, zsines, ytable):
    ywidth = ytable.shape[1] // 2
    left_real = (
        zcosines[None, :, :] * xcosines[:, None, :] - zsines[None, :, :] * xsines[:, None, :]
    )
    left_imag = (
        zcosines[None, :, :] * xsines[:, None, :] + zsines[None, :, :] * xcosines[:, None, :]
    )
    left_pair = jnp.stack([left_real, left_imag], axis=2)
    product = jnp.einsum(
        "xzca,ad->xzcd",
        left_pair,
        ytable,
        precision=lax.Precision.HIGHEST,
        preferred_element_type=jnp.float32,
    )
    real_part = product[:, :, 0, :ywidth] - product[:, :, 1, ywidth:]
    imag_part = product[:, :, 0, ywidth:] + product[:, :, 1, :ywidth]
    return jnp.stack([real_part, imag_part], axis=1)


def phase_tables(position, xwaves, ywaves, zwaves):
    xangle = xwaves[:, None] * position[0][None, :]
    yangle = position[1][:, None] * ywaves[None, :]
    zangle = zwaves[:, None] * position[2][None, :]
    ytable = jnp.concatenate([jnp.cos(yangle), jnp.sin(yangle)], axis=1)
    return (jnp.cos(xangle), jnp.sin(xangle), jnp.cos(zangle), jnp.sin(zangle), ytable)


def body(atom_site, loop_cells, loop_burgers, loop_habit, loop_radius):
    anchor = site_anchor(atom_site)
    centre = loop_centre(loop_cells)
    burgers = lookup(loop_burgers, BURGERS_TABLE)
    normal = lookup(loop_habit, NORMAL_TABLE)
    loop_count = centre.shape[1]
    block_size = math.gcd(loop_count, 64)

    def add_block(number, running):
        begin = number * block_size
        return running + loop_field(
            anchor,
            lax.dynamic_slice_in_dim(centre, begin, block_size, 1),
            lax.dynamic_slice_in_dim(burgers, begin, block_size, 1),
            lax.dynamic_slice_in_dim(normal, begin, block_size, 1),
            lax.dynamic_slice_in_dim(loop_radius, begin, block_size, 0),
        )

    partial_field = lax.fori_loop(
        0, loop_count // block_size, add_block, jnp.zeros(anchor.shape, jnp.float32)
    )
    displacement = lax.psum(partial_field, "loops")
    position = anchor + displacement
    group_count = lax.axis_size("atoms")
    zrows = QZ // lax.axis_size("loops")
    atom_total = position.shape[1] * group_count
    zfirst = (lax.axis_index("loops") * zrows).astype(jnp.float32)
    zwaves = waves(zfirst, zrows, QZ, 0.0)
    ywaves = waves(jnp.float32(0.0), QY, QY, 1.0)
    xwaves = waves(jnp.float32(0.0), QX, QX, 1.0)
    xcosines, xsines, zcosines, zsines, ytable = phase_tables(position, xwaves, ywaves, zwaves)
    summed = lax.psum_scatter(
        factor_block(xcosines, xsines, zcosines, zsines, ytable),
        "atoms",
        scatter_dimension=0,
        tiled=True,
    )
    power = summed[:, 0] ** 2 + summed[:, 1] ** 2
    return jnp.log1p(jnp.transpose(power, (1, 0, 2)) / atom_total)


def solution(mesh):
    placed = (P("atoms"), P(None, "loops"), P("loops"), P("loops"), P("loops"))
    return jax.shard_map(
        body, mesh=mesh, in_specs=placed, out_specs=P("loops", "atoms", None), check_vma=False
    )
```

profile of v0, /device:TPU:1, one launch (start us, length us, event | category | flops | bytes accessed | tf_op | source)
XLA Modules:
  0.0 405.5 jit_solution(9753702923087607838)
XLA Ops:
  6.5 0.8 add_select_fusion.4
  7.3 0.7 fusion.25
  8.1 0.7 select_add_fusion.2
  8.8 0.7 select_add_fusion.7
  9.4 0.7 add_multiply_fusion
  10.2 16.8 %while.14 = (s32[]{:T(128)}, f32[3,4096]{1,0:T(4,128)S(1)}, f32[256]{0:T(256)}, f32[3,4096]{1,0:T(4,128)S(1)}, f32[3,256]{1,0:T(4,128)S(1)}, /*index=5*/f32[3,25...) while((s32[]{:T(128)}, f32[3,4096]{1,0:T(4,128)S(1)}, ...), condition=%wide.region_6.7_spmd.clone, body=%wide.region_0.6_spmd.clone.sunk | while | flops 17052036 | bytes 16084141 | solution.py:131
  10.3 0.4 fusion.41
  10.7 0.8 dynamic-slice_multiply_fusion.4
  11.8 0.8 fusion.42
  12.8 1.5 fusion.43
  14.5 0.4 fusion.41
  14.9 0.8 dynamic-slice_multiply_fusion.4
  16.0 0.8 fusion.42
  17.0 1.5 fusion.43
  18.7 0.4 fusion.41
  19.1 0.8 dynamic-slice_multiply_fusion.4
  20.2 0.8 fusion.42
  21.2 1.5 fusion.43
  22.9 0.4 fusion.41
  23.3 0.8 dynamic-slice_multiply_fusion.4
  24.4 0.8 fusion.42
  25.4 1.5 fusion.43
  27.0 50.9 %psum.7 = f32[3,4096]{1,0:T(4,128)S(1)} all-reduce(f32[3,4096]{1,0:T(4,128)S(1)} %get-tuple-element.129), channel_id=1, replica_groups=mesh['atoms'=32,'loops'=16] {'loops'}, use_global_device_ids=true, to_apply=%region_7.8 | all-reduce | flops 12288 | bytes 98304 | tf_op jit(solution)/shard_map/psum | solution.py:134
  78.1 7.3 %multiply_cosine_fusion.1 = (f32[128,4096]{1,0:T(8,128)S(1)}, f32[128,4096]{1,0:T(8,128)S(1)}) fusion(f32[4096]{0:T(1024)S(1)} %bitcast.43, f32[128]{0:T(128)S(1)} %add_multiply_fusion.1), kind=kLoop, calls=%fused_computation.34 | loop fusion | flops 524288 | bytes 4211200 | tf_op jit(solution)/shard_map/cos | solution.py:110
  85.3 7.5 %multiply_cosine_fusion = (f32[4096,128]{1,0:T(8,128)S(1)}, f32[4096,128]{1,0:T(8,128)S(1)}) fusion(f32[128]{0:T(128)S(1)} %add_multiply_fusion.1, f32[4096]{0:T(1024)S(1)} %bitcast.42), kind=kLoop, calls=%fused_computation.32 | loop fusion | flops 524288 | bytes 4211200 | tf_op jit(solution)/shard_map/cos | solution.py:109
  92.9 0.5 multiply_cosine_fusion.2
  93.4 2.6 multiply_subtract_fusion
  96.0 14.5 %fusion.11 = f32[128,4,2,256]{3,0,2,1:T(8,128)S(1)} fusion(f32[128,4,1,4096]{3,0,2,1:T(8,128)S(1)} %get-tuple-element.177, f32[128,4,1,4096]{3,0,2,1:T(8,128)S(1)} %get-tuple-element.176, f32[4096,128]{1,0:T(8,128)S(1)} %get-tuple-element.182, f32[4096,128]{1,0:T(8,128)S(1)} %get-tuple-element.181), kind=kOutput, calls=%fused_computation.22 | convolution fusion | flops 12890144768 | bytes 22020096 | tf_op jit(solution)/shard_map/xzca,ad->xzcd/dot_general | solution.py:93
  110.6 0.8 pad_maximum_fusion
  111.5 1.3 dynamic-slice
  113.4 283.9 %all-reduce.3.cloned.1.call-done = f32[128,2,4,128]{3,0,2,1:T(8,128)} async-done(((f32[128,2,4,128]{3,0,2,1:T(8,128)}), f32[128,2,4,128]{3,0,2,1:T(8,128)}) %all-reduce.3.cloned.1.call-update) | async-done | bytes 524304
  397.3 1.4 fusion.33
  (27 shorter events, 2.8 us)
Async XLA Ops:
  6.5 390.8 %all-reduce.3.cloned.1.call-start = ((), (), s32[]{:S(2)}) async-start(), calls=%async_computation | async-start | bytes 1048576
Sparse Core Ops, SparseCore 0:
  111.6 285.6 all-reduce.2
where the time goes:
time: 406 us; the launch traced here: 405 us
  waiting for transfers between devices  284 us (70%)
  blocking collectives  50.9 us (13%)
  other arithmetic  40.5 us (10%)
  matrix products  14.5 us (4%)
  between operations  14.1 us (3%)
    unnamed x2, waiting for transfers between devices  284 us
    psum x1, blocking collectives, body(): displacement = lax.psum(partial_field, 'loops')  50.9 us
    dot_general x1, matrix products, factor_block(): jnp.einsum('xzca,ad->xzcd', left_pair, ytable, precision=lax.Precision.HI...  14.5 us
  transfers between devices with their start and end apart: 1, of which 1 were waited for; matrix products, arithmetic and copies ran while one was open for 0% of the time, Pallas kernels for 0%

commit v1 on v0

--- a/solution.py
+++ b/solution.py
@@ -131,7 +131,14 @@
     partial_field = lax.fori_loop(
         0, loop_count // block_size, add_block, jnp.zeros(anchor.shape, jnp.float32)
     )
-    displacement = lax.psum(partial_field, "loops")
+    loop_groups = lax.axis_size("loops")
+    chunk = partial_field.shape[1] // loop_groups
+    owned = lax.all_to_all(
+        partial_field.reshape(3, loop_groups, chunk), "loops", 1, 1, tiled=True
+    ).sum(axis=1)
+    displacement = lax.all_to_all(
+        jnp.broadcast_to(owned[:, None], (3, loop_groups, chunk)), "loops", 1, 1, tiled=True
+    ).reshape(3, -1)
     position = anchor + displacement
     group_count = lax.axis_size("atoms")
     zrows = QZ // lax.axis_size("loops")
@@ -141,12 +148,9 @@
     ywaves = waves(jnp.float32(0.0), QY, QY, 1.0)
     xwaves = waves(jnp.float32(0.0), QX, QX, 1.0)
     xcosines, xsines, zcosines, zsines, ytable = phase_tables(position, xwaves, ywaves, zwaves)
-    summed = lax.psum_scatter(
-        factor_block(xcosines, xsines, zcosines, zsines, ytable),
-        "atoms",
-        scatter_dimension=0,
-        tiled=True,
-    )
+    partial = factor_block(xcosines, xsines, zcosines, zsines, ytable)
+    blocks = partial.reshape(group_count, -1, *partial.shape[1:])
+    summed = lax.all_to_all(blocks, "atoms", 0, 0, tiled=True).sum(axis=0)
     power = summed[:, 0] ** 2 + summed[:, 1] ** 2
     return jnp.log1p(jnp.transpose(power, (1, 0, 2)) / atom_total)
 

time: 406 us -> 121 us (0.30)
  waiting for transfers between devices: 284 us -> 14.5 us
  blocking collectives: 50.9 us -> 33.8 us
  between operations: 14.1 us -> 0.12 us
  starting transfers between devices: 0.01 us -> 12.4 us
    unnamed x2 -> x0, waiting for transfers between devices: 284 us -> none
    psum x1 -> x0, blocking collectives: 50.9 us -> none  [body(): displacement = lax.psum(partial_field, 'loops')]
    all_to_all x0 -> x1, blocking collectives: none -> 33.8 us  [body(): summed = lax.all_to_all(blocks, 'atoms', 0, 0, tiled=True).sum(axis=0)]
    all_to_all x0 -> x2, waiting for transfers between devices: none -> 14.5 us  [the longest x1 7.35 us: body(): lax.all_to_all(partial_field.reshape(3, loop_groups, chunk), 'loops', 1,...]
    all_to_all x0 -> x2, starting transfers between devices: none -> 12.4 us  [the longest x1 8.68 us: body(): lax.all_to_all(partial_field.reshape(3, loop_groups, chunk), 'loops', 1,...]
    add x4, other arithmetic: 0.29 us -> 5.12 us  [add_block(): running + loop_field(anchor, lax.dynamic_slice_in_dim(centre, begin, bloc...]
  transfers between devices with their start and end apart: 1 -> 2, of which waited for: 1 -> 2; matrix products, arithmetic and copies ran while one was open for 0% -> 0% of each run, Pallas kernels for 0% -> 0%
where the time goes in v1:
time: 121 us
  other arithmetic  44.3 us (37%)
  blocking collectives  33.8 us (28%)
  waiting for transfers between devices  14.5 us (12%)
  matrix products  14.5 us (12%)
  starting transfers between devices  12.4 us (10%)
    all_to_all x1, blocking collectives, body(): summed = lax.all_to_all(blocks, 'atoms', 0, 0, tiled=True).sum(axis=0)  33.8 us
    dot_general x1, matrix products, factor_block(): jnp.einsum('xzca,ad->xzcd', left_pair, ytable, precision=lax.Precision.HI...  14.5 us
    all_to_all x1, starting transfers between devices, body(): lax.all_to_all(partial_field.reshape(3, loop_groups, chunk), 'loops', 1,...  8.68 us
    cos x1, other arithmetic, phase_tables(): ytable = jnp.concatenate([jnp.cos(yangle), jnp.sin(yangle)], axis=1)  7.51 us
    all_to_all x1, waiting for transfers between devices, body(): lax.all_to_all(partial_field.reshape(3, loop_groups, chunk), 'loops', 1,...  7.35 us
    cos x1, other arithmetic, phase_tables(): jnp.cos(xangle)  7.29 us
    all_to_all x1, waiting for transfers between devices, body(): lax.all_to_all(jnp.broadcast_to(owned[:, None], (3, loop_groups, chunk)),...  7.14 us
    reduce_sum x4, other arithmetic, loop_field(): return jnp.sum(strength[None] * field, axis=1)  6.38 us
  transfers between devices with their start and end apart: 2, of which 2 were waited for; matrix products, arithmetic and copies ran while one was open for 0% of the time, Pallas kernels for 0%

profile of v1, /device:TPU:1, one launch (start us, length us, event | category | flops | bytes accessed | tf_op | source)
XLA Modules:
  0.0 120.5 jit_solution(7138967387665250373)
XLA Ops:
  0.0 0.8 add_select_fusion.4
  0.8 0.7 fusion.22
  1.5 0.7 select_add_fusion.2
  2.2 0.7 select_add_fusion.7
  2.9 0.7 add_multiply_fusion
  3.7 21.9 %while.14 = (s32[]{:T(128)}, f32[3,4096]{1,0:T(4,128)}, f32[256]{0:T(256)}, f32[3,4096]{1,0:T(4,128)S(1)}, f32[3,256]{1,0:T(4,128)S(1)}, /*index=5*/f32[3,256]{1...) while((s32[]{:T(128)}, f32[3,4096]{1,0:T(4,128)}, ...), condition=%wide.region_6.7_spmd.clone, body=%wide.region_0.6_spmd.clone.sunk | while | flops 17052036 | bytes 16084141 | solution.py:131
  4.2 0.8 dynamic-slice_multiply_fusion.2
  5.3 0.9 fusion.39
  6.3 1.6 %fusion.40 = f32[3,4096]{1,0:T(4,128)S(1)} fusion(f32[64,4096]{1,0:T(8,128)S(1)} %multiply_multiply_fusion.2, f32[64]{0:T(128)S(1)} %get-tuple-element.257, f32[64,4096]{1,0:T(8,128)S(1)} %get-tuple-element.255, f32[64,4096]{1,0:T(8,128)S(1)} %get-tuple-element.256, f32[64,4096]{1,0:T(8,128)S(1)} %get-tuple-element.252, ...), kind=kLoop, calls=%fused_computation.11.clone.1 | loop fusion | flops 9424896 | bytes 5343744 | tf_op jit(solution)/shard_map/while/body/eval_jaxpr/reduce_sum | solution.py:76
  7.9 0.7 select_add_fusion.10
  9.0 0.8 dynamic-slice_multiply_fusion.2
  10.1 0.9 fusion.39
  11.1 1.6 %fusion.40 = f32[3,4096]{1,0:T(4,128)S(1)} fusion(f32[64,4096]{1,0:T(8,128)S(1)} %multiply_multiply_fusion.2, f32[64]{0:T(128)S(1)} %get-tuple-element.257, f32[64,4096]{1,0:T(8,128)S(1)} %get-tuple-element.255, f32[64,4096]{1,0:T(8,128)S(1)} %get-tuple-element.256, f32[64,4096]{1,0:T(8,128)S(1)} %get-tuple-element.252, ...), kind=kLoop, calls=%fused_computation.11.clone.1 | loop fusion | flops 9424896 | bytes 5343744 | tf_op jit(solution)/shard_map/while/body/eval_jaxpr/reduce_sum | solution.py:76
  12.7 1.5 %select_add_fusion.10 = f32[3,4096]{1,0:T(4,128)} fusion(f32[3,4096]{1,0:T(4,128)S(1)} %fusion.40, f32[3,4096]{1,0:T(4,128)} %get-tuple-element.271, pred[]{:T(512)S(6)} %compare.12), kind=kLoop, calls=%fused_computation.16.clone.1 | loop fusion | flops 24576 | bytes 147457 | tf_op jit(solution)/shard_map/while/body/eval_jaxpr/add | solution.py:123
  14.7 0.8 dynamic-slice_multiply_fusion.2
  15.8 0.9 fusion.39
  16.8 1.6 %fusion.40 = f32[3,4096]{1,0:T(4,128)S(1)} fusion(f32[64,4096]{1,0:T(8,128)S(1)} %multiply_multiply_fusion.2, f32[64]{0:T(128)S(1)} %get-tuple-element.257, f32[64,4096]{1,0:T(8,128)S(1)} %get-tuple-element.255, f32[64,4096]{1,0:T(8,128)S(1)} %get-tuple-element.256, f32[64,4096]{1,0:T(8,128)S(1)} %get-tuple-element.252, ...), kind=kLoop, calls=%fused_computation.11.clone.1 | loop fusion | flops 9424896 | bytes 5343744 | tf_op jit(solution)/shard_map/while/body/eval_jaxpr/reduce_sum | solution.py:76
  18.4 1.5 %select_add_fusion.10 = f32[3,4096]{1,0:T(4,128)} fusion(f32[3,4096]{1,0:T(4,128)S(1)} %fusion.40, f32[3,4096]{1,0:T(4,128)} %get-tuple-element.271, pred[]{:T(512)S(6)} %compare.12), kind=kLoop, calls=%fused_computation.16.clone.1 | loop fusion | flops 24576 | bytes 147457 | tf_op jit(solution)/shard_map/while/body/eval_jaxpr/add | solution.py:123
  20.4 0.8 dynamic-slice_multiply_fusion.2
  21.5 0.9 fusion.39
  22.5 1.6 %fusion.40 = f32[3,4096]{1,0:T(4,128)S(1)} fusion(f32[64,4096]{1,0:T(8,128)S(1)} %multiply_multiply_fusion.2, f32[64]{0:T(128)S(1)} %get-tuple-element.257, f32[64,4096]{1,0:T(8,128)S(1)} %get-tuple-element.255, f32[64,4096]{1,0:T(8,128)S(1)} %get-tuple-element.256, f32[64,4096]{1,0:T(8,128)S(1)} %get-tuple-element.252, ...), kind=kLoop, calls=%fused_computation.11.clone.1 | loop fusion | flops 9424896 | bytes 5343744 | tf_op jit(solution)/shard_map/while/body/eval_jaxpr/reduce_sum | solution.py:76
  24.1 1.5 %select_add_fusion.10 = f32[3,4096]{1,0:T(4,128)} fusion(f32[3,4096]{1,0:T(4,128)S(1)} %fusion.40, f32[3,4096]{1,0:T(4,128)} %get-tuple-element.271, pred[]{:T(512)S(6)} %compare.12), kind=kLoop, calls=%fused_computation.16.clone.1 | loop fusion | flops 24576 | bytes 147457 | tf_op jit(solution)/shard_map/while/body/eval_jaxpr/add | solution.py:123
  25.6 8.7 %all-to-all-start = ((f32[3,16,256]{2,0,1:T(4,128)}), f32[3,16,256]{2,0,1:T(4,128)S(1)}, u32[]{:S(2)}, u32[]{:S(2)}) async-start(f32[3,16,256]{2,0,1:T(4,128)} %bitcast.9), calls=%async_computation | async-start | bytes 131072 | tf_op jit(solution)/shard_map/all_to_all | solution.py:136
  34.3 7.4 %all-to-all-done = f32[3,16,256]{2,0,1:T(4,128)S(1)} async-done(((f32[3,16,256]{2,0,1:T(4,128)}), f32[3,16,256]{2,0,1:T(4,128)S(1)}, u32[]{:S(2)}, u32[]{:S(2)}) %all-to-all-start) | async-done | bytes 49184 | tf_op jit(solution)/shard_map/all_to_all | solution.py:136
  41.7 0.6 broadcast_in_dim.134
  42.3 3.7 %all-to-all-start.1 = ((f32[3,16,256]{2,0,1:T(4,128)}), f32[3,16,256]{2,0,1:T(4,128)S(1)}, u32[]{:S(2)}, u32[]{:S(2)}) async-start(f32[3,16,256]{2,0,1:T(4,128)} %broadcast_in_dim.134), calls=%async_computation.1 | async-start | bytes 131072 | tf_op jit(solution)/shard_map/all_to_all | solution.py:139
  46.0 7.1 %all-to-all-done.1 = f32[3,16,256]{2,0,1:T(4,128)S(1)} async-done(((f32[3,16,256]{2,0,1:T(4,128)}), f32[3,16,256]{2,0,1:T(4,128)S(1)}, u32[]{:S(2)}, u32[]{:S(2)}) %all-to-all-start.1) | async-done | bytes 49184 | tf_op jit(solution)/shard_map/all_to_all | solution.py:139
  53.2 7.3 %multiply_cosine_fusion.1 = (f32[128,4096]{1,0:T(8,128)S(1)}, f32[128,4096]{1,0:T(8,128)S(1)}) fusion(f32[4096]{0:T(1024)S(1)} %bitcast.35, f32[128]{0:T(128)S(1)} %add_multiply_fusion.1), kind=kLoop, calls=%fused_computation.34 | loop fusion | flops 524288 | bytes 4211200 | tf_op jit(solution)/shard_map/cos | solution.py:110
  60.5 7.5 %multiply_cosine_fusion = (f32[4096,128]{1,0:T(8,128)S(1)}, f32[4096,128]{1,0:T(8,128)S(1)}) fusion(f32[128]{0:T(128)S(1)} %add_multiply_fusion.1, f32[4096]{0:T(1024)S(1)} %bitcast.34), kind=kLoop, calls=%fused_computation.32 | loop fusion | flops 524288 | bytes 4211200 | tf_op jit(solution)/shard_map/cos | solution.py:109
  68.6 2.6 %multiply_subtract_fusion = (f32[128,4,1,4096]{3,0,2,1:T(8,128)S(1)}, f32[128,4,1,4096]{3,0,2,1:T(8,128)S(1)}) fusion(f32[128,4096]{1,0:T(8,128)S(1)} %get-tuple-element.188, f32[4,4096]{1,0:T(4,128)S(1)} %get-tuple-element.186, f32[128,4096]{1,0:T(8,128)S(1)} %get-tuple-element.187, f32[4,4096]{1,0:T(4,128)S(1)} %get-tuple-element.185), kind=kLoop, calls=%fused_computation.27 | loop fusion | flops 12582912 | bytes 21102592 | tf_op jit(solution)/shard_map/sub | solution.py:87
  71.2 14.5 %fusion.11 = f32[128,4,2,256]{3,0,2,1:T(8,128)S(1)} fusion(f32[128,4,1,4096]{3,0,2,1:T(8,128)S(1)} %get-tuple-element.177, f32[128,4,1,4096]{3,0,2,1:T(8,128)S(1)} %get-tuple-element.176, f32[4096,128]{1,0:T(8,128)S(1)} %get-tuple-element.184, f32[4096,128]{1,0:T(8,128)S(1)} %get-tuple-element.183), kind=kOutput, calls=%fused_computation.22 | convolution fusion | flops 12890144768 | bytes 22020096 | tf_op jit(solution)/shard_map/xzca,ad->xzcd/dot_general | solution.py:93
  86.0 33.8 %all_to_all.15 = f32[32,4,2,4,128]{4,1,3,2,0:T(4,128)S(1)} all-to-all(f32[32,4,2,4,128]{4,1,3,2,0:T(4,128)S(1)} %copy.11), channel_id=1, replica_groups=mesh['atoms'=32,'loops'=16] {'atoms'}, dimensions={0} | all-to-all | bytes 1048576 | tf_op jit(solution)/shard_map/all_to_all | solution.py:153
  (30 shorter events, 5.6 us)
Async XLA Ops:
  25.6 16.1 %all-to-all-start = ((f32[3,16,256]{2,0,1:T(4,128)}), f32[3,16,256]{2,0,1:T(4,128)S(1)}, u32[]{:S(2)}, u32[]{:S(2)}) async-start(f32[3,16,256]{2,0,1:T(4,128)} %bitcast.9), calls=%async_computation | async-start | bytes 131072 | tf_op jit(solution)/shard_map/all_to_all | solution.py:136
  42.3 10.8 %all-to-all-start.1 = ((f32[3,16,256]{2,0,1:T(4,128)}), f32[3,16,256]{2,0,1:T(4,128)S(1)}, u32[]{:S(2)}, u32[]{:S(2)}) async-start(f32[3,16,256]{2,0,1:T(4,128)} %broadcast_in_dim.134), calls=%async_computation.1 | async-start | bytes 131072 | tf_op jit(solution)/shard_map/all_to_all | solution.py:139

commit v2 on v1

--- a/solution.py
+++ b/solution.py
@@ -94,7 +94,7 @@
         "xzca,ad->xzcd",
         left_pair,
         ytable,
-        precision=lax.Precision.HIGHEST,
+        precision=lax.Precision.HIGH,
         preferred_element_type=jnp.float32,
     )
     real_part = product[:, :, 0, :ywidth] - product[:, :, 1, ywidth:]

time: 121 us -> 113 us (0.934)
  matrix products: 14.5 us -> 6.78 us
    dot_general x1, matrix products: 14.5 us -> 6.78 us  [factor_block(): jnp.einsum('xzca,ad->xzcd', left_pair, ytable, precision=lax.Precision.HI...]
where the time goes in v2:
time: 113 us
  other arithmetic  44.2 us (39%)
  blocking collectives  33.8 us (30%)
  waiting for transfers between devices  14.5 us (13%)
  starting transfers between devices  12.4 us (11%)
  matrix products  6.78 us (6%)
    all_to_all x1, blocking collectives, body(): summed = lax.all_to_all(blocks, 'atoms', 0, 0, tiled=True).sum(axis=0)  33.8 us
    all_to_all x1, starting transfers between devices, body(): lax.all_to_all(partial_field.reshape(3, loop_groups, chunk), 'loops', 1,...  8.68 us
    cos x1, other arithmetic, phase_tables(): ytable = jnp.concatenate([jnp.cos(yangle), jnp.sin(yangle)], axis=1)  7.51 us
    all_to_all x1, waiting for transfers between devices, body(): lax.all_to_all(partial_field.reshape(3, loop_groups, chunk), 'loops', 1,...  7.35 us
    cos x1, other arithmetic, phase_tables(): jnp.cos(xangle)  7.29 us
    all_to_all x1, waiting for transfers between devices, body(): lax.all_to_all(jnp.broadcast_to(owned[:, None], (3, loop_groups, chunk)),...  7.14 us
    dot_general x1, matrix products, factor_block(): jnp.einsum('xzca,ad->xzcd', left_pair, ytable, precision=lax.Precision.HI...  6.78 us
    reduce_sum x4, other arithmetic, loop_field(): return jnp.sum(strength[None] * field, axis=1)  6.38 us
  transfers between devices with their start and end apart: 2, of which 2 were waited for; matrix products, arithmetic and copies ran while one was open for 0% of the time, Pallas kernels for 0%

profile of v2, /device:TPU:1, one launch (start us, length us, event | category | flops | bytes accessed | tf_op | source)
XLA Modules:
  0.0 112.6 jit_solution(13552209367083385847)
XLA Ops:
  0.0 0.8 add_select_fusion.4
  0.8 0.7 fusion.22
  1.5 0.7 select_add_fusion.2
  2.2 0.7 select_add_fusion.7
  2.9 0.7 add_multiply_fusion
  3.7 21.9 %while.14 = (s32[]{:T(128)}, f32[3,4096]{1,0:T(4,128)}, f32[256]{0:T(256)}, f32[3,4096]{1,0:T(4,128)S(1)}, f32[3,256]{1,0:T(4,128)S(1)}, /*index=5*/f32[3,256]{1...) while((s32[]{:T(128)}, f32[3,4096]{1,0:T(4,128)}, ...), condition=%wide.region_6.7_spmd.clone, body=%wide.region_0.6_spmd.clone.sunk | while | flops 17052036 | bytes 16084141 | solution.py:131
  4.2 0.8 dynamic-slice_multiply_fusion.2
  5.3 0.9 fusion.39
  6.3 1.6 %fusion.40 = f32[3,4096]{1,0:T(4,128)S(1)} fusion(f32[64,4096]{1,0:T(8,128)S(1)} %multiply_multiply_fusion.2, f32[64]{0:T(128)S(1)} %get-tuple-element.257, f32[64,4096]{1,0:T(8,128)S(1)} %get-tuple-element.255, f32[64,4096]{1,0:T(8,128)S(1)} %get-tuple-element.256, f32[64,4096]{1,0:T(8,128)S(1)} %get-tuple-element.252, ...), kind=kLoop, calls=%fused_computation.11.clone.1 | loop fusion | flops 9424896 | bytes 5343744 | tf_op jit(solution)/shard_map/while/body/eval_jaxpr/reduce_sum | solution.py:76
  7.9 0.7 select_add_fusion.10
  9.0 0.8 dynamic-slice_multiply_fusion.2
  10.1 0.9 fusion.39
  11.1 1.6 %fusion.40 = f32[3,4096]{1,0:T(4,128)S(1)} fusion(f32[64,4096]{1,0:T(8,128)S(1)} %multiply_multiply_fusion.2, f32[64]{0:T(128)S(1)} %get-tuple-element.257, f32[64,4096]{1,0:T(8,128)S(1)} %get-tuple-element.255, f32[64,4096]{1,0:T(8,128)S(1)} %get-tuple-element.256, f32[64,4096]{1,0:T(8,128)S(1)} %get-tuple-element.252, ...), kind=kLoop, calls=%fused_computation.11.clone.1 | loop fusion | flops 9424896 | bytes 5343744 | tf_op jit(solution)/shard_map/while/body/eval_jaxpr/reduce_sum | solution.py:76
  12.7 1.5 %select_add_fusion.10 = f32[3,4096]{1,0:T(4,128)} fusion(f32[3,4096]{1,0:T(4,128)S(1)} %fusion.40, f32[3,4096]{1,0:T(4,128)} %get-tuple-element.271, pred[]{:T(512)S(6)} %compare.12), kind=kLoop, calls=%fused_computation.16.clone.1 | loop fusion | flops 24576 | bytes 147457 | tf_op jit(solution)/shard_map/while/body/eval_jaxpr/add | solution.py:123
  14.7 0.8 dynamic-slice_multiply_fusion.2
  15.8 0.9 fusion.39
  16.8 1.6 %fusion.40 = f32[3,4096]{1,0:T(4,128)S(1)} fusion(f32[64,4096]{1,0:T(8,128)S(1)} %multiply_multiply_fusion.2, f32[64]{0:T(128)S(1)} %get-tuple-element.257, f32[64,4096]{1,0:T(8,128)S(1)} %get-tuple-element.255, f32[64,4096]{1,0:T(8,128)S(1)} %get-tuple-element.256, f32[64,4096]{1,0:T(8,128)S(1)} %get-tuple-element.252, ...), kind=kLoop, calls=%fused_computation.11.clone.1 | loop fusion | flops 9424896 | bytes 5343744 | tf_op jit(solution)/shard_map/while/body/eval_jaxpr/reduce_sum | solution.py:76
  18.4 1.5 %select_add_fusion.10 = f32[3,4096]{1,0:T(4,128)} fusion(f32[3,4096]{1,0:T(4,128)S(1)} %fusion.40, f32[3,4096]{1,0:T(4,128)} %get-tuple-element.271, pred[]{:T(512)S(6)} %compare.12), kind=kLoop, calls=%fused_computation.16.clone.1 | loop fusion | flops 24576 | bytes 147457 | tf_op jit(solution)/shard_map/while/body/eval_jaxpr/add | solution.py:123
  20.4 0.8 dynamic-slice_multiply_fusion.2
  21.5 0.9 fusion.39
  22.5 1.6 %fusion.40 = f32[3,4096]{1,0:T(4,128)S(1)} fusion(f32[64,4096]{1,0:T(8,128)S(1)} %multiply_multiply_fusion.2, f32[64]{0:T(128)S(1)} %get-tuple-element.257, f32[64,4096]{1,0:T(8,128)S(1)} %get-tuple-element.255, f32[64,4096]{1,0:T(8,128)S(1)} %get-tuple-element.256, f32[64,4096]{1,0:T(8,128)S(1)} %get-tuple-element.252, ...), kind=kLoop, calls=%fused_computation.11.clone.1 | loop fusion | flops 9424896 | bytes 5343744 | tf_op jit(solution)/shard_map/while/body/eval_jaxpr/reduce_sum | solution.py:76
  24.1 1.5 %select_add_fusion.10 = f32[3,4096]{1,0:T(4,128)} fusion(f32[3,4096]{1,0:T(4,128)S(1)} %fusion.40, f32[3,4096]{1,0:T(4,128)} %get-tuple-element.271, pred[]{:T(512)S(6)} %compare.12), kind=kLoop, calls=%fused_computation.16.clone.1 | loop fusion | flops 24576 | bytes 147457 | tf_op jit(solution)/shard_map/while/body/eval_jaxpr/add | solution.py:123
  25.6 8.7 %all-to-all-start = ((f32[3,16,256]{2,0,1:T(4,128)}), f32[3,16,256]{2,0,1:T(4,128)S(1)}, u32[]{:S(2)}, u32[]{:S(2)}) async-start(f32[3,16,256]{2,0,1:T(4,128)} %bitcast.9), calls=%async_computation | async-start | bytes 131072 | tf_op jit(solution)/shard_map/all_to_all | solution.py:136
  34.3 7.4 %all-to-all-done = f32[3,16,256]{2,0,1:T(4,128)S(1)} async-done(((f32[3,16,256]{2,0,1:T(4,128)}), f32[3,16,256]{2,0,1:T(4,128)S(1)}, u32[]{:S(2)}, u32[]{:S(2)}) %all-to-all-start) | async-done | bytes 49184 | tf_op jit(solution)/shard_map/all_to_all | solution.py:136
  41.7 0.6 broadcast_in_dim.134
  42.3 3.7 %all-to-all-start.1 = ((f32[3,16,256]{2,0,1:T(4,128)}), f32[3,16,256]{2,0,1:T(4,128)S(1)}, u32[]{:S(2)}, u32[]{:S(2)}) async-start(f32[3,16,256]{2,0,1:T(4,128)} %broadcast_in_dim.134), calls=%async_computation.1 | async-start | bytes 131072 | tf_op jit(solution)/shard_map/all_to_all | solution.py:139
  46.0 7.1 %all-to-all-done.1 = f32[3,16,256]{2,0,1:T(4,128)S(1)} async-done(((f32[3,16,256]{2,0,1:T(4,128)}), f32[3,16,256]{2,0,1:T(4,128)S(1)}, u32[]{:S(2)}, u32[]{:S(2)}) %all-to-all-start.1) | async-done | bytes 49184 | tf_op jit(solution)/shard_map/all_to_all | solution.py:139
  53.2 7.3 %multiply_cosine_fusion.1 = (f32[128,4096]{1,0:T(8,128)S(1)}, f32[128,4096]{1,0:T(8,128)S(1)}) fusion(f32[4096]{0:T(1024)S(1)} %bitcast.35, f32[128]{0:T(128)S(1)} %add_multiply_fusion.1), kind=kLoop, calls=%fused_computation.34 | loop fusion | flops 524288 | bytes 4211200 | tf_op jit(solution)/shard_map/cos | solution.py:110
  60.5 7.5 %multiply_cosine_fusion = (f32[4096,128]{1,0:T(8,128)S(1)}, f32[4096,128]{1,0:T(8,128)S(1)}) fusion(f32[128]{0:T(128)S(1)} %add_multiply_fusion.1, f32[4096]{0:T(1024)S(1)} %bitcast.34), kind=kLoop, calls=%fused_computation.32 | loop fusion | flops 524288 | bytes 4211200 | tf_op jit(solution)/shard_map/cos | solution.py:109
  68.6 2.4 %multiply_subtract_fusion = (f32[128,4,1,4096]{3,0,2,1:T(8,128)S(1)}, f32[128,4,1,4096]{3,0,2,1:T(8,128)S(1)}) fusion(f32[128,4096]{1,0:T(8,128)S(1)} %get-tuple-element.188, f32[4,4096]{1,0:T(4,128)S(1)} %get-tuple-element.186, f32[128,4096]{1,0:T(8,128)S(1)} %get-tuple-element.187, f32[4,4096]{1,0:T(4,128)S(1)} %get-tuple-element.185), kind=kLoop, calls=%fused_computation.27 | loop fusion | flops 12582912 | bytes 21102592 | tf_op jit(solution)/shard_map/sub | solution.py:87
  71.0 6.8 %fusion.11 = f32[128,4,2,256]{3,0,2,1:T(8,128)S(1)} fusion(f32[128,4,1,4096]{3,0,2,1:T(8,128)S(1)} %get-tuple-element.177, f32[128,4,1,4096]{3,0,2,1:T(8,128)S(1)} %get-tuple-element.176, f32[4096,128]{1,0:T(8,128)S(1)} %get-tuple-element.184, f32[4096,128]{1,0:T(8,128)S(1)} %get-tuple-element.183), kind=kOutput, calls=%fused_computation.22 | convolution fusion | flops 6447693824 | bytes 22020096 | tf_op jit(solution)/shard_map/xzca,ad->xzcd/dot_general | solution.py:93
  78.2 33.8 %all_to_all.15 = f32[32,4,2,4,128]{4,1,3,2,0:T(4,128)S(1)} all-to-all(f32[32,4,2,4,128]{4,1,3,2,0:T(4,128)S(1)} %copy.11), channel_id=1, replica_groups=mesh['atoms'=32,'loops'=16] {'atoms'}, dimensions={0} | all-to-all | bytes 1048576 | tf_op jit(solution)/shard_map/all_to_all | solution.py:153
  (30 shorter events, 5.6 us)
Async XLA Ops:
  25.6 16.1 %all-to-all-start = ((f32[3,16,256]{2,0,1:T(4,128)}), f32[3,16,256]{2,0,1:T(4,128)S(1)}, u32[]{:S(2)}, u32[]{:S(2)}) async-start(f32[3,16,256]{2,0,1:T(4,128)} %bitcast.9), calls=%async_computation | async-start | bytes 131072 | tf_op jit(solution)/shard_map/all_to_all | solution.py:136
  42.3 10.8 %all-to-all-start.1 = ((f32[3,16,256]{2,0,1:T(4,128)}), f32[3,16,256]{2,0,1:T(4,128)S(1)}, u32[]{:S(2)}, u32[]{:S(2)}) async-start(f32[3,16,256]{2,0,1:T(4,128)} %broadcast_in_dim.134), calls=%async_computation.1 | async-start | bytes 131072 | tf_op jit(solution)/shard_map/all_to_all | solution.py:139

commit v3 on v2

--- a/solution.py
+++ b/solution.py
@@ -4,6 +4,8 @@
 import jax.numpy as jnp
 import numpy as np
 from jax import lax
+from jax.experimental import pallas as pl
+from jax.experimental.pallas import tpu as pltpu
 from jax.sharding import PartitionSpec as P
 
 WIN_X = 32
@@ -110,31 +112,73 @@
     return (jnp.cos(xangle), jnp.sin(xangle), jnp.cos(zangle), jnp.sin(zangle), ytable)
 
 
+FIELD_ROWS = 16
+
+
+def field_kernel(table, anchor, out):
+    ax, ay, az = anchor[0], anchor[1], anchor[2]
+
+    def one_loop(number, running):
+        cx, cy, cz = table[0, number], table[1, number], table[2, number]
+        bx, by, bz = table[3, number], table[4, number], table[5, number]
+        nx, ny, nz = table[6, number], table[7, number], table[8, number]
+        radius_sq, scale, burgers_normal = table[9, number], table[10, number], table[11, number]
+        dx, dy, dz = ax - cx, ay - cy, az - cz
+        distance_sq = dx * dx + dy * dy + dz * dz + radius_sq
+        inverse = lax.rsqrt(distance_sq)
+        ux, uy, uz = dx * inverse, dy * inverse, dz * inverse
+        along_b = bx * ux + by * uy + bz * uz
+        along_n = nx * ux + ny * uy + nz * uz
+        strength = scale * (inverse * inverse)
+        mixed = 3.0 * (along_b * along_n) - burgers_normal
+        fx, fy, fz = running
+        gx = (1.0 - 2.0 * POISSON) * (bx * along_n + nx * along_b) + ux * mixed
+        gy = (1.0 - 2.0 * POISSON) * (by * along_n + ny * along_b) + uy * mixed
+        gz = (1.0 - 2.0 * POISSON) * (bz * along_n + nz * along_b) + uz * mixed
+        return (fx + strength * gx, fy + strength * gy, fz + strength * gz)
+
+    zero = jnp.zeros(ax.shape, jnp.float32)
+    fx, fy, fz = lax.fori_loop(0, table.shape[1], one_loop, (zero, zero, zero), unroll=4)
+    out[0] = fx
+    out[1] = fy
+    out[2] = fz
+
+
+def partial_field(anchor, centre, burgers, normal, radius):
+    atoms = anchor.shape[1]
+    loops = centre.shape[1]
+    radius_sq = radius * radius
+    scale = radius_sq / (8.0 * (1.0 - POISSON))
+    burgers_normal = jnp.sum(burgers * normal, axis=0)
+    table = jnp.concatenate(
+        [centre, burgers, normal, radius_sq[None], scale[None], burgers_normal[None]], axis=0
+    )
+    rows = atoms // 128
+    tiled = anchor.reshape(3, rows, 128)
+    spec = pl.BlockSpec((3, FIELD_ROWS, 128), lambda i: (0, i, 0))
+    field = pl.pallas_call(
+        field_kernel,
+        grid=(rows // FIELD_ROWS,),
+        in_specs=[pl.BlockSpec(memory_space=pltpu.SMEM), spec],
+        out_specs=spec,
+        out_shape=jax.ShapeDtypeStruct(tiled.shape, jnp.float32),
+        cost_estimate=pl.CostEstimate(
+            flops=55 * atoms * loops, transcendentals=atoms * loops, bytes_accessed=24 * atoms
+        ),
+    )(table, tiled)
+    return field.reshape(3, atoms)
+
+
 def body(atom_site, loop_cells, loop_burgers, loop_habit, loop_radius):
     anchor = site_anchor(atom_site)
     centre = loop_centre(loop_cells)
     burgers = lookup(loop_burgers, BURGERS_TABLE)
     normal = lookup(loop_habit, NORMAL_TABLE)
-    loop_count = centre.shape[1]
-    block_size = math.gcd(loop_count, 64)
-
-    def add_block(number, running):
-        begin = number * block_size
-        return running + loop_field(
-            anchor,
-            lax.dynamic_slice_in_dim(centre, begin, block_size, 1),
-            lax.dynamic_slice_in_dim(burgers, begin, block_size, 1),
-            lax.dynamic_slice_in_dim(normal, begin, block_size, 1),
-            lax.dynamic_slice_in_dim(loop_radius, begin, block_size, 0),
-        )
-
-    partial_field = lax.fori_loop(
-        0, loop_count // block_size, add_block, jnp.zeros(anchor.shape, jnp.float32)
-    )
+    partial_field_value = partial_field(anchor, centre, burgers, normal, loop_radius)
     loop_groups = lax.axis_size("loops")
-    chunk = partial_field.shape[1] // loop_groups
+    chunk = partial_field_value.shape[1] // loop_groups
     owned = lax.all_to_all(
-        partial_field.reshape(3, loop_groups, chunk), "loops", 1, 1, tiled=True
+        partial_field_value.reshape(3, loop_groups, chunk), "loops", 1, 1, tiled=True
     ).sum(axis=1)
     displacement = lax.all_to_all(
         jnp.broadcast_to(owned[:, None], (3, loop_groups, chunk)), "loops", 1, 1, tiled=True

time: 113 us -> 107 us (0.947)
  other arithmetic: 44.2 us -> 24.4 us
  Pallas kernels: 0 us -> 11.3 us
  local copies, waits for them, and re-layouts: 0.8 us -> 3.48 us
    reduce_sum x17 -> x2, other arithmetic: 11.8 us -> 0.06 us  [the longest x1 0.03 us: body(): owned = lax.all_to_all(partial_field_value.reshape(3, loop_groups, chunk)...]
    pallas_call x0 -> x1, Pallas kernels: none -> 11.3 us  [partial_field(): pl.pallas_call(field_kernel, grid=(rows // FIELD_ROWS,), in_specs=[pl.Blo...]
    add x4 -> x1, other arithmetic: 5.12 us -> 0.73 us  [site_anchor(): return LATTICE * (cells + 0.5 * basis.astype(jnp.float32)[None, :])]
    mul x8 -> x0, other arithmetic: 3.47 us -> none  [the longest x4 3.04 us: loop_field(): radius_sq = (radius * radius)[:, None]]
    another operation x0 -> x2, local copies, waits for them, and re-layouts: none -> 1.46 us  [body(): partial_field_value.reshape(3, loop_groups, chunk)]
    concatenate x0 -> x1, local copies, waits for them, and re-layouts: none -> 1.22 us  [partial_field(): jnp.concatenate([centre, burgers, normal, radius_sq[None], scale[None], b...]
  transfers between devices with their start and end apart: 2 -> 2, of which waited for: 2 -> 2; matrix products, arithmetic and copies ran while one was open for 0% -> 1% of each run, Pallas kernels for 0% -> 0%
where the time goes in v3:
time: 107 us; the launch traced here: 106 us
  blocking collectives  33.8 us (32%)
  other arithmetic  24.4 us (23%)
  waiting for transfers between devices  13.9 us (13%)
  starting transfers between devices  12.2 us (11%)
  Pallas kernels  11.3 us (11%)
  matrix products  6.78 us (6%)
  local copies, waits for them, and re-layouts  3.48 us (3%)
    all_to_all x1, blocking collectives, body(): summed = lax.all_to_all(blocks, 'atoms', 0, 0, tiled=True).sum(axis=0)  33.8 us
    pallas_call x1, Pallas kernels, partial_field(): pl.pallas_call(field_kernel, grid=(rows // FIELD_ROWS,), in_specs=[pl.Blo...  11.3 us
    all_to_all x1, starting transfers between devices, body(): lax.all_to_all(partial_field_value.reshape(3, loop_groups, chunk), 'loops...  8.68 us
    cos x1, other arithmetic, phase_tables(): ytable = jnp.concatenate([jnp.cos(yangle), jnp.sin(yangle)], axis=1)  7.47 us
    all_to_all x1, waiting for transfers between devices, body(): lax.all_to_all(jnp.broadcast_to(owned[:, None], (3, loop_groups, chunk)),...  7.32 us
    cos x1, other arithmetic, phase_tables(): jnp.cos(xangle)  7.29 us
    dot_general x1, matrix products, factor_block(): jnp.einsum('xzca,ad->xzcd', left_pair, ytable, precision=lax.Precision.HI...  6.78 us
    all_to_all x1, waiting for transfers between devices, body(): lax.all_to_all(partial_field_value.reshape(3, loop_groups, chunk), 'loops...  6.62 us
  transfers between devices with their start and end apart: 2, of which 2 were waited for; matrix products, arithmetic and copies ran while one was open for 1% of the time, Pallas kernels for 0%

profile of v3, /device:TPU:1, one launch (start us, length us, event | category | flops | bytes accessed | tf_op | source)
XLA Modules:
  0.0 105.9 jit_solution(1095292022774591640)
XLA Ops:
  0.0 0.8 add_select_fusion.4
  0.8 0.7 fusion.29
  1.5 0.7 fusion.24
  2.2 0.7 select_add_fusion.4
  2.9 0.7 broadcast_multiply_fusion
  3.6 0.7 add_multiply_fusion
  4.3 1.2 %concatenate.9.table = f32[12,256]{1,0:T(8,128)} concatenate(f32[3,256]{1,0:T(4,128)S(1)} %add_multiply_fusion, f32[1,256]{1,0:T(1,128)S(1)} %bitcast.47, f32[1,256]{1,0:T(1,128)S(1)} %bitcast.49, f32[1,256]{1,0:T(1,128)S(1)} %bitcast.45, f32[1,256]{1,0:T(1,128)S(1)} %bitcast.53, f32[1,256]{1,0:T(1,128)S(1)} %bitcast.55, f32[1,256]{1,0:T(1,128)S(1)} %bitcast.51, ...), dimensions={0} | concatenate | bytes 24576 | tf_op jit(solution)/shard_map/concatenate | solution.py:153
  5.5 0.6 fusion.10.anchor
  6.1 11.3 %shard_map.55 = f32[3,32,128]{2,1,0:T(8,128)} custom-call(f32[12,256]{1,0:T(8,128)} %concatenate.9.table, f32[3,32,128]{2,1,0:T(8,128)} %fusion.10.anchor), custom_call_target="tpu_custom_call" | custom-call | flops 57671680 | bytes 98304 | tf_op jit(solution)/shard_map/pallas_call | solution.py:159
  17.4 0.8 reshape_reshape.3
  18.2 0.7 copy.6
  18.9 8.7 %all-to-all-start = ((f32[3,16,256]{2,0,1:T(4,128)}), f32[3,16,256]{2,0,1:T(4,128)S(1)}, u32[]{:S(2)}, u32[]{:S(2)}) async-start(f32[3,16,256]{2,0,1:T(4,128)} %copy.6), calls=%async_computation | async-start | bytes 131072 | tf_op jit(solution)/shard_map/all_to_all | solution.py:180
  27.6 0.7 fusion.14
  28.3 6.6 %all-to-all-done = f32[3,16,256]{2,0,1:T(4,128)S(1)} async-done(((f32[3,16,256]{2,0,1:T(4,128)}), f32[3,16,256]{2,0,1:T(4,128)S(1)}, u32[]{:S(2)}, u32[]{:S(2)}) %all-to-all-start) | async-done | bytes 49184 | tf_op jit(solution)/shard_map/all_to_all | solution.py:180
  35.0 0.6 broadcast_in_dim.107
  35.6 3.5 %all-to-all-start.1 = ((f32[3,16,256]{2,0,1:T(4,128)}), f32[3,16,256]{2,0,1:T(4,128)S(1)}, u32[]{:S(2)}, u32[]{:S(2)}) async-start(f32[3,16,256]{2,0,1:T(4,128)} %broadcast_in_dim.107), calls=%async_computation.1 | async-start | bytes 131072 | tf_op jit(solution)/shard_map/all_to_all | solution.py:183
  39.1 7.3 %all-to-all-done.1 = f32[3,16,256]{2,0,1:T(4,128)S(1)} async-done(((f32[3,16,256]{2,0,1:T(4,128)}), f32[3,16,256]{2,0,1:T(4,128)S(1)}, u32[]{:S(2)}, u32[]{:S(2)}) %all-to-all-start.1) | async-done | bytes 49184 | tf_op jit(solution)/shard_map/all_to_all | solution.py:183
  46.4 0.1 fusion.8
  46.5 7.3 %multiply_cosine_fusion.1 = (f32[128,4096]{1,0:T(8,128)S(1)}, f32[128,4096]{1,0:T(8,128)S(1)}) fusion(f32[4096]{0:T(1024)S(1)} %bitcast.40, f32[128]{0:T(128)S(1)} %add_multiply_fusion.1), kind=kLoop, calls=%fused_computation.12 | loop fusion | flops 524288 | bytes 4211200 | tf_op jit(solution)/shard_map/cos | solution.py:112
  53.8 7.5 %multiply_cosine_fusion = (f32[4096,128]{1,0:T(8,128)S(1)}, f32[4096,128]{1,0:T(8,128)S(1)}) fusion(f32[128]{0:T(128)S(1)} %add_multiply_fusion.1, f32[4096]{0:T(1024)S(1)} %bitcast.39), kind=kLoop, calls=%fused_computation.10 | loop fusion | flops 524288 | bytes 4211200 | tf_op jit(solution)/shard_map/cos | solution.py:111
  61.3 0.5 multiply_cosine_fusion.2
  61.8 2.4 %multiply_subtract_fusion = (f32[128,4,1,4096]{3,0,2,1:T(8,128)S(1)}, f32[128,4,1,4096]{3,0,2,1:T(8,128)S(1)}) fusion(f32[128,4096]{1,0:T(8,128)S(1)} %get-tuple-element.17, f32[4,4096]{1,0:T(4,128)S(1)} %get-tuple-element.15, f32[128,4096]{1,0:T(8,128)S(1)} %get-tuple-element.16, f32[4,4096]{1,0:T(4,128)S(1)} %get-tuple-element.14), kind=kLoop, calls=%fused_computation.5 | loop fusion | flops 12582912 | bytes 21102592 | tf_op jit(solution)/shard_map/sub | solution.py:89
  64.3 6.8 %fusion = f32[128,4,2,256]{3,0,2,1:T(8,128)S(1)} fusion(f32[128,4,1,4096]{3,0,2,1:T(8,128)S(1)} %get-tuple-element.6, f32[128,4,1,4096]{3,0,2,1:T(8,128)S(1)} %get-tuple-element.5, f32[4096,128]{1,0:T(8,128)S(1)} %get-tuple-element.13, f32[4096,128]{1,0:T(8,128)S(1)} %get-tuple-element.12), kind=kOutput, calls=%fused_computation | convolution fusion | flops 6447693824 | bytes 22020096 | tf_op jit(solution)/shard_map/xzca,ad->xzcd/dot_general | solution.py:95
  71.1 0.1 slice_subtract_fusion
  71.1 0.1 pad_maximum_fusion
  71.3 0.1 copy.10
  71.4 33.8 %all_to_all.15 = f32[32,4,2,4,128]{4,1,3,2,0:T(4,128)S(1)} all-to-all(f32[32,4,2,4,128]{4,1,3,2,0:T(4,128)S(1)} %copy.10), channel_id=1, replica_groups=mesh['atoms'=32,'loops'=16] {'atoms'}, dimensions={0} | all-to-all | bytes 1048576 | tf_op jit(solution)/shard_map/all_to_all | solution.py:197
  105.2 0.1 reduce_sum.29
  105.3 0.6 fusion.22
  (5 shorter events, 0.1 us)
Async XLA Ops:
  18.9 16.1 %all-to-all-start = ((f32[3,16,256]{2,0,1:T(4,128)}), f32[3,16,256]{2,0,1:T(4,128)S(1)}, u32[]{:S(2)}, u32[]{:S(2)}) async-start(f32[3,16,256]{2,0,1:T(4,128)} %copy.6), calls=%async_computation | async-start | bytes 131072 | tf_op jit(solution)/shard_map/all_to_all | solution.py:180
  35.6 10.8 %all-to-all-start.1 = ((f32[3,16,256]{2,0,1:T(4,128)}), f32[3,16,256]{2,0,1:T(4,128)S(1)}, u32[]{:S(2)}, u32[]{:S(2)}) async-start(f32[3,16,256]{2,0,1:T(4,128)} %broadcast_in_dim.107), calls=%async_computation.1 | async-start | bytes 131072 | tf_op jit(solution)/shard_map/all_to_all | solution.py:183

commit v4 on v3

--- a/solution.py
+++ b/solution.py
@@ -84,7 +84,7 @@
 
 
 def factor_block(xcosines, xsines, zcosines, zsines, ytable):
-    ywidth = ytable.shape[1] // 2
+    ywidth = ytable.shape[0] // 2
     left_real = (
         zcosines[None, :, :] * xcosines[:, None, :] - zsines[None, :, :] * xsines[:, None, :]
     )
@@ -93,7 +93,7 @@
     )
     left_pair = jnp.stack([left_real, left_imag], axis=2)
     product = jnp.einsum(
-        "xzca,ad->xzcd",
+        "xzca,da->xzcd",
         left_pair,
         ytable,
         precision=lax.Precision.HIGH,
@@ -104,12 +104,28 @@
     return jnp.stack([real_part, imag_part], axis=1)
 
 
+FINE_STEPS = 16
+
+
+def sincos_rows(waves_row, values):
+    coarse = waves_row[::FINE_STEPS]
+    fine = waves_row[:FINE_STEPS] - waves_row[0]
+    coarse_angle = coarse[:, None] * values[None, :]
+    fine_angle = fine[:, None] * values[None, :]
+    cc, sc = jnp.cos(coarse_angle), jnp.sin(coarse_angle)
+    cf, sf = jnp.cos(fine_angle), jnp.sin(fine_angle)
+    cosines = cc[:, None, :] * cf[None, :, :] - sc[:, None, :] * sf[None, :, :]
+    sines = sc[:, None, :] * cf[None, :, :] + cc[:, None, :] * sf[None, :, :]
+    shape = (waves_row.shape[0], values.shape[0])
+    return cosines.reshape(shape), sines.reshape(shape)
+
+
 def phase_tables(position, xwaves, ywaves, zwaves):
-    xangle = xwaves[:, None] * position[0][None, :]
-    yangle = position[1][:, None] * ywaves[None, :]
+    xcosines, xsines = sincos_rows(xwaves, position[0])
+    ycosines, ysines = sincos_rows(ywaves, position[1])
     zangle = zwaves[:, None] * position[2][None, :]
-    ytable = jnp.concatenate([jnp.cos(yangle), jnp.sin(yangle)], axis=1)
-    return (jnp.cos(xangle), jnp.sin(xangle), jnp.cos(zangle), jnp.sin(zangle), ytable)
+    ytable = jnp.concatenate([ycosines, ysines], axis=0)
+    return (xcosines, xsines, jnp.cos(zangle), jnp.sin(zangle), ytable)
 
 
 FIELD_ROWS = 16

time: 107 us -> 101 us (0.944)
  other arithmetic: 24.4 us -> 15.5 us
  matrix products: 6.78 us -> 9.45 us
    cos x3, other arithmetic: 15.3 us -> 3.41 us  [the longest x1 1.89 us: sincos_rows(): cf, sf = (jnp.cos(fine_angle), jnp.sin(fine_angle))]
    dot_general x1, matrix products: 6.78 us -> 9.45 us  [factor_block(): jnp.einsum('xzca,da->xzcd', left_pair, ytable, precision=lax.Precision.HI...]
    sub x0 -> x2, other arithmetic: none -> 2.35 us  [the longest x1 2.31 us: sincos_rows(): cosines = cc[:, None, :] * cf[None, :, :] - sc[:, None, :] * sf[None, :, :]]
    sub x1, other arithmetic: 0.05 us -> 1.26 us  [factor_block(): real_part = product[:, :, 0, :ywidth] - product[:, :, 1, ywidth:]]
  transfers between devices with their start and end apart: 2 -> 2, of which waited for: 2 -> 2; matrix products, arithmetic and copies ran while one was open for 1% -> 0% of each run, Pallas kernels for 0% -> 0%
where the time goes in v4:
time: 101 us; the launch traced here: 100 us
  blocking collectives  33.8 us (33%)
  other arithmetic  15.5 us (15%)
  waiting for transfers between devices  14.5 us (14%)
  starting transfers between devices  12.2 us (12%)
  Pallas kernels  11.3 us (11%)
  matrix products  9.45 us (9%)
  local copies, waits for them, and re-layouts  3.6 us (4%)
    all_to_all x1, blocking collectives, body(): summed = lax.all_to_all(blocks, 'atoms', 0, 0, tiled=True).sum(axis=0)  33.8 us
    pallas_call x1, Pallas kernels, partial_field(): pl.pallas_call(field_kernel, grid=(rows // FIELD_ROWS,), in_specs=[pl.Blo...  11.3 us
    dot_general x1, matrix products, factor_block(): jnp.einsum('xzca,da->xzcd', left_pair, ytable, precision=lax.Precision.HI...  9.45 us
    all_to_all x1, starting transfers between devices, body(): lax.all_to_all(partial_field_value.reshape(3, loop_groups, chunk), 'loops...  8.68 us
    all_to_all x1, waiting for transfers between devices, body(): lax.all_to_all(jnp.broadcast_to(owned[:, None], (3, loop_groups, chunk)),...  7.32 us
    all_to_all x1, waiting for transfers between devices, body(): lax.all_to_all(partial_field_value.reshape(3, loop_groups, chunk), 'loops...  7.18 us
    all_to_all x1, starting transfers between devices, body(): lax.all_to_all(jnp.broadcast_to(owned[:, None], (3, loop_groups, chunk)),...  3.48 us
    sub x1, other arithmetic, factor_block(): zcosines[None, :, :] * xcosines[:, None, :]  2.56 us
  transfers between devices with their start and end apart: 2, of which 2 were waited for; matrix products, arithmetic and copies ran while one was open for 0% of the time, Pallas kernels for 0%

profile of v4, /device:TPU:1, one launch (start us, length us, event | category | flops | bytes accessed | tf_op | source)
XLA Modules:
  0.0 100.4 jit_solution(5890665054818982283)
XLA Ops:
  0.0 0.0 copy-start
  0.0 0.8 fusion.29
  0.8 0.8 add_select_fusion.4
  1.6 0.7 broadcast_multiply_fusion
  2.3 0.7 fusion.24
  2.9 0.7 select_add_fusion.4
  3.6 0.7 add_multiply_fusion
  4.3 1.2 %concatenate.9.table = f32[12,256]{1,0:T(8,128)} concatenate(f32[3,256]{1,0:T(4,128)S(1)} %add_multiply_fusion, f32[1,256]{1,0:T(1,128)S(1)} %bitcast.59, f32[1,256]{1,0:T(1,128)S(1)} %bitcast.61, f32[1,256]{1,0:T(1,128)S(1)} %bitcast.57, f32[1,256]{1,0:T(1,128)S(1)} %bitcast.65, f32[1,256]{1,0:T(1,128)S(1)} %bitcast.67, f32[1,256]{1,0:T(1,128)S(1)} %bitcast.63, ...), dimensions={0} | concatenate | bytes 24576 | tf_op jit(solution)/shard_map/concatenate | solution.py:169
  5.6 0.6 fusion.10.anchor
  6.2 11.3 %shard_map.55 = f32[3,32,128]{2,1,0:T(8,128)} custom-call(f32[12,256]{1,0:T(8,128)} %concatenate.9.table, f32[3,32,128]{2,1,0:T(8,128)} %fusion.10.anchor), custom_call_target="tpu_custom_call" | custom-call | flops 57671680 | bytes 98304 | tf_op jit(solution)/shard_map/pallas_call | solution.py:175
  17.5 0.8 reshape_reshape.3
  18.3 0.7 copy.6
  19.0 8.7 %all-to-all-start = ((f32[3,16,256]{2,0,1:T(4,128)}), f32[3,16,256]{2,0,1:T(4,128)S(1)}, u32[]{:S(2)}, u32[]{:S(2)}) async-start(f32[3,16,256]{2,0,1:T(4,128)} %copy.6), calls=%async_computation | async-start | bytes 131072 | tf_op jit(solution)/shard_map/all_to_all | solution.py:196
  27.7 0.0 copy-done
  27.7 0.1 slice.47
  27.8 7.2 %all-to-all-done = f32[3,16,256]{2,0,1:T(4,128)S(1)} async-done(((f32[3,16,256]{2,0,1:T(4,128)}), f32[3,16,256]{2,0,1:T(4,128)S(1)}, u32[]{:S(2)}, u32[]{:S(2)}) %all-to-all-start) | async-done | bytes 49184 | tf_op jit(solution)/shard_map/all_to_all | solution.py:196
  35.0 0.6 broadcast_in_dim.121
  35.7 3.5 %all-to-all-start.1 = ((f32[3,16,256]{2,0,1:T(4,128)}), f32[3,16,256]{2,0,1:T(4,128)S(1)}, u32[]{:S(2)}, u32[]{:S(2)}) async-start(f32[3,16,256]{2,0,1:T(4,128)} %broadcast_in_dim.121), calls=%async_computation.1 | async-start | bytes 131072 | tf_op jit(solution)/shard_map/all_to_all | solution.py:199
  39.2 7.3 %all-to-all-done.1 = f32[3,16,256]{2,0,1:T(4,128)S(1)} async-done(((f32[3,16,256]{2,0,1:T(4,128)}), f32[3,16,256]{2,0,1:T(4,128)S(1)}, u32[]{:S(2)}, u32[]{:S(2)}) %all-to-all-start.1) | async-done | bytes 49184 | tf_op jit(solution)/shard_map/all_to_all | solution.py:199
  46.5 0.1 fusion.8
  46.6 1.0 multiply_cosine_fusion.2
  47.6 1.9 %multiply_cosine_fusion = (f32[16,4096]{1,0:T(8,128)S(1)}, f32[16,4096]{1,0:T(8,128)S(1)}, f32[16,4096]{1,0:T(8,128)S(1)}, f32[16,4096]{1,0:T(8,128)S(1)}) fusion(f32[4096]{0:T(1024)S(1)} %bitcast.48, f32[16]{0:T(128)S(1)} %slice_subtract_fusion.1, f32[4096]{0:T(1024)S(1)} %bitcast.50), kind=kLoop, calls=%fused_computation.15 | loop fusion | flops 131072 | bytes 1081408 | tf_op jit(solution)/shard_map/cos | solution.py:116
  49.5 0.5 multiply_cosine_fusion.4
  50.0 2.3 %multiply_subtract_fusion.1 = (f32[8,16,4096]{2,1,0:T(8,128)S(1)}, f32[8,16,4096]{2,1,0:T(8,128)}, f32[8,16,4096]{2,1,0:T(8,128)S(1)}, f32[8,16,4096]{2,1,0:T(8,128)S(1)}) fusion(f32[16,4096]{1,0:T(8,128)S(1)} %get-tuple-element.19, f32[8,4096]{1,0:T(8,128)S(1)} %get-tuple-element.17, f32[16,4096]{1,0:T(8,128)S(1)} %get-tuple-element.18, ...), kind=kLoop, calls=%fused_computation.10 | loop fusion | flops 6291456 | bytes 9961472 | tf_op jit(solution)/shard_map/sub | solution.py:117
  52.3 2.6 %multiply_subtract_fusion = (f32[128,4,1,4096]{3,0,2,1:T(8,128)S(1)}, f32[128,4,1,4096]{3,0,2,1:T(8,128)S(1)}) fusion(f32[128,4096]{1,0:T(8,128)S(1)} %bitcast.40, f32[4,4096]{1,0:T(4,128)S(1)} %get-tuple-element.21, f32[128,4096]{1,0:T(8,128)S(1)} %bitcast.41, f32[4,4096]{1,0:T(4,128)S(1)} %get-tuple-element.20), kind=kLoop, calls=%fused_computation.5 | loop fusion | flops 12582912 | bytes 21102592 | tf_op jit(solution)/shard_map/sub | solution.py:89
  54.9 9.5 %fusion = f32[128,4,2,256]{3,0,2,1:T(8,128)} fusion(f32[128,4,1,4096]{3,0,2,1:T(8,128)S(1)} %get-tuple-element.6, f32[128,4,1,4096]{3,0,2,1:T(8,128)S(1)} %get-tuple-element.5, f32[128,4096]{1,0:T(8,128)} %bitcast.43, f32[128,4096]{1,0:T(8,128)S(1)} %bitcast.42), kind=kOutput, calls=%fused_computation | convolution fusion | flops 6447693824 | bytes 22020096 | tf_op jit(solution)/shard_map/xzca,da->xzcd/dot_general | solution.py:95
  64.4 1.3 %slice_subtract_fusion = (f32[128,4,1,128]{3,0,2,1:T(8,128)S(1)}, f32[128,4,1,128]{3,0,2,1:T(8,128)S(1)}) fusion(f32[128,4,2,256]{3,0,2,1:T(8,128)} %fusion), kind=kLoop, calls=%fused_computation.19 | loop fusion | flops 131072 | bytes 1572864 | tf_op jit(solution)/shard_map/sub | solution.py:102
  65.6 0.1 pad_maximum_fusion
  65.8 0.1 copy.10
  65.9 33.8 %all_to_all.15 = f32[32,4,2,4,128]{4,1,3,2,0:T(4,128)S(1)} all-to-all(f32[32,4,2,4,128]{4,1,3,2,0:T(4,128)S(1)} %copy.10), channel_id=1, replica_groups=mesh['atoms'=32,'loops'=16] {'atoms'}, dimensions={0} | all-to-all | bytes 1048576 | tf_op jit(solution)/shard_map/all_to_all | solution.py:213
  99.7 0.1 reduce_sum.29
  99.8 0.6 fusion.22
  (7 shorter events, 0.2 us)
Async XLA Ops:
  0.0 27.7 %copy-start = (s32[4096]{0:T(1024)S(1)}, s32[4096]{0:T(1024)}, u32[]{:S(2)}) copy-start(s32[4096]{0:T(1024)} %param.5) | copy-start | bytes 49156
  19.0 16.1 %all-to-all-start = ((f32[3,16,256]{2,0,1:T(4,128)}), f32[3,16,256]{2,0,1:T(4,128)S(1)}, u32[]{:S(2)}, u32[]{:S(2)}) async-start(f32[3,16,256]{2,0,1:T(4,128)} %copy.6), calls=%async_computation | async-start | bytes 131072 | tf_op jit(solution)/shard_map/all_to_all | solution.py:196
  35.7 10.8 %all-to-all-start.1 = ((f32[3,16,256]{2,0,1:T(4,128)}), f32[3,16,256]{2,0,1:T(4,128)S(1)}, u32[]{:S(2)}, u32[]{:S(2)}) async-start(f32[3,16,256]{2,0,1:T(4,128)} %broadcast_in_dim.121), calls=%async_computation.1 | async-start | bytes 131072 | tf_op jit(solution)/shard_map/all_to_all | solution.py:199

commit v5 on v4

--- a/solution.py
+++ b/solution.py
@@ -128,76 +128,98 @@
     return (xcosines, xsines, jnp.cos(zangle), jnp.sin(zangle), ytable)
 
 
-FIELD_ROWS = 16
-
-
-def field_kernel(table, anchor, out):
-    ax, ay, az = anchor[0], anchor[1], anchor[2]
+HALF_BURGERS = float(BURGERS_TABLE[0, 0])
+HABIT_SCALE = float(NORMAL_TABLE[0, 0])
+STRENGTH_SCALE = 1.0 / (8.0 * (1.0 - POISSON))
+FIELD_SPLIT = 2
+
+
+def field_kernel(cells, burgers_index, habit_index, radius, site, anchor_out, field_out):
+    whole = site[...]
+    basis = jnp.bitwise_and(whole, 1)
+    cell = jnp.right_shift(whole, 1)
+    first = jnp.bitwise_and(cell, WIN_X - 1)
+    second = jnp.bitwise_and(jnp.right_shift(cell, 5), WIN_Y - 1)
+    third = jnp.right_shift(cell, 10)
+    half = 0.5 * basis.astype(jnp.float32)
+    coords = [LATTICE * (c.astype(jnp.float32) + half) for c in (first, second, third)]
+    for axis in range(3):
+        anchor_out[axis] = coords[axis]
+    rows = whole.shape[0] // FIELD_SPLIT
+    pieces = [[c[p * rows : (p + 1) * rows] for c in coords] for p in range(FIELD_SPLIT)]
 
     def one_loop(number, running):
-        cx, cy, cz = table[0, number], table[1, number], table[2, number]
-        bx, by, bz = table[3, number], table[4, number], table[5, number]
-        nx, ny, nz = table[6, number], table[7, number], table[8, number]
-        radius_sq, scale, burgers_normal = table[9, number], table[10, number], table[11, number]
-        dx, dy, dz = ax - cx, ay - cy, az - cz
-        distance_sq = dx * dx + dy * dy + dz * dz + radius_sq
-        inverse = lax.rsqrt(distance_sq)
-        ux, uy, uz = dx * inverse, dy * inverse, dz * inverse
-        along_b = bx * ux + by * uy + bz * uz
-        along_n = nx * ux + ny * uy + nz * uz
-        strength = scale * (inverse * inverse)
-        mixed = 3.0 * (along_b * along_n) - burgers_normal
-        fx, fy, fz = running
-        gx = (1.0 - 2.0 * POISSON) * (bx * along_n + nx * along_b) + ux * mixed
-        gy = (1.0 - 2.0 * POISSON) * (by * along_n + ny * along_b) + uy * mixed
-        gz = (1.0 - 2.0 * POISSON) * (bz * along_n + nz * along_b) + uz * mixed
-        return (fx + strength * gx, fy + strength * gy, fz + strength * gz)
-
-    zero = jnp.zeros(ax.shape, jnp.float32)
-    fx, fy, fz = lax.fori_loop(0, table.shape[1], one_loop, (zero, zero, zero), unroll=4)
-    out[0] = fx
-    out[1] = fy
-    out[2] = fz
-
-
-def partial_field(anchor, centre, burgers, normal, radius):
-    atoms = anchor.shape[1]
-    loops = centre.shape[1]
-    radius_sq = radius * radius
-    scale = radius_sq / (8.0 * (1.0 - POISSON))
-    burgers_normal = jnp.sum(burgers * normal, axis=0)
-    table = jnp.concatenate(
-        [centre, burgers, normal, radius_sq[None], scale[None], burgers_normal[None]], axis=0
-    )
-    rows = atoms // 128
-    tiled = anchor.reshape(3, rows, 128)
-    spec = pl.BlockSpec((3, FIELD_ROWS, 128), lambda i: (0, i, 0))
-    field = pl.pallas_call(
+        cx = LATTICE * (cells[0, number].astype(jnp.float32) + 0.25)
+        cy = LATTICE * (cells[1, number].astype(jnp.float32) + 0.25)
+        cz = LATTICE * (cells[2, number].astype(jnp.float32) + 0.25)
+        kb = burgers_index[number]
+        kh = habit_index[number]
+        h = jnp.float32(HALF_BURGERS)
+        bx = jnp.where(kb == 1, -h, h)
+        by = jnp.where(kb == 2, -h, h)
+        bz = jnp.where(kb == 3, -h, h)
+        c = jnp.float32(HABIT_SCALE)
+        zero = jnp.float32(0.0)
+        nx = jnp.where(kh < 4, c, zero)
+        ny = jnp.where(kh == 1, -c, jnp.where((kh == 2) | (kh == 3), zero, c))
+        nz = jnp.where((kh == 2) | (kh == 4), c, jnp.where((kh == 3) | (kh == 5), -c, zero))
+        burgers_normal = bx * nx + by * ny + bz * nz
+        r = radius[number]
+        radius_sq = r * r
+        scale = radius_sq * jnp.float32(STRENGTH_SCALE)
+        out = []
+        for p in range(FIELD_SPLIT):
+            ax, ay, az = pieces[p]
+            fx, fy, fz = running[p]
+            dx, dy, dz = ax - cx, ay - cy, az - cz
+            distance_sq = dx * dx + dy * dy + dz * dz + radius_sq
+            inverse = lax.rsqrt(distance_sq)
+            ux, uy, uz = dx * inverse, dy * inverse, dz * inverse
+            along_b = bx * ux + by * uy + bz * uz
+            along_n = nx * ux + ny * uy + nz * uz
+            strength = scale * (inverse * inverse)
+            mixed = 3.0 * (along_b * along_n) - burgers_normal
+            gx = (1.0 - 2.0 * POISSON) * (bx * along_n + nx * along_b) + ux * mixed
+            gy = (1.0 - 2.0 * POISSON) * (by * along_n + ny * along_b) + uy * mixed
+            gz = (1.0 - 2.0 * POISSON) * (bz * along_n + nz * along_b) + uz * mixed
+            out.append((fx + strength * gx, fy + strength * gy, fz + strength * gz))
+        return tuple(out)
+
+    zero = jnp.zeros((rows, whole.shape[1]), jnp.float32)
+    start = tuple((zero, zero, zero) for _ in range(FIELD_SPLIT))
+    totals = lax.fori_loop(0, radius.shape[0], one_loop, start, unroll=2)
+    for p in range(FIELD_SPLIT):
+        for axis in range(3):
+            field_out[axis, p * rows : (p + 1) * rows] = totals[p][axis]
+
+
+def anchor_and_field(atom_site, loop_cells, loop_burgers, loop_habit, loop_radius):
+    atoms = atom_site.shape[0]
+    loops = loop_radius.shape[0]
+    tiled = atom_site.reshape(atoms // 128, 128)
+    smem = pl.BlockSpec(memory_space=pltpu.SMEM)
+    vmem = pl.BlockSpec(memory_space=pltpu.VMEM)
+    shape = jax.ShapeDtypeStruct((3, *tiled.shape), jnp.float32)
+    anchor, field = pl.pallas_call(
         field_kernel,
-        grid=(rows // FIELD_ROWS,),
-        in_specs=[pl.BlockSpec(memory_space=pltpu.SMEM), spec],
-        out_specs=spec,
-        out_shape=jax.ShapeDtypeStruct(tiled.shape, jnp.float32),
+        in_specs=[smem, smem, smem, smem, vmem],
+        out_specs=[vmem, vmem],
+        out_shape=[shape, shape],
         cost_estimate=pl.CostEstimate(
-            flops=55 * atoms * loops, transcendentals=atoms * loops, bytes_accessed=24 * atoms
+            flops=55 * atoms * loops, transcendentals=atoms * loops, bytes_accessed=28 * atoms
         ),
-    )(table, tiled)
-    return field.reshape(3, atoms)
-
+    )(loop_cells, loop_burgers, loop_habit, loop_radius, tiled)
+    return anchor.reshape(3, atoms), field
 
 def body(atom_site, loop_cells, loop_burgers, loop_habit, loop_radius):
-    anchor = site_anchor(atom_site)
-    centre = loop_centre(loop_cells)
-    burgers = lookup(loop_burgers, BURGERS_TABLE)
-    normal = lookup(loop_habit, NORMAL_TABLE)
-    partial_field_value = partial_field(anchor, centre, burgers, normal, loop_radius)
+    anchor, field = anchor_and_field(atom_site, loop_cells, loop_burgers, loop_habit, loop_radius)
     loop_groups = lax.axis_size("loops")
-    chunk = partial_field_value.shape[1] // loop_groups
+    rows = field.shape[1] // loop_groups
     owned = lax.all_to_all(
-        partial_field_value.reshape(3, loop_groups, chunk), "loops", 1, 1, tiled=True
+        field.reshape(3, loop_groups, rows, field.shape[2]), "loops", 1, 1, tiled=True
     ).sum(axis=1)
     displacement = lax.all_to_all(
-        jnp.broadcast_to(owned[:, None], (3, loop_groups, chunk)), "loops", 1, 1, tiled=True
+        jnp.broadcast_to(owned[:, None], (3, loop_groups, *owned.shape[1:])), "loops", 1, 1, tiled=True
     ).reshape(3, -1)
     position = anchor + displacement
     group_count = lax.axis_size("atoms")

time: 101 us -> 95.3 us (0.944)
  other arithmetic: 15.5 us -> 11.3 us
  local copies, waits for them, and re-layouts: 3.6 us -> 2.4 us
    add x3 -> x0, other arithmetic: 2.17 us -> none  [the longest x2 1.37 us: lookup(): total + jnp.where(index == entry, jnp.float32(table[entry, column]), jnp....]
    reshape x0 -> x2, local copies, waits for them, and re-layouts: none -> 1.48 us  [the longest x1 1.43 us: body(): field.reshape(3, loop_groups, rows, field.shape[2])]
    another operation x2 -> x0, local copies, waits for them, and re-layouts: 1.47 us -> none  [body(): partial_field_value.reshape(3, loop_groups, chunk)]
    mul x3 -> x0, other arithmetic: 1.32 us -> none  [the longest x1 0.69 us: loop_centre(): return LATTICE * (cells.astype(jnp.float32) + 0.25)]
    concatenate x1 -> x0, local copies, waits for them, and re-layouts: 1.23 us -> none  [partial_field(): jnp.concatenate([centre, burgers, normal, radius_sq[None], scale[None], b...]
where the time goes in v5:
time: 95.3 us; the launch traced here: 94.8 us
  blocking collectives  33.8 us (35%)
  waiting for transfers between devices  14.5 us (15%)
  starting transfers between devices  12.1 us (13%)
  other arithmetic  11.3 us (12%)
  Pallas kernels  11.1 us (12%)
  matrix products  9.47 us (10%)
  local copies, waits for them, and re-layouts  2.4 us (3%)
    all_to_all x1, blocking collectives, body(): summed = lax.all_to_all(blocks, 'atoms', 0, 0, tiled=True).sum(axis=0)  33.8 us
    pallas_call x1, Pallas kernels, anchor_and_field(): pl.pallas_call(field_kernel, in_specs=[smem, smem, smem, smem, vmem], out...  11.1 us
    dot_general x1, matrix products, factor_block(): jnp.einsum('xzca,da->xzcd', left_pair, ytable, precision=lax.Precision.HI...  9.47 us
    all_to_all x1, starting transfers between devices, body(): lax.all_to_all(field.reshape(3, loop_groups, rows, field.shape[2]), 'loop...  8.68 us
    all_to_all x1, waiting for transfers between devices, body(): lax.all_to_all(jnp.broadcast_to(owned[:, None], (3, loop_groups, *owned.s...  7.31 us
    all_to_all x1, waiting for transfers between devices, body(): lax.all_to_all(field.reshape(3, loop_groups, rows, field.shape[2]), 'loop...  7.2 us
    all_to_all x1, starting transfers between devices, body(): lax.all_to_all(jnp.broadcast_to(owned[:, None], (3, loop_groups, *owned.s...  3.47 us
    sub x1, other arithmetic, factor_block(): zcosines[None, :, :] * xcosines[:, None, :]  2.56 us
  transfers between devices with their start and end apart: 2, of which 2 were waited for; matrix products, arithmetic and copies ran while one was open for 0% of the time, Pallas kernels for 0%

profile of v5, /device:TPU:1, one launch (start us, length us, event | category | flops | bytes accessed | tf_op | source)
XLA Modules:
  0.0 94.8 jit_solution(17935596368982369832)
XLA Ops:
  0.0 11.1 %shard_map.55 = (f32[3,32,128]{2,1,0:T(8,128)}, f32[3,32,128]{2,1,0:T(8,128)}) custom-call(s32[3,256]{1,0:T(4,128)} %cells.1, s32[256]{0:T(256)} %burgers_index.1, s32[256]{0:T(256)} %habit_index.1, f32[256]{0:T(256)} %radius.1, s32[32,128]{1,0:T(8,128)} %bitcast.38), custom_call_target="tpu_custom_call" | custom-call | flops 57671680 | bytes 114688 | tf_op jit(solution)/shard_map/pallas_call | solution.py:203
  11.1 1.4 %copy.9 = f32[3,16,2,128]{3,2,0,1:T(2,128)} copy(f32[3,16,2,128]{3,2,1,0:T(2,128)} %bitcast.36) | data formatting | bytes 98304 | tf_op jit(solution)/shard_map/reshape | solution.py:219
  12.6 8.7 %all-to-all-start = ((f32[3,16,2,128]{3,2,0,1:T(2,128)}), f32[3,16,2,128]{3,2,0,1:T(2,128)S(1)}, u32[]{:S(2)}, u32[]{:S(2)}) async-start(f32[3,16,2,128]{3,2,0,1:T(2,128)} %copy.9), calls=%async_computation | async-start | bytes 98304 | tf_op jit(solution)/shard_map/all_to_all | solution.py:218
  21.3 0.1 slice.47
  21.4 7.2 %all-to-all-done = f32[3,16,2,128]{3,2,0,1:T(2,128)S(1)} async-done(((f32[3,16,2,128]{3,2,0,1:T(2,128)}), f32[3,16,2,128]{3,2,0,1:T(2,128)S(1)}, u32[]{:S(2)}, u32[]{:S(2)}) %all-to-all-start) | async-done | bytes 49184 | tf_op jit(solution)/shard_map/all_to_all | solution.py:218
  28.6 0.6 broadcast_in_dim.2
  29.3 3.5 %all-to-all-start.1 = ((f32[3,16,2,128]{3,2,0,1:T(2,128)}), f32[3,16,2,128]{3,2,0,1:T(2,128)S(1)}, u32[]{:S(2)}, u32[]{:S(2)}) async-start(f32[3,16,2,128]{3,2,0,1:T(2,128)} %broadcast_in_dim.2), calls=%async_computation.1 | async-start | bytes 98304 | tf_op jit(solution)/shard_map/all_to_all | solution.py:221
  32.8 7.3 %all-to-all-done.1 = f32[3,16,2,128]{3,2,0,1:T(2,128)S(1)} async-done(((f32[3,16,2,128]{3,2,0,1:T(2,128)}), f32[3,16,2,128]{3,2,0,1:T(2,128)S(1)}, u32[]{:S(2)}, u32[]{:S(2)}) %all-to-all-start.1) | async-done | bytes 49184 | tf_op jit(solution)/shard_map/all_to_all | solution.py:221
  40.1 0.1 reshape.424
  40.2 0.8 bitcast_add_fusion
  41.0 1.0 %multiply_cosine_fusion.2 = (f32[8,4096]{1,0:T(8,128)S(1)}, f32[8,4096]{1,0:T(8,128)S(1)}, f32[8,4096]{1,0:T(8,128)S(1)}, f32[8,4096]{1,0:T(8,128)S(1)}) fusion(f32[4096]{0:T(1024)S(1)} %bitcast.31, f32[8]{0:T(128)S(1)} %slice.47, f32[4096]{0:T(1024)S(1)} %bitcast.33), kind=kLoop, calls=%fused_computation.21 | loop fusion | flops 65536 | bytes 557088 | tf_op jit(solution)/shard_map/cos | solution.py:115
  42.0 1.9 %multiply_cosine_fusion = (f32[16,4096]{1,0:T(8,128)S(1)}, f32[16,4096]{1,0:T(8,128)S(1)}, f32[16,4096]{1,0:T(8,128)S(1)}, f32[16,4096]{1,0:T(8,128)S(1)}) fusion(f32[4096]{0:T(1024)S(1)} %bitcast.32, f32[16]{0:T(128)S(1)} %slice_subtract_fusion.1, f32[4096]{0:T(1024)S(1)} %bitcast.34), kind=kLoop, calls=%fused_computation.15 | loop fusion | flops 131072 | bytes 1081408 | tf_op jit(solution)/shard_map/cos | solution.py:116
  43.9 0.5 multiply_cosine_fusion.4
  44.5 2.3 %multiply_subtract_fusion.1 = (f32[8,16,4096]{2,1,0:T(8,128)S(1)}, f32[8,16,4096]{2,1,0:T(8,128)}, f32[8,16,4096]{2,1,0:T(8,128)S(1)}, f32[8,16,4096]{2,1,0:T(8,128)S(1)}) fusion(f32[16,4096]{1,0:T(8,128)S(1)} %get-tuple-element.23, f32[8,4096]{1,0:T(8,128)S(1)} %get-tuple-element.21, f32[16,4096]{1,0:T(8,128)S(1)} %get-tuple-element.22, ...), kind=kLoop, calls=%fused_computation.10 | loop fusion | flops 6291456 | bytes 9961472 | tf_op jit(solution)/shard_map/sub | solution.py:117
  46.8 2.6 %multiply_subtract_fusion = (f32[128,4,1,4096]{3,0,2,1:T(8,128)S(1)}, f32[128,4,1,4096]{3,0,2,1:T(8,128)S(1)}) fusion(f32[128,4096]{1,0:T(8,128)S(1)} %bitcast.25, f32[4,4096]{1,0:T(4,128)S(1)} %get-tuple-element.25, f32[128,4096]{1,0:T(8,128)S(1)} %bitcast.26, f32[4,4096]{1,0:T(4,128)S(1)} %get-tuple-element.24), kind=kLoop, calls=%fused_computation.5 | loop fusion | flops 12582912 | bytes 21102592 | tf_op jit(solution)/shard_map/sub | solution.py:89
  49.3 9.5 %fusion = f32[128,4,2,256]{3,0,2,1:T(8,128)} fusion(f32[128,4,1,4096]{3,0,2,1:T(8,128)S(1)} %get-tuple-element.10, f32[128,4,1,4096]{3,0,2,1:T(8,128)S(1)} %get-tuple-element.9, f32[128,4096]{1,0:T(8,128)} %bitcast.28, f32[128,4096]{1,0:T(8,128)S(1)} %bitcast.27), kind=kOutput, calls=%fused_computation | convolution fusion | flops 6447693824 | bytes 22020096 | tf_op jit(solution)/shard_map/xzca,da->xzcd/dot_general | solution.py:95
  58.8 1.3 %slice_subtract_fusion = (f32[128,4,1,128]{3,0,2,1:T(8,128)S(1)}, f32[128,4,1,128]{3,0,2,1:T(8,128)S(1)}) fusion(f32[128,4,2,256]{3,0,2,1:T(8,128)} %fusion), kind=kLoop, calls=%fused_computation.19 | loop fusion | flops 131072 | bytes 1572864 | tf_op jit(solution)/shard_map/sub | solution.py:102
  60.1 0.1 pad_maximum_fusion
  60.2 0.1 copy.14
  60.4 33.8 %all_to_all.15 = f32[32,4,2,4,128]{4,1,3,2,0:T(4,128)S(1)} all-to-all(f32[32,4,2,4,128]{4,1,3,2,0:T(4,128)S(1)} %copy.14), channel_id=1, replica_groups=mesh['atoms'=32,'loops'=16] {'atoms'}, dimensions={0} | all-to-all | bytes 1048576 | tf_op jit(solution)/shard_map/all_to_all | solution.py:235
  94.1 0.1 reduce_sum.19
  94.2 0.6 fusion.9
  (6 shorter events, 0.2 us)
Async XLA Ops:
  12.6 16.1 %all-to-all-start = ((f32[3,16,2,128]{3,2,0,1:T(2,128)}), f32[3,16,2,128]{3,2,0,1:T(2,128)S(1)}, u32[]{:S(2)}, u32[]{:S(2)}) async-start(f32[3,16,2,128]{3,2,0,1:T(2,128)} %copy.9), calls=%async_computation | async-start | bytes 98304 | tf_op jit(solution)/shard_map/all_to_all | solution.py:218
  29.3 10.8 %all-to-all-start.1 = ((f32[3,16,2,128]{3,2,0,1:T(2,128)}), f32[3,16,2,128]{3,2,0,1:T(2,128)S(1)}, u32[]{:S(2)}, u32[]{:S(2)}) async-start(f32[3,16,2,128]{3,2,0,1:T(2,128)} %broadcast_in_dim.2), calls=%async_computation.1 | async-start | bytes 98304 | tf_op jit(solution)/shard_map/all_to_all | solution.py:221

commit v6 on v5

--- a/solution.py
+++ b/solution.py
@@ -6,7 +6,7 @@
 from jax import lax
 from jax.experimental import pallas as pl
 from jax.experimental.pallas import tpu as pltpu
-from jax.sharding import PartitionSpec as P
+from jax.sharding import Mesh, PartitionSpec as P
 
 WIN_X = 32
 WIN_Y = 32
@@ -222,7 +222,7 @@
         jnp.broadcast_to(owned[:, None], (3, loop_groups, *owned.shape[1:])), "loops", 1, 1, tiled=True
     ).reshape(3, -1)
     position = anchor + displacement
-    group_count = lax.axis_size("atoms")
+    group_count = lax.axis_size((ATOM_OUTER, ATOM_CORE))
     zrows = QZ // lax.axis_size("loops")
     atom_total = position.shape[1] * group_count
     zfirst = (lax.axis_index("loops") * zrows).astype(jnp.float32)
@@ -230,15 +230,36 @@
     ywaves = waves(jnp.float32(0.0), QY, QY, 1.0)
     xwaves = waves(jnp.float32(0.0), QX, QX, 1.0)
     xcosines, xsines, zcosines, zsines, ytable = phase_tables(position, xwaves, ywaves, zwaves)
-    partial = factor_block(xcosines, xsines, zcosines, zsines, ytable)
-    blocks = partial.reshape(group_count, -1, *partial.shape[1:])
-    summed = lax.all_to_all(blocks, "atoms", 0, 0, tiled=True).sum(axis=0)
+    outer = lax.axis_size(ATOM_OUTER)
+    core = lax.axis_index(ATOM_CORE)
+    split = (outer, 2, xcosines.shape[0] // (2 * outer), xcosines.shape[1])
+
+    def rows_of(table, side):
+        picked = lax.dynamic_index_in_dim(table.reshape(split), side, axis=1, keepdims=False)
+        return picked.reshape(-1, table.shape[1])
+
+    away = 1 - core
+    sent = factor_block(rows_of(xcosines, away), rows_of(xsines, away), zcosines, zsines, ytable)
+    arrived = lax.ppermute(sent, ATOM_CORE, [(0, 1), (1, 0)])
+    kept = factor_block(rows_of(xcosines, core), rows_of(xsines, core), zcosines, zsines, ytable)
+    partial = kept + arrived
+    blocks = partial.reshape(outer, -1, *partial.shape[1:])
+    summed = lax.all_to_all(blocks, ATOM_OUTER, 0, 0, tiled=True).sum(axis=0)
     power = summed[:, 0] ** 2 + summed[:, 1] ** 2
     return jnp.log1p(jnp.transpose(power, (1, 0, 2)) / atom_total)
 
 
+ATOM_OUTER = "atom_pairs"
+ATOM_CORE = "atom_core"
+
+
 def solution(mesh):
-    placed = (P("atoms"), P(None, "loops"), P("loops"), P("loops"), P("loops"))
+    groups, loop_groups = mesh.devices.shape
+    paired = Mesh(
+        mesh.devices.reshape(groups // 2, 2, loop_groups), (ATOM_OUTER, ATOM_CORE, "loops")
+    )
+    atoms = (ATOM_OUTER, ATOM_CORE)
+    placed = (P(atoms), P(None, "loops"), P("loops"), P("loops"), P("loops"))
     return jax.shard_map(
-        body, mesh=mesh, in_specs=placed, out_specs=P("loops", "atoms", None), check_vma=False
-    )
+        body, mesh=paired, in_specs=placed, out_specs=P("loops", atoms, None), check_vma=False
+    )

time: 95.3 us -> 105 us (1.10)
  local copies, waits for them, and re-layouts: 2.4 us -> 17.2 us
  blocking collectives: 33.8 us -> 21.9 us
  starting transfers between devices: 12.1 us -> 18.2 us
  other arithmetic: 11.3 us -> 14.6 us
  matrix products: 9.47 us -> 7.29 us
    mul x0 -> x12, local copies, waits for them, and re-layouts: none -> 13.2 us  [the longest x8 8.34 us: sincos_rows(): cosines = cc[:, None, :] * cf[None, :, :] - sc[:, None, :] * sf[None, :, :]]
    all_to_all x1, blocking collectives: 33.8 us -> 21.9 us  [body(): summed = lax.all_to_all(blocks, ATOM_OUTER, 0, 0, tiled=True).sum(axis=0)]
    ppermute x0 -> x1, starting transfers between devices: none -> 6.04 us  [body(): arrived = lax.ppermute(sent, ATOM_CORE, [(0, 1), (1, 0)])]
    dot_general x1 -> x2, matrix products: 9.47 us -> 7.29 us  [factor_block(): jnp.einsum('xzca,da->xzcd', left_pair, ytable, precision=lax.Precision.HI...]
    sub x1 -> x2, other arithmetic: 2.31 us -> 4.3 us  [sincos_rows(): cosines = cc[:, None, :] * cf[None, :, :] - sc[:, None, :] * sf[None, :, :]]
    dynamic_slice x0 -> x1, local copies, waits for them, and re-layouts: none -> 1.7 us  [rows_of(): lax.dynamic_index_in_dim(table.reshape(split), side, axis=1, keepdims=False)]
    sub x1 -> x2, other arithmetic: 1.26 us -> 0.04 us  [factor_block(): real_part = product[:, :, 0, :ywidth] - product[:, :, 1, ywidth:]]
  transfers between devices with their start and end apart: 2 -> 3, of which waited for: 2 -> 2; matrix products, arithmetic and copies ran while one was open for 0% -> 4% of each run, Pallas kernels for 0% -> 0%
where the time goes in v6:
time: 105 us
  blocking collectives  21.9 us (21%)
  starting transfers between devices  18.2 us (17%)
  local copies, waits for them, and re-layouts  17.2 us (16%)
  other arithmetic  14.6 us (14%)
  waiting for transfers between devices  14 us (13%)
  Pallas kernels  11.1 us (11%)
  matrix products  7.29 us (7%)
    all_to_all x1, blocking collectives, body(): summed = lax.all_to_all(blocks, ATOM_OUTER, 0, 0, tiled=True).sum(axis=0)  21.9 us
    pallas_call x1, Pallas kernels, anchor_and_field(): pl.pallas_call(field_kernel, in_specs=[smem, smem, smem, smem, vmem], out...  11.1 us
    all_to_all x1, starting transfers between devices, body(): lax.all_to_all(field.reshape(3, loop_groups, rows, field.shape[2]), 'loop...  8.68 us
    mul x8, local copies, waits for them, and re-layouts, sincos_rows(): cosines = cc[:, None, :] * cf[None, :, :] - sc[:, None, :] * sf[None, :, :]  8.34 us
    dot_general x2, matrix products, factor_block(): jnp.einsum('xzca,da->xzcd', left_pair, ytable, precision=lax.Precision.HI...  7.29 us
    all_to_all x1, waiting for transfers between devices, body(): lax.all_to_all(field.reshape(3, loop_groups, rows, field.shape[2]), 'loop...  7.21 us
    all_to_all x1, waiting for transfers between devices, body(): lax.all_to_all(jnp.broadcast_to(owned[:, None], (3, loop_groups, *owned.s...  6.8 us
    ppermute x1, starting transfers between devices, body(): arrived = lax.ppermute(sent, ATOM_CORE, [(0, 1), (1, 0)])  6.04 us
  transfers between devices with their start and end apart: 3, of which 2 were waited for; matrix products, arithmetic and copies ran while one was open for 4% of the time, Pallas kernels for 0%

profile of v6, /device:TPU:1, one launch (start us, length us, event | category | flops | bytes accessed | tf_op | source)
XLA Modules:
  0.0 104.6 jit_solution(15185203753641704300)
XLA Ops:
  0.0 11.1 %shard_map.55 = (f32[3,32,128]{2,1,0:T(8,128)}, f32[3,32,128]{2,1,0:T(8,128)}) custom-call(s32[3,256]{1,0:T(4,128)} %cells.1, s32[256]{0:T(256)} %burgers_index.1, s32[256]{0:T(256)} %habit_index.1, f32[256]{0:T(256)} %radius.1, s32[32,128]{1,0:T(8,128)} %bitcast.54), custom_call_target="tpu_custom_call" | custom-call | flops 57671680 | bytes 114688 | tf_op jit(solution)/shard_map/pallas_call | solution.py:203
  11.1 1.4 %copy.26 = f32[3,16,2,128]{3,2,0,1:T(2,128)} copy(f32[3,16,2,128]{3,2,1,0:T(2,128)} %bitcast.52) | data formatting | bytes 98304 | tf_op jit(solution)/shard_map/reshape | solution.py:219
  12.6 8.7 %all-to-all-start = ((f32[3,16,2,128]{3,2,0,1:T(2,128)}), f32[3,16,2,128]{3,2,0,1:T(2,128)S(1)}, u32[]{:S(2)}, u32[]{:S(2)}) async-start(f32[3,16,2,128]{3,2,0,1:T(2,128)} %copy.26), calls=%async_computation | async-start | bytes 98304 | tf_op jit(solution)/shard_map/all_to_all | solution.py:218
  21.3 0.1 slice.59
  21.4 7.2 %all-to-all-done = f32[3,16,2,128]{3,2,0,1:T(2,128)S(1)} async-done(((f32[3,16,2,128]{3,2,0,1:T(2,128)}), f32[3,16,2,128]{3,2,0,1:T(2,128)S(1)}, u32[]{:S(2)}, u32[]{:S(2)}) %all-to-all-start) | async-done | bytes 49184 | tf_op jit(solution)/shard_map/all_to_all | solution.py:218
  28.6 0.6 broadcast_in_dim.2
  29.3 3.5 %all-to-all-start.1 = ((f32[3,16,2,128]{3,2,0,1:T(2,128)}), f32[3,16,2,128]{3,2,0,1:T(2,128)S(1)}, u32[]{:S(2)}, u32[]{:S(2)}) async-start(f32[3,16,2,128]{3,2,0,1:T(2,128)} %broadcast_in_dim.2), calls=%async_computation.1 | async-start | bytes 98304 | tf_op jit(solution)/shard_map/all_to_all | solution.py:221
  32.8 0.5 add_multiply_fusion.1
  33.3 6.8 %all-to-all-done.1 = f32[3,16,2,128]{3,2,0,1:T(2,128)S(1)} async-done(((f32[3,16,2,128]{3,2,0,1:T(2,128)}), f32[3,16,2,128]{3,2,0,1:T(2,128)S(1)}, u32[]{:S(2)}, u32[]{:S(2)}) %all-to-all-start.1) | async-done | bytes 49184 | tf_op jit(solution)/shard_map/all_to_all | solution.py:221
  40.2 0.8 bitcast_add_fusion
  41.1 2.6 %multiply_cosine_fusion = (f32[16,4096]{1,0:T(8,128)S(1)}, f32[16,4096]{1,0:T(8,128)}, f32[16,4096]{1,0:T(8,128)S(1)}, f32[16,4096]{1,0:T(8,128)S(1)}) fusion(f32[4096]{0:T(1024)S(1)} %bitcast.47, f32[16]{0:T(128)S(1)} %slice_subtract_fusion.1, f32[4096]{0:T(1024)S(1)} %bitcast.49), kind=kLoop, calls=%fused_computation.19 | loop fusion | flops 131072 | bytes 1081408 | tf_op jit(solution)/shard_map/cos | solution.py:116
  43.7 1.5 %mul.406 = f32[8,16,4096]{2,1,0:T(8,128)} broadcast(f32[16,4096]{1,0:T(8,128)S(1)} %get-tuple-element.41), dimensions={1,2} | broadcast | bytes 2359296 | tf_op jit(solution)/shard_map/mul | solution.py:117
  45.2 1.9 %mul.407 = f32[16,2,4,4096]{3,2,1,0:T(4,128)S(1)} reshape(f32[8,16,4096]{2,1,0:T(8,128)} %mul.406) | data formatting | bytes 4194304 | tf_op jit(solution)/shard_map/mul | solution.py:117
  47.1 1.5 %mul.412 = f32[8,16,4096]{2,1,0:T(8,128)} broadcast(f32[16,4096]{1,0:T(8,128)S(1)} %get-tuple-element.40), dimensions={1,2} | broadcast | bytes 2359296 | tf_op jit(solution)/shard_map/mul | solution.py:117
  48.6 2.9 %mul.413 = f32[16,2,4,4096]{3,2,1,0:T(4,128)} reshape(f32[8,16,4096]{2,1,0:T(8,128)} %mul.412) | data formatting | bytes 4194304 | tf_op jit(solution)/shard_map/mul | solution.py:117
  51.5 1.7 %multiply_cosine_fusion.2 = (f32[8,4096]{1,0:T(8,128)S(1)}, f32[8,4096]{1,0:T(8,128)}, f32[8,4096]{1,0:T(8,128)S(1)}, f32[8,4096]{1,0:T(8,128)S(1)}) fusion(f32[4096]{0:T(1024)S(1)} %bitcast.48, f32[8]{0:T(128)S(1)} %slice.59, f32[4096]{0:T(1024)S(1)} %bitcast.50), kind=kLoop, calls=%fused_computation.25 | loop fusion | flops 65536 | bytes 557088 | tf_op jit(solution)/shard_map/cos | solution.py:115
  53.3 0.2 mul.401
  53.6 0.2 mul.410
  53.8 2.7 %multiply_subtract_fusion.3 = (f32[16,2,4,4096]{3,2,1,0:T(4,128)S(1)}, f32[16,2,4,4096]{3,2,1,0:T(4,128)S(1)}) fusion(f32[16,2,4,4096]{3,2,1,0:T(4,128)} %mul.413, f32[16,2,4,4096]{3,2,1,0:T(4,128)S(1)} %mul.407, f32[16,4096]{1,0:T(8,128)S(1)} %mul.410, f32[16,4096]{1,0:T(8,128)S(1)} %mul.401), kind=kLoop, calls=%fused_computation.17 | loop fusion | flops 3145728 | bytes 8912896 | tf_op jit(solution)/shard_map/sub | solution.py:117
  56.5 1.7 %constant_dynamic-slice_fusion.2 = (f32[16,1,4,4096]{3,2,1,0:T(4,128)S(1)}, f32[16,1,4,4096]{3,2,1,0:T(4,128)}, f32[16,1,4,4096]{3,2,1,0:T(4,128)}, f32[16,1,4,4096]{3,2,1,0:T(4,128)S(1)}) fusion(f32[16,2,4,4096]{3,2,1,0:T(4,128)S(1)} %get-tuple-element.10, s32[]{:T(128)S(6)} %select_n.9, s32[]{:T(128)S(6)} %select_n.10, ...), kind=kLoop, calls=%fused_computation.49 | loop fusion | bytes 8388616 | tf_op jit(solution)/shard_map/jit(dynamic_index_in_dim)/dynamic_slice | solution.py:238
  58.2 0.4 mul.415
  58.6 0.4 mul.421
  58.9 1.6 %mul.439 = f32[64,4096]{1,0:T(8,128)S(1)} reshape(f32[16,1,4,4096]{3,2,1,0:T(4,128)} %get-tuple-element.42) | data formatting | bytes 2097152 | tf_op jit(solution)/shard_map/mul | solution.py:89
  60.5 2.6 %mul.442 = f32[64,4096]{1,0:T(8,128)} reshape(f32[16,1,4,4096]{3,2,1,0:T(4,128)} %get-tuple-element.18) | data formatting | bytes 2097152 | tf_op jit(solution)/shard_map/mul | solution.py:89
  63.1 1.3 %multiply_cosine_fusion.4 = (f32[4,4096]{1,0:T(4,128)S(1)}, f32[4,4096]{1,0:T(4,128)S(1)}) fusion(f32[4096]{0:T(1024)S(1)} %bitcast.51, f32[4]{0:T(128)} %add_multiply_fusion.1), kind=kLoop, calls=%fused_computation.39 | loop fusion | flops 16384 | bytes 147472 | tf_op jit(solution)/shard_map/cos | solution.py:128
  64.4 1.6 %multiply_subtract_fusion.2 = (f32[8,16,4096]{2,1,0:T(8,128)S(1)}, f32[8,16,4096]{2,1,0:T(8,128)S(1)}) fusion(f32[16,4096]{1,0:T(8,128)} %get-tuple-element.31, f32[8,4096]{1,0:T(8,128)} %get-tuple-element.29, f32[16,4096]{1,0:T(8,128)S(1)} %get-tuple-element.30, f32[8,4096]{1,0:T(8,128)S(1)} %get-tuple-element.28), kind=kLoop, calls=%fused_computation.15 | loop fusion | flops 3145728 | bytes 4980736 | tf_op jit(solution)/shard_map/sub | solution.py:117
  66.0 2.4 %multiply_subtract_fusion.1 = (f32[64,4,1,4096]{3,0,2,1:T(8,128)S(1)}, f32[64,4,1,4096]{3,0,2,1:T(8,128)S(1)}, f32[64,4,1,4096]{3,0,2,1:T(8,128)S(1)}, f32[64,4,1,4096]{3,0,2,1:T(8,128)S(1)}) fusion(f32[64,4096]{1,0:T(8,128)S(1)} %mul.421, f32[4,4096]{1,0:T(4,128)S(1)} %get-tuple-element.33, f32[64,4096]{1,0:T(8,128)S(1)} %mul.415, ...), kind=kLoop, calls=%fused_computation.13 | loop fusion | flops 12582912 | bytes 21102592 | tf_op jit(solution)/shard_map/sub | solution.py:89
  68.4 3.6 %fusion.4 = f32[64,4,2,256]{3,0,1,2:T(8,128)S(1)} fusion(f32[128,4096]{1,0:T(8,128)S(1)} %bitcast.44, f32[128,4096]{1,0:T(8,128)S(1)} %bitcast.42, f32[64,4,1,4096]{3,0,2,1:T(8,128)S(1)} %get-tuple-element.23, f32[64,4,1,4096]{3,0,2,1:T(8,128)S(1)} %get-tuple-element.24), kind=kOutput, calls=%fused_computation.5 | convolution fusion | flops 3224371200 | bytes 13107200 | tf_op jit(solution)/shard_map/xzca,da->xzcd/dot_general | solution.py:95
  72.1 6.0 %collective-permute-start = (f32[64,2,4,128]{3,0,2,1:T(8,128)S(1)}, f32[64,2,4,128]{3,0,2,1:T(8,128)S(1)}, u32[]{:S(2)}, u32[]{:S(2)}) collective-permute-start(f32[64,2,4,128]{3,0,2,1:T(8,128)S(1)} %pad_maximum_fusion.4), channel_id=1, source_target_pairs={{0,16},{16,0},{1,17},{17,1},{2,18},{18,2},{3,19},{19,3},{4,20},{20... | collective-permute-start | bytes 786440 | tf_op jit(solution)/shard_map/ppermute | solution.py:243
  78.2 3.6 %fusion = f32[64,4,2,256]{3,0,2,1:T(8,128)S(1)} fusion(f32[64,4,1,4096]{3,0,2,1:T(8,128)S(1)} %get-tuple-element.12, f32[64,4,1,4096]{3,0,2,1:T(8,128)S(1)} %get-tuple-element.11, f32[128,4096]{1,0:T(8,128)S(1)} %bitcast.45, f32[128,4096]{1,0:T(8,128)S(1)} %bitcast.43), kind=kOutput, calls=%fused_computation | convolution fusion | flops 3224371200 | bytes 13107200 | tf_op jit(solution)/shard_map/xzca,da->xzcd/dot_general | solution.py:95
  82.0 21.9 %all_to_all.15 = f32[16,4,2,4,128]{4,1,3,2,0:T(4,128)S(1)} all-to-all(f32[16,4,2,4,128]{4,1,3,2,0:T(4,128)S(1)} %copy.34), channel_id=1, replica_groups=mesh['atom_pairs'=16,'atom_core'=2,'loops'=16] {'atom_pairs'}, dimensions={0} | all-to-all | bytes 524288 | tf_op jit(solution)/shard_map/all_to_all | solution.py:247
  104.0 0.6 fusion.16
  (18 shorter events, 0.6 us)
Async XLA Ops:
  12.6 16.1 %all-to-all-start = ((f32[3,16,2,128]{3,2,0,1:T(2,128)}), f32[3,16,2,128]{3,2,0,1:T(2,128)S(1)}, u32[]{:S(2)}, u32[]{:S(2)}) async-start(f32[3,16,2,128]{3,2,0,1:T(2,128)} %copy.26), calls=%async_computation | async-start | bytes 98304 | tf_op jit(solution)/shard_map/all_to_all | solution.py:218
  29.3 10.8 %all-to-all-start.1 = ((f32[3,16,2,128]{3,2,0,1:T(2,128)}), f32[3,16,2,128]{3,2,0,1:T(2,128)S(1)}, u32[]{:S(2)}, u32[]{:S(2)}) async-start(f32[3,16,2,128]{3,2,0,1:T(2,128)} %broadcast_in_dim.2), calls=%async_computation.1 | async-start | bytes 98304 | tf_op jit(solution)/shard_map/all_to_all | solution.py:221
  63.1 2.9 %copy-start = (f32[64,4096]{1,0:T(8,128)S(1)}, f32[64,4096]{1,0:T(8,128)}, u32[]{:S(2)}) copy-start(f32[64,4096]{1,0:T(8,128)} %mul.442) | copy-start | bytes 3145732
  72.1 9.7 %collective-permute-start = (f32[64,2,4,128]{3,0,2,1:T(8,128)S(1)}, f32[64,2,4,128]{3,0,2,1:T(8,128)S(1)}, u32[]{:S(2)}, u32[]{:S(2)}) collective-permute-start(f32[64,2,4,128]{3,0,2,1:T(8,128)S(1)} %pad_maximum_fusion.4), channel_id=1, source_target_pairs={{0,16},{16,0},{1,17},{17,1},{2,18},{18,2},{3,19},{19,3},{4,20},{20... | collective-permute-start | bytes 786440 | tf_op jit(solution)/shard_map/ppermute | solution.py:243

commit v7 on v6

--- a/solution.py
+++ b/solution.py
@@ -107,25 +107,29 @@
 FINE_STEPS = 16
 
 
-def sincos_rows(waves_row, values):
-    coarse = waves_row[::FINE_STEPS]
-    fine = waves_row[:FINE_STEPS] - waves_row[0]
+def sincos_rows(coarse, fine, values):
     coarse_angle = coarse[:, None] * values[None, :]
     fine_angle = fine[:, None] * values[None, :]
     cc, sc = jnp.cos(coarse_angle), jnp.sin(coarse_angle)
     cf, sf = jnp.cos(fine_angle), jnp.sin(fine_angle)
     cosines = cc[:, None, :] * cf[None, :, :] - sc[:, None, :] * sf[None, :, :]
     sines = sc[:, None, :] * cf[None, :, :] + cc[:, None, :] * sf[None, :, :]
-    shape = (waves_row.shape[0], values.shape[0])
+    shape = (coarse.shape[0] * fine.shape[0], values.shape[0])
     return cosines.reshape(shape), sines.reshape(shape)
 
 
-def phase_tables(position, xwaves, ywaves, zwaves):
-    xcosines, xsines = sincos_rows(xwaves, position[0])
-    ycosines, ysines = sincos_rows(ywaves, position[1])
+def steps_of(waves_row, picked=None):
+    fine = waves_row[:FINE_STEPS] - waves_row[0]
+    if picked is not None:
+        fine = jnp.take(fine, picked)
+    return waves_row[::FINE_STEPS], fine
+
+
+def phase_tables(position, ywaves, zwaves):
+    ycosines, ysines = sincos_rows(*steps_of(ywaves), position[1])
     zangle = zwaves[:, None] * position[2][None, :]
     ytable = jnp.concatenate([ycosines, ysines], axis=0)
-    return (xcosines, xsines, jnp.cos(zangle), jnp.sin(zangle), ytable)
+    return jnp.cos(zangle), jnp.sin(zangle), ytable
 
 
 HALF_BURGERS = float(BURGERS_TABLE[0, 0])
@@ -229,19 +233,20 @@
     zwaves = waves(zfirst, zrows, QZ, 0.0)
     ywaves = waves(jnp.float32(0.0), QY, QY, 1.0)
     xwaves = waves(jnp.float32(0.0), QX, QX, 1.0)
-    xcosines, xsines, zcosines, zsines, ytable = phase_tables(position, xwaves, ywaves, zwaves)
+    zcosines, zsines, ytable = phase_tables(position, ywaves, zwaves)
     outer = lax.axis_size(ATOM_OUTER)
     core = lax.axis_index(ATOM_CORE)
-    split = (outer, 2, xcosines.shape[0] // (2 * outer), xcosines.shape[1])
-
-    def rows_of(table, side):
-        picked = lax.dynamic_index_in_dim(table.reshape(split), side, axis=1, keepdims=False)
-        return picked.reshape(-1, table.shape[1])
-
-    away = 1 - core
-    sent = factor_block(rows_of(xcosines, away), rows_of(xsines, away), zcosines, zsines, ytable)
+    block = QX // (2 * outer)
+    lanes = np.arange(FINE_STEPS)
+    first_side = jnp.asarray(lanes[(lanes // block) % 2 == 0], jnp.int32)
+
+    def half(side):
+        xcosines, xsines = sincos_rows(*steps_of(xwaves, first_side + block * side), position[0])
+        return factor_block(xcosines, xsines, zcosines, zsines, ytable)
+
+    sent = half(1 - core)
     arrived = lax.ppermute(sent, ATOM_CORE, [(0, 1), (1, 0)])
-    kept = factor_block(rows_of(xcosines, core), rows_of(xsines, core), zcosines, zsines, ytable)
+    kept = half(core)
     partial = kept + arrived
     blocks = partial.reshape(outer, -1, *partial.shape[1:])
     summed = lax.all_to_all(blocks, ATOM_OUTER, 0, 0, tiled=True).sum(axis=0)

time: 105 us -> 84.7 us (0.81)
  local copies, waits for them, and re-layouts: 17.2 us -> 3.61 us
  other arithmetic: 14.6 us -> 10 us
  waiting for transfers between devices: 14 us -> 11.9 us
    mul x12 -> x0, local copies, waits for them, and re-layouts: 13.2 us -> none  [the longest x8 8.34 us: sincos_rows(): cosines = cc[:, None, :] * cf[None, :, :] - sc[:, None, :] * sf[None, :, :]]
    sub x2, other arithmetic: 4.3 us -> 1.14 us  [sincos_rows(): cosines = cc[:, None, :] * cf[None, :, :] - sc[:, None, :] * sf[None, :, :]]
    all_to_all x1, waiting for transfers between devices: 7.21 us -> 4.57 us  [body(): lax.all_to_all(field.reshape(3, loop_groups, rows, field.shape[2]), 'loop...]
    cos x2 -> x1, other arithmetic: 2.97 us -> 0.54 us  [phase_tables(): return (jnp.cos(zangle), jnp.sin(zangle), ytable)]
    dynamic_slice x1 -> x0, local copies, waits for them, and re-layouts: 1.7 us -> none  [rows_of(): lax.dynamic_index_in_dim(table.reshape(split), side, axis=1, keepdims=False)]
    select_n x0 -> x2, other arithmetic: none -> 1.33 us  [steps_of(): fine = jnp.take(fine, picked)]
    gather x0 -> x2, local copies, waits for them, and re-layouts: none -> 1.29 us  [steps_of(): fine = jnp.take(fine, picked)]
    cos x1 -> x2, other arithmetic: 2.64 us -> 2.87 us  [sincos_rows(): cf, sf = (jnp.cos(fine_angle), jnp.sin(fine_angle))]
  transfers between devices with their start and end apart: 3 -> 3, of which waited for: 2 -> 2; matrix products, arithmetic and copies ran while one was open for 4% -> 8% of each run, Pallas kernels for 0% -> 0%
where the time goes in v7:
time: 84.7 us; the launch traced here: 84.2 us
  blocking collectives  21.9 us (26%)
  starting transfers between devices  18.2 us (21%)
  waiting for transfers between devices  11.9 us (14%)
  Pallas kernels  11.1 us (13%)
  other arithmetic  10 us (12%)
  matrix products  7.29 us (9%)
  local copies, waits for them, and re-layouts  3.61 us (4%)
    all_to_all x1, blocking collectives, body(): summed = lax.all_to_all(blocks, ATOM_OUTER, 0, 0, tiled=True).sum(axis=0)  21.9 us
    pallas_call x1, Pallas kernels, anchor_and_field(): pl.pallas_call(field_kernel, in_specs=[smem, smem, smem, smem, vmem], out...  11.1 us
    all_to_all x1, starting transfers between devices, body(): lax.all_to_all(field.reshape(3, loop_groups, rows, field.shape[2]), 'loop...  8.68 us
    all_to_all x1, waiting for transfers between devices, body(): lax.all_to_all(jnp.broadcast_to(owned[:, None], (3, loop_groups, *owned.s...  7.31 us
    dot_general x2, matrix products, factor_block(): jnp.einsum('xzca,da->xzcd', left_pair, ytable, precision=lax.Precision.HI...  7.29 us
    ppermute x1, starting transfers between devices, body(): arrived = lax.ppermute(sent, ATOM_CORE, [(0, 1), (1, 0)])  6.04 us
    all_to_all x1, waiting for transfers between devices, body(): lax.all_to_all(field.reshape(3, loop_groups, rows, field.shape[2]), 'loop...  4.57 us
    all_to_all x1, starting transfers between devices, body(): lax.all_to_all(jnp.broadcast_to(owned[:, None], (3, loop_groups, *owned.s...  3.49 us
  transfers between devices with their start and end apart: 3, of which 2 were waited for; matrix products, arithmetic and copies ran while one was open for 8% of the time, Pallas kernels for 0%

profile of v7, /device:TPU:1, one launch (start us, length us, event | category | flops | bytes accessed | tf_op | source)
XLA Modules:
  0.0 84.2 jit_solution(7417775852060154995)
XLA Ops:
  0.0 11.1 %shard_map.64 = (f32[3,32,128]{2,1,0:T(8,128)}, f32[3,32,128]{2,1,0:T(8,128)}) custom-call(s32[3,256]{1,0:T(4,128)} %cells.1, s32[256]{0:T(256)} %burgers_index.1, s32[256]{0:T(256)} %habit_index.1, f32[256]{0:T(256)} %radius.1, s32[32,128]{1,0:T(8,128)} %bitcast.61), custom_call_target="tpu_custom_call" | custom-call | flops 57671680 | bytes 114688 | tf_op jit(solution)/shard_map/pallas_call | solution.py:207
  11.1 1.4 %copy.27 = f32[3,16,2,128]{3,2,0,1:T(2,128)} copy(f32[3,16,2,128]{3,2,1,0:T(2,128)} %bitcast.59) | data formatting | bytes 98304 | tf_op jit(solution)/shard_map/reshape | solution.py:223
  12.6 8.7 %all-to-all-start = ((f32[3,16,2,128]{3,2,0,1:T(2,128)}), f32[3,16,2,128]{3,2,0,1:T(2,128)S(1)}, u32[]{:S(2)}, u32[]{:S(2)}) async-start(f32[3,16,2,128]{3,2,0,1:T(2,128)} %copy.27), calls=%async_computation | async-start | bytes 98304 | tf_op jit(solution)/shard_map/all_to_all | solution.py:222
  21.3 0.7 compare_select_fusion.1
  22.0 0.6 gather_fusion
  22.6 0.6 gather_fusion.1
  23.3 0.7 and_select_fusion.1
  23.9 0.1 slice.65
  24.0 4.6 %all-to-all-done = f32[3,16,2,128]{3,2,0,1:T(2,128)S(1)} async-done(((f32[3,16,2,128]{3,2,0,1:T(2,128)}), f32[3,16,2,128]{3,2,0,1:T(2,128)S(1)}, u32[]{:S(2)}, u32[]{:S(2)}) %all-to-all-start) | async-done | bytes 49184 | tf_op jit(solution)/shard_map/all_to_all | solution.py:222
  28.6 0.6 broadcast_in_dim.4
  29.3 3.5 %all-to-all-start.1 = ((f32[3,16,2,128]{3,2,0,1:T(2,128)}), f32[3,16,2,128]{3,2,0,1:T(2,128)S(1)}, u32[]{:S(2)}, u32[]{:S(2)}) async-start(f32[3,16,2,128]{3,2,0,1:T(2,128)} %broadcast_in_dim.4), calls=%async_computation.1 | async-start | bytes 98304 | tf_op jit(solution)/shard_map/all_to_all | solution.py:225
  32.8 7.3 %all-to-all-done.1 = f32[3,16,2,128]{3,2,0,1:T(2,128)S(1)} async-done(((f32[3,16,2,128]{3,2,0,1:T(2,128)}), f32[3,16,2,128]{3,2,0,1:T(2,128)S(1)}, u32[]{:S(2)}, u32[]{:S(2)}) %all-to-all-start.1) | async-done | bytes 49184 | tf_op jit(solution)/shard_map/all_to_all | solution.py:225
  40.1 0.1 reshape.596
  40.2 0.8 %bitcast_add_fusion = f32[3,4096]{1,0:T(4,128)S(1)} fusion(f32[3,4096]{1,0:T(4,128)S(1)} %reshape.596, f32[1,3,32,128]{3,2,1,0:T(8,128)} %bitcast.60), kind=kLoop, calls=%fused_computation.46 | loop fusion | flops 12288 | bytes 147456 | tf_op jit(solution)/shard_map/add | solution.py:228
  41.1 1.0 %multiply_cosine_fusion = (f32[16,4096]{1,0:T(8,128)S(1)}, f32[16,4096]{1,0:T(8,128)S(1)}) fusion(f32[4096]{0:T(1024)S(1)} %bitcast.55, f32[16]{0:T(128)S(1)} %slice_subtract_fusion.1), kind=kLoop, calls=%fused_computation.23 | loop fusion | flops 65536 | bytes 540736 | tf_op jit(solution)/shard_map/cos | solution.py:114
  42.0 0.5 multiply_cosine_fusion.5
  42.6 1.9 %multiply_cosine_fusion.3 = (f32[8,4096]{1,0:T(8,128)S(1)}, f32[8,4096]{1,0:T(8,128)S(1)}, f32[8,4096]{1,0:T(8,128)S(1)}, f32[8,4096]{1,0:T(8,128)S(1)}, f32[8,4...) fusion(f32[8]{0:T(128)S(1)} %get-tuple-element.47, ...), kind=kLoop, calls=%fused_computation.31 | loop fusion | flops 131072 | bytes 1081440 | tf_op jit(solution)/shard_map/cos | solution.py:114
  44.5 0.6 multiply_subtract_fusion.2
  45.1 0.6 subtract_bitcast_fusion.1
  45.6 2.4 %multiply_subtract_fusion.1 = (f32[64,4,1,4096]{3,0,2,1:T(8,128)S(1)}, f32[64,4,1,4096]{3,0,2,1:T(8,128)S(1)}, f32[64,4,1,4096]{3,0,2,1:T(8,128)S(1)}, f32[64,4,1,4096]{3,0,2,1:T(8,128)S(1)}) fusion(f32[64,4096]{1,0:T(8,128)S(1)} %get-tuple-element.17, f32[4,4096]{1,0:T(4,128)S(1)} %get-tuple-element.36, f32[64,4096]{1,0:T(8,128)S(1)} %get-tuple-element.16, ...), kind=kLoop, calls=%fused_computation.15 | loop fusion | flops 12582912 | bytes 21102592 | tf_op jit(solution)/shard_map/sub | solution.py:89
  48.0 3.6 %fusion.4 = f32[64,4,2,256]{3,0,1,2:T(8,128)S(1)} fusion(f32[128,4096]{1,0:T(8,128)S(1)} %bitcast.52, f32[128,4096]{1,0:T(8,128)S(1)} %bitcast.50, f32[64,4,1,4096]{3,0,2,1:T(8,128)S(1)} %get-tuple-element.24, f32[64,4,1,4096]{3,0,2,1:T(8,128)S(1)} %get-tuple-element.25), kind=kOutput, calls=%fused_computation.7 | convolution fusion | flops 3224371200 | bytes 13107200 | tf_op jit(solution)/shard_map/xzca,da->xzcd/dot_general | solution.py:95
  51.8 6.0 %collective-permute-start = (f32[64,2,4,128]{3,0,2,1:T(8,128)S(1)}, f32[64,2,4,128]{3,0,2,1:T(8,128)S(1)}, u32[]{:S(2)}, u32[]{:S(2)}) collective-permute-start(f32[64,2,4,128]{3,0,2,1:T(8,128)S(1)} %pad_maximum_fusion.4), channel_id=1, source_target_pairs={{0,16},{16,0},{1,17},{17,1},{2,18},{18,2},{3,19},{19,3},{4,20},{20... | collective-permute-start | bytes 786440 | tf_op jit(solution)/shard_map/ppermute | solution.py:248
  57.8 3.6 %fusion = f32[64,4,2,256]{3,0,2,1:T(8,128)S(1)} fusion(f32[64,4,1,4096]{3,0,2,1:T(8,128)S(1)} %get-tuple-element.11, f32[64,4,1,4096]{3,0,2,1:T(8,128)S(1)} %get-tuple-element.10, f32[128,4096]{1,0:T(8,128)S(1)} %bitcast.53, f32[128,4096]{1,0:T(8,128)S(1)} %bitcast.51), kind=kOutput, calls=%fused_computation.2 | convolution fusion | flops 3224371200 | bytes 13107200 | tf_op jit(solution)/shard_map/xzca,da->xzcd/dot_general | solution.py:95
  61.5 0.0 collective-permute-done
  61.6 0.1 copy.35
  61.6 21.9 %all_to_all.15 = f32[16,4,2,4,128]{4,1,3,2,0:T(4,128)S(1)} all-to-all(f32[16,4,2,4,128]{4,1,3,2,0:T(4,128)S(1)} %copy.35), channel_id=1, replica_groups=mesh['atom_pairs'=16,'atom_core'=2,'loops'=16] {'atom_pairs'}, dimensions={0} | all-to-all | bytes 524288 | tf_op jit(solution)/shard_map/all_to_all | solution.py:252
  83.6 0.1 reduce_sum.19
  83.6 0.6 fusion.16
  (12 shorter events, 0.3 us)
Async XLA Ops:
  12.6 16.1 %all-to-all-start = ((f32[3,16,2,128]{3,2,0,1:T(2,128)}), f32[3,16,2,128]{3,2,0,1:T(2,128)S(1)}, u32[]{:S(2)}, u32[]{:S(2)}) async-start(f32[3,16,2,128]{3,2,0,1:T(2,128)} %copy.27), calls=%async_computation | async-start | bytes 98304 | tf_op jit(solution)/shard_map/all_to_all | solution.py:222
  29.3 10.8 %all-to-all-start.1 = ((f32[3,16,2,128]{3,2,0,1:T(2,128)}), f32[3,16,2,128]{3,2,0,1:T(2,128)S(1)}, u32[]{:S(2)}, u32[]{:S(2)}) async-start(f32[3,16,2,128]{3,2,0,1:T(2,128)} %broadcast_in_dim.4), calls=%async_computation.1 | async-start | bytes 98304 | tf_op jit(solution)/shard_map/all_to_all | solution.py:225
  51.8 9.8 %collective-permute-start = (f32[64,2,4,128]{3,0,2,1:T(8,128)S(1)}, f32[64,2,4,128]{3,0,2,1:T(8,128)S(1)}, u32[]{:S(2)}, u32[]{:S(2)}) collective-permute-start(f32[64,2,4,128]{3,0,2,1:T(8,128)S(1)} %pad_maximum_fusion.4), channel_id=1, source_target_pairs={{0,16},{16,0},{1,17},{17,1},{2,18},{18,2},{3,19},{19,3},{4,20},{20... | collective-permute-start | bytes 786440 | tf_op jit(solution)/shard_map/ppermute | solution.py:248

commit v8 on v7

--- a/solution.py
+++ b/solution.py
@@ -107,11 +107,13 @@
 FINE_STEPS = 16
 
 
-def sincos_rows(coarse, fine, values):
+def sincos_rows(coarse, fine, values, fine_major=False):
     coarse_angle = coarse[:, None] * values[None, :]
     fine_angle = fine[:, None] * values[None, :]
     cc, sc = jnp.cos(coarse_angle), jnp.sin(coarse_angle)
     cf, sf = jnp.cos(fine_angle), jnp.sin(fine_angle)
+    if fine_major:
+        cc, sc, cf, sf = cf, sf, cc, sc
     cosines = cc[:, None, :] * cf[None, :, :] - sc[:, None, :] * sf[None, :, :]
     sines = sc[:, None, :] * cf[None, :, :] + cc[:, None, :] * sf[None, :, :]
     shape = (coarse.shape[0] * fine.shape[0], values.shape[0])
@@ -226,7 +228,7 @@
         jnp.broadcast_to(owned[:, None], (3, loop_groups, *owned.shape[1:])), "loops", 1, 1, tiled=True
     ).reshape(3, -1)
     position = anchor + displacement
-    group_count = lax.axis_size((ATOM_OUTER, ATOM_CORE))
+    group_count = lax.axis_size((ATOM_OUTER, ATOM_PAIR, ATOM_CORE))
     zrows = QZ // lax.axis_size("loops")
     atom_total = position.shape[1] * group_count
     zfirst = (lax.axis_index("loops") * zrows).astype(jnp.float32)
@@ -236,35 +238,44 @@
     zcosines, zsines, ytable = phase_tables(position, ywaves, zwaves)
     outer = lax.axis_size(ATOM_OUTER)
     core = lax.axis_index(ATOM_CORE)
-    block = QX // (2 * outer)
-    lanes = np.arange(FINE_STEPS)
-    first_side = jnp.asarray(lanes[(lanes // block) % 2 == 0], jnp.int32)
-
-    def half(side):
-        xcosines, xsines = sincos_rows(*steps_of(xwaves, first_side + block * side), position[0])
-        return factor_block(xcosines, xsines, zcosines, zsines, ytable)
-
-    sent = half(1 - core)
-    arrived = lax.ppermute(sent, ATOM_CORE, [(0, 1), (1, 0)])
-    kept = half(core)
-    partial = kept + arrived
-    blocks = partial.reshape(outer, -1, *partial.shape[1:])
-    summed = lax.all_to_all(blocks, ATOM_OUTER, 0, 0, tiled=True).sum(axis=0)
+    pair = lax.axis_index(ATOM_PAIR)
+    block = QX // (4 * outer)
+    run = jnp.arange(block, dtype=jnp.int32)
+
+    def rows(fine_picked):
+        tables = sincos_rows(*steps_of(xwaves, fine_picked), position[0], fine_major=True)
+        return factor_block(*tables, zcosines, zsines, ytable)
+
+    for_core = jnp.concatenate([run, run + 2 * block]) + block * (1 - core)
+    arrived = lax.ppermute(rows(for_core), ATOM_CORE, [(0, 1), (1, 0)])
+    arrived = arrived.reshape(2, -1, *arrived.shape[1:])
+    mine = 2 * block * pair + block * core
+    away = rows(2 * block * (1 - pair) + block * core + run)
+    away = away + lax.dynamic_index_in_dim(arrived, 1 - pair, axis=0, keepdims=False)
+    away, kept_picked = lax.optimization_barrier((away, mine + run))
+    returned = lax.ppermute(away, ATOM_PAIR, [(0, 1), (1, 0)])
+    kept = rows(kept_picked)
+    kept = kept + lax.dynamic_index_in_dim(arrived, pair, axis=0, keepdims=False)
+    partial = kept + returned
+    blocks = partial.reshape(block, outer, *partial.shape[1:])
+    summed = lax.all_to_all(blocks, ATOM_OUTER, 1, 1, tiled=True).sum(axis=1)
     power = summed[:, 0] ** 2 + summed[:, 1] ** 2
     return jnp.log1p(jnp.transpose(power, (1, 0, 2)) / atom_total)
 
 
-ATOM_OUTER = "atom_pairs"
+ATOM_OUTER = "atom_outer"
+ATOM_PAIR = "atom_pair"
 ATOM_CORE = "atom_core"
 
 
 def solution(mesh):
     groups, loop_groups = mesh.devices.shape
-    paired = Mesh(
-        mesh.devices.reshape(groups // 2, 2, loop_groups), (ATOM_OUTER, ATOM_CORE, "loops")
-    )
-    atoms = (ATOM_OUTER, ATOM_CORE)
+    split = Mesh(
+        mesh.devices.reshape(groups // 4, 2, 2, loop_groups),
+        (ATOM_OUTER, ATOM_PAIR, ATOM_CORE, "loops"),
+    )
+    atoms = (ATOM_OUTER, ATOM_PAIR, ATOM_CORE)
     placed = (P(atoms), P(None, "loops"), P("loops"), P("loops"), P("loops"))
     return jax.shard_map(
-        body, mesh=paired, in_specs=placed, out_specs=P("loops", atoms, None), check_vma=False
-    )
+        body, mesh=split, in_specs=placed, out_specs=P("loops", atoms, None), check_vma=False
+    )

time: 84.7 us -> 89.8 us (1.060)
  starting transfers between devices: 18.2 us -> 21.5 us
  local copies, waits for them, and re-layouts: 3.61 us -> 5.24 us
  blocking collectives: 21.9 us -> 20.6 us
  waiting for transfers between devices: 11.9 us -> 13 us
  matrix products: 7.29 us -> 8.19 us
    ppermute x1 -> x2, starting transfers between devices: 6.04 us -> 9.34 us  [the longest x1 6.04 us: body(): arrived = lax.ppermute(rows(for_core), ATOM_CORE, [(0, 1), (1, 0)])]
    all_to_all x1, blocking collectives: 21.9 us -> 20.6 us  [body(): summed = lax.all_to_all(blocks, ATOM_OUTER, 1, 1, tiled=True).sum(axis=1)]
    select_n x2 -> x6, other arithmetic: 1.33 us -> 0.18 us  [steps_of(): fine = jnp.take(fine, picked)]
    all_to_all x1, waiting for transfers between devices: 4.57 us -> 5.65 us  [body(): lax.all_to_all(field.reshape(3, loop_groups, rows, field.shape[2]), 'loop...]
    unnamed x0 -> x4, local copies, waits for them, and re-layouts: none -> 1.01 us
    dot_general x2 -> x3, matrix products: 7.29 us -> 8.19 us  [factor_block(): jnp.einsum('xzca,da->xzcd', left_pair, ytable, precision=lax.Precision.HI...]
    gather x2 -> x3, local copies, waits for them, and re-layouts: 1.29 us -> 1.93 us  [steps_of(): fine = jnp.take(fine, picked)]
    cos x2 -> x4, other arithmetic: 2.87 us -> 3.5 us  [sincos_rows(): cf, sf = (jnp.cos(fine_angle), jnp.sin(fine_angle))]
  transfers between devices with their start and end apart: 3 -> 4, of which waited for: 2 -> 2; matrix products, arithmetic and copies ran while one was open for 8% -> 9% of each run, Pallas kernels for 0% -> 0%
where the time goes in v8:
time: 89.8 us; the launch traced here: 89.3 us
  starting transfers between devices  21.5 us (24%)
  blocking collectives  20.6 us (23%)
  waiting for transfers between devices  13 us (14%)
  Pallas kernels  11.1 us (12%)
  other arithmetic  9.38 us (10%)
  matrix products  8.19 us (9%)
  local copies, waits for them, and re-layouts  5.24 us (6%)
    all_to_all x1, blocking collectives, body(): summed = lax.all_to_all(blocks, ATOM_OUTER, 1, 1, tiled=True).sum(axis=1)  20.6 us
    pallas_call x1, Pallas kernels, anchor_and_field(): pl.pallas_call(field_kernel, in_specs=[smem, smem, smem, smem, vmem], out...  11.1 us
    all_to_all x1, starting transfers between devices, body(): lax.all_to_all(field.reshape(3, loop_groups, rows, field.shape[2]), 'loop...  8.68 us
    dot_general x3, matrix products, factor_block(): jnp.einsum('xzca,da->xzcd', left_pair, ytable, precision=lax.Precision.HI...  8.19 us
    all_to_all x1, waiting for transfers between devices, body(): lax.all_to_all(jnp.broadcast_to(owned[:, None], (3, loop_groups, *owned.s...  7.31 us
    ppermute x1, starting transfers between devices, body(): arrived = lax.ppermute(rows(for_core), ATOM_CORE, [(0, 1), (1, 0)])  6.04 us
    all_to_all x1, waiting for transfers between devices, body(): lax.all_to_all(field.reshape(3, loop_groups, rows, field.shape[2]), 'loop...  5.65 us
    cos x4, other arithmetic, sincos_rows(): cf, sf = (jnp.cos(fine_angle), jnp.sin(fine_angle))  3.5 us
  transfers between devices with their start and end apart: 4, of which 2 were waited for; matrix products, arithmetic and copies ran while one was open for 9% of the time, Pallas kernels for 0%

profile of v8, /device:TPU:1, one launch (start us, length us, event | category | flops | bytes accessed | tf_op | source)
XLA Modules:
  0.0 89.3 jit_solution(4173530958379288618)
XLA Ops:
  0.0 11.1 %shard_map.55 = (f32[3,32,128]{2,1,0:T(8,128)}, f32[3,32,128]{2,1,0:T(8,128)}) custom-call(s32[3,256]{1,0:T(4,128)} %cells.1, s32[256]{0:T(256)} %burgers_index.1, s32[256]{0:T(256)} %habit_index.1, f32[256]{0:T(256)} %radius.1, s32[32,128]{1,0:T(8,128)} %bitcast.100), custom_call_target="tpu_custom_call" | custom-call | flops 57671680 | bytes 114688 | tf_op jit(solution)/shard_map/pallas_call | solution.py:209
  11.1 1.4 %copy.38 = f32[3,16,2,128]{3,2,0,1:T(2,128)} copy(f32[3,16,2,128]{3,2,1,0:T(2,128)} %bitcast.98) | data formatting | bytes 98304 | tf_op jit(solution)/shard_map/reshape | solution.py:225
  12.5 8.7 %all-to-all-start = ((f32[3,16,2,128]{3,2,0,1:T(2,128)}), f32[3,16,2,128]{3,2,0,1:T(2,128)S(1)}, u32[]{:S(2)}, u32[]{:S(2)}) async-start(f32[3,16,2,128]{3,2,0,1:T(2,128)} %copy.38), calls=%async_computation | async-start | bytes 98304 | tf_op jit(solution)/shard_map/all_to_all | solution.py:224
  21.3 0.1 slice.86
  21.5 0.6 gather_fusion
  22.2 0.6 gather_fusion.1
  22.9 5.7 %all-to-all-done = f32[3,16,2,128]{3,2,0,1:T(2,128)S(1)} async-done(((f32[3,16,2,128]{3,2,0,1:T(2,128)}), f32[3,16,2,128]{3,2,0,1:T(2,128)S(1)}, u32[]{:S(2)}, u32[]{:S(2)}) %all-to-all-start) | async-done | bytes 49184 | tf_op jit(solution)/shard_map/all_to_all | solution.py:224
  28.6 0.6 broadcast_in_dim.5
  29.3 3.5 %all-to-all-start.1 = ((f32[3,16,2,128]{3,2,0,1:T(2,128)}), f32[3,16,2,128]{3,2,0,1:T(2,128)S(1)}, u32[]{:S(2)}, u32[]{:S(2)}) async-start(f32[3,16,2,128]{3,2,0,1:T(2,128)} %broadcast_in_dim.5), calls=%async_computation.1 | async-start | bytes 98304 | tf_op jit(solution)/shard_map/all_to_all | solution.py:227
  32.8 7.3 %all-to-all-done.1 = f32[3,16,2,128]{3,2,0,1:T(2,128)S(1)} async-done(((f32[3,16,2,128]{3,2,0,1:T(2,128)}), f32[3,16,2,128]{3,2,0,1:T(2,128)S(1)}, u32[]{:S(2)}, u32[]{:S(2)}) %all-to-all-start.1) | async-done | bytes 49184 | tf_op jit(solution)/shard_map/all_to_all | solution.py:227
  40.2 0.8 bitcast_add_fusion
  41.1 1.0 %multiply_cosine_fusion = (f32[16,4096]{1,0:T(8,128)S(1)}, f32[16,4096]{1,0:T(8,128)S(1)}) fusion(f32[4096]{0:T(1024)S(1)} %bitcast.95, f32[16]{0:T(128)S(1)} %slice_subtract_fusion.1), kind=kLoop, calls=%fused_computation.33 | loop fusion | flops 65536 | bytes 540736 | tf_op jit(solution)/shard_map/cos | solution.py:114
  42.0 0.5 multiply_cosine_fusion.6
  42.6 1.4 %multiply_cosine_fusion.1 = (f32[8,4096]{1,0:T(8,128)S(1)}, f32[8,4096]{1,0:T(8,128)S(1)}, f32[8,4096]{1,0:T(8,128)S(1)}, f32[8,4096]{1,0:T(8,128)S(1)}, f32[8,4096]{1,0:T(8,128)S(1)}, /*index=5*/f32[8,4096]{1,0:T(8,128)S(1)}) fusion(f32[8]{0:T(128)S(1)} %and_select_fusion.2, f32[4096]{0:T(1024)S(1)} %bitcast.92, f32[8]{0:T(128)S(1)} %slice.86, ...), kind=kLoop, calls=%fused_computation.36 | loop fusion | flops 98304 | bytes 819264 | tf_op jit(solution)/shard_map/cos | solution.py:114
  44.0 0.3 subtract_bitcast_fusion
  44.3 1.2 %multiply_subtract_fusion = (f32[64,4,1,4096]{3,0,2,1:T(8,128)S(1)}, f32[64,4,1,4096]{3,0,2,1:T(8,128)S(1)}) fusion(f32[64,4096]{1,0:T(8,128)S(1)} %get-tuple-element.23, f32[4,4096]{1,0:T(4,128)S(1)} %get-tuple-element.42, f32[64,4096]{1,0:T(8,128)S(1)} %get-tuple-element.22, f32[4,4096]{1,0:T(4,128)S(1)} %get-tuple-element.41), kind=kLoop, calls=%fused_computation.19 | loop fusion | flops 6291456 | bytes 10616832 | tf_op jit(solution)/shard_map/sub | solution.py:89
  45.5 0.6 multiply_subtract_fusion.2
  46.1 3.6 %fusion = f32[64,4,2,256]{3,0,2,1:T(8,128)S(1)} fusion(f32[64,4,1,4096]{3,0,2,1:T(8,128)S(1)} %get-tuple-element.15, f32[64,4,1,4096]{3,0,2,1:T(8,128)S(1)} %get-tuple-element.14, f32[128,4096]{1,0:T(8,128)S(1)} %bitcast.87, f32[128,4096]{1,0:T(8,128)S(1)} %bitcast.84), kind=kOutput, calls=%fused_computation.3 | convolution fusion | flops 3224371200 | bytes 13107200 | tf_op jit(solution)/shard_map/xzca,da->xzcd/dot_general | solution.py:95
  49.8 6.0 %collective-permute-start = (f32[64,2,4,128]{3,0,2,1:T(8,128)S(1)}, f32[64,2,4,128]{3,0,2,1:T(8,128)S(1)}, u32[]{:S(2)}, u32[]{:S(2)}) collective-permute-start(f32[64,2,4,128]{3,0,2,1:T(8,128)S(1)} %pad_maximum_fusion.5), channel_id=1, source_target_pairs={{0,16},{16,0},{1,17},{17,1},{2,18},{18,2},{3,19},{19,3},{4,20},{20... | collective-permute-start | bytes 786440 | tf_op jit(solution)/shard_map/ppermute | solution.py:250
  55.8 0.5 multiply_cosine_fusion.5
  56.4 0.1 subtract_bitcast_fusion.2
  56.5 0.6 multiply_subtract_fusion.3
  57.1 2.3 %fusion.4 = f32[32,4,2,256]{3,0,2,1:T(8,128)S(1)} fusion(f32[32,4,1,4096]{3,0,2,1:T(8,128)S(1)} %get-tuple-element.19, f32[32,4,1,4096]{3,0,2,1:T(8,128)S(1)} %get-tuple-element.18, f32[128,4096]{1,0:T(8,128)S(1)} %bitcast.88, f32[128,4096]{1,0:T(8,128)S(1)} %bitcast.85), kind=kOutput, calls=%fused_computation.7 | convolution fusion | flops 1612709888 | bytes 8650752 | tf_op jit(solution)/shard_map/xzca,da->xzcd/dot_general | solution.py:95
  59.5 0.6 gather_fusion.2
  60.2 0.5 multiply_cosine_fusion.4
  60.7 3.3 %collective-permute-start.1 = (f32[32,2,4,128]{3,0,2,1:T(8,128)S(1)}, f32[32,2,4,128]{3,0,2,1:T(8,128)S(1)}, u32[]{:S(2)}, u32[]{:S(2)}) collective-permute-start(f32[32,2,4,128]{3,0,2,1:T(8,128)S(1)} %maximum_add_fusion), channel_id=1, source_target_pairs={{0,32},{32,0},{1,33},{33,1},{2,34},{34,2},{3,35},{35,3},{4,36},{36... | collective-permute-start | bytes 393224 | tf_op jit(solution)/shard_map/ppermute | solution.py:256
  64.0 0.1 subtract_bitcast_fusion.1
  64.2 0.6 multiply_subtract_fusion.1
  64.7 1.0 %copy-done.1 = f32[8,16,4096]{2,1,0:T(8,128)S(1)} copy-done((f32[8,16,4096]{2,1,0:T(8,128)S(1)}, f32[8,16,4096]{2,1,0:T(8,128)}, u32[]{:S(2)}) %copy-start.1) | copy-done | bytes 2097176
  65.7 2.2 %fusion.10 = f32[32,4,2,256]{3,0,1,2:T(8,128)S(1)} fusion(f32[128,4096]{1,0:T(8,128)S(1)} %bitcast.89, f32[128,4096]{1,0:T(8,128)S(1)} %bitcast.86, f32[32,4,1,4096]{3,0,2,1:T(8,128)S(1)} %get-tuple-element.17, f32[32,4,1,4096]{3,0,2,1:T(8,128)S(1)} %get-tuple-element.16), kind=kOutput, calls=%fused_computation.15 | convolution fusion | flops 1612709888 | bytes 8650752 | tf_op jit(solution)/shard_map/xzca,da->xzcd/dot_general | solution.py:95
  68.1 20.6 %all_to_all.15 = f32[4,8,2,4,128]{4,0,3,2,1:T(4,128)S(1)} all-to-all(f32[4,8,2,4,128]{4,0,3,2,1:T(4,128)S(1)} %copy.50), channel_id=1, replica_groups=mesh['atom_outer'=8,'atom_pair'=2,'atom_core'=2,'loops'=16] {'atom_outer'}, dimensions={1} | all-to-all | bytes 262144 | tf_op jit(solution)/shard_map/all_to_all | solution.py:261
  88.7 0.6 fusion.26
  (36 shorter events, 0.7 us)
Async XLA Ops:
  12.5 16.1 %all-to-all-start = ((f32[3,16,2,128]{3,2,0,1:T(2,128)}), f32[3,16,2,128]{3,2,0,1:T(2,128)S(1)}, u32[]{:S(2)}, u32[]{:S(2)}) async-start(f32[3,16,2,128]{3,2,0,1:T(2,128)} %copy.38), calls=%async_computation | async-start | bytes 98304 | tf_op jit(solution)/shard_map/all_to_all | solution.py:224
  29.3 10.8 %all-to-all-start.1 = ((f32[3,16,2,128]{3,2,0,1:T(2,128)}), f32[3,16,2,128]{3,2,0,1:T(2,128)S(1)}, u32[]{:S(2)}, u32[]{:S(2)}) async-start(f32[3,16,2,128]{3,2,0,1:T(2,128)} %broadcast_in_dim.5), calls=%async_computation.1 | async-start | bytes 98304 | tf_op jit(solution)/shard_map/all_to_all | solution.py:227
  46.1 11.0 %copy-start = (f32[8,16,4096]{2,1,0:T(8,128)}, f32[8,16,4096]{2,1,0:T(8,128)S(1)}, u32[]{:S(2)}) copy-start(f32[8,16,4096]{2,1,0:T(8,128)S(1)} %get-tuple-element.21) | copy-start | bytes 6291460
  49.8 9.7 %collective-permute-start = (f32[64,2,4,128]{3,0,2,1:T(8,128)S(1)}, f32[64,2,4,128]{3,0,2,1:T(8,128)S(1)}, u32[]{:S(2)}, u32[]{:S(2)}) collective-permute-start(f32[64,2,4,128]{3,0,2,1:T(8,128)S(1)} %pad_maximum_fusion.5), channel_id=1, source_target_pairs={{0,16},{16,0},{1,17},{17,1},{2,18},{18,2},{3,19},{19,3},{4,20},{20... | collective-permute-start | bytes 786440 | tf_op jit(solution)/shard_map/ppermute | solution.py:250
  60.7 7.3 %collective-permute-start.1 = (f32[32,2,4,128]{3,0,2,1:T(8,128)S(1)}, f32[32,2,4,128]{3,0,2,1:T(8,128)S(1)}, u32[]{:S(2)}, u32[]{:S(2)}) collective-permute-start(f32[32,2,4,128]{3,0,2,1:T(8,128)S(1)} %maximum_add_fusion), channel_id=1, source_target_pairs={{0,32},{32,0},{1,33},{33,1},{2,34},{34,2},{3,35},{35,3},{4,36},{36... | collective-permute-start | bytes 393224 | tf_op jit(solution)/shard_map/ppermute | solution.py:256
  64.1 1.6 %copy-start.1 = (f32[8,16,4096]{2,1,0:T(8,128)S(1)}, f32[8,16,4096]{2,1,0:T(8,128)}, u32[]{:S(2)}) copy-start(f32[8,16,4096]{2,1,0:T(8,128)} %copy-done) | copy-start | bytes 6291460

commit v9 on v7

--- a/solution.py
+++ b/solution.py
@@ -136,6 +136,7 @@
 HABIT_SCALE = float(NORMAL_TABLE[0, 0])
 STRENGTH_SCALE = 1.0 / (8.0 * (1.0 - POISSON))
 FIELD_SPLIT = 2
+FIELD_UNROLL = 2
 
 
 def field_kernel(cells, burgers_index, habit_index, radius, site, anchor_out, field_out):
@@ -171,27 +172,33 @@
         r = radius[number]
         radius_sq = r * r
         scale = radius_sq * jnp.float32(STRENGTH_SCALE)
+        scaled_b = [jnp.float32(1.0 - 2.0 * POISSON) * v for v in (bx, by, bz)]
+        scaled_n = [jnp.float32(1.0 - 2.0 * POISSON) * v for v in (nx, ny, nz)]
         out = []
         for p in range(FIELD_SPLIT):
             ax, ay, az = pieces[p]
-            fx, fy, fz = running[p]
             dx, dy, dz = ax - cx, ay - cy, az - cz
             distance_sq = dx * dx + dy * dy + dz * dz + radius_sq
             inverse = lax.rsqrt(distance_sq)
-            ux, uy, uz = dx * inverse, dy * inverse, dz * inverse
-            along_b = bx * ux + by * uy + bz * uz
-            along_n = nx * ux + ny * uy + nz * uz
-            strength = scale * (inverse * inverse)
-            mixed = 3.0 * (along_b * along_n) - burgers_normal
-            gx = (1.0 - 2.0 * POISSON) * (bx * along_n + nx * along_b) + ux * mixed
-            gy = (1.0 - 2.0 * POISSON) * (by * along_n + ny * along_b) + uy * mixed
-            gz = (1.0 - 2.0 * POISSON) * (bz * along_n + nz * along_b) + uz * mixed
-            out.append((fx + strength * gx, fy + strength * gy, fz + strength * gz))
+            inverse_sq = inverse * inverse
+            toward_b = bx * dx + by * dy + bz * dz
+            toward_n = nx * dx + ny * dy + nz * dz
+            weight = scale * (inverse_sq * inverse)
+            mixed = (3.0 * inverse_sq) * (toward_b * toward_n) - burgers_normal
+            on_n = weight * toward_n
+            on_b = weight * toward_b
+            on_d = weight * mixed
+            out.append(
+                tuple(
+                    total + (sb * on_n + sn * on_b + d * on_d)
+                    for total, sb, sn, d in zip(running[p], scaled_b, scaled_n, (dx, dy, dz))
+                )
+            )
         return tuple(out)
 
     zero = jnp.zeros((rows, whole.shape[1]), jnp.float32)
     start = tuple((zero, zero, zero) for _ in range(FIELD_SPLIT))
-    totals = lax.fori_loop(0, radius.shape[0], one_loop, start, unroll=2)
+    totals = lax.fori_loop(0, radius.shape[0], one_loop, start, unroll=FIELD_UNROLL)
     for p in range(FIELD_SPLIT):
         for axis in range(3):
             field_out[axis, p * rows : (p + 1) * rows] = totals[p][axis]

time: 84.7 us -> 83.9 us (level)
  no operation moved by 1% of the time
where the time goes in v9:
time: 83.9 us; the launch traced here: 83.4 us
  blocking collectives  21.9 us (26%)
  starting transfers between devices  18.2 us (22%)
  waiting for transfers between devices  11.9 us (14%)
  Pallas kernels  10.3 us (12%)
  other arithmetic  10 us (12%)
  matrix products  7.29 us (9%)
  local copies, waits for them, and re-layouts  3.61 us (4%)
    all_to_all x1, blocking collectives, body(): summed = lax.all_to_all(blocks, ATOM_OUTER, 0, 0, tiled=True).sum(axis=0)  21.9 us
    pallas_call x1, Pallas kernels, anchor_and_field(): pl.pallas_call(field_kernel, in_specs=[smem, smem, smem, smem, vmem], out...  10.3 us
    all_to_all x1, starting transfers between devices, body(): lax.all_to_all(field.reshape(3, loop_groups, rows, field.shape[2]), 'loop...  8.68 us
    all_to_all x1, waiting for transfers between devices, body(): lax.all_to_all(jnp.broadcast_to(owned[:, None], (3, loop_groups, *owned.s...  7.31 us
    dot_general x2, matrix products, factor_block(): jnp.einsum('xzca,da->xzcd', left_pair, ytable, precision=lax.Precision.HI...  7.29 us
    ppermute x1, starting transfers between devices, body(): arrived = lax.ppermute(sent, ATOM_CORE, [(0, 1), (1, 0)])  6.04 us
    all_to_all x1, waiting for transfers between devices, body(): lax.all_to_all(field.reshape(3, loop_groups, rows, field.shape[2]), 'loop...  4.57 us
    all_to_all x1, starting transfers between devices, body(): lax.all_to_all(jnp.broadcast_to(owned[:, None], (3, loop_groups, *owned.s...  3.49 us
  transfers between devices with their start and end apart: 3, of which 2 were waited for; matrix products, arithmetic and copies ran while one was open for 8% of the time, Pallas kernels for 0%

profile of v9, /device:TPU:1, one launch (start us, length us, event | category | flops | bytes accessed | tf_op | source)
XLA Modules:
  0.0 83.4 jit_solution(8412441557924160615)
XLA Ops:
  0.0 10.3 %shard_map.64 = (f32[3,32,128]{2,1,0:T(8,128)}, f32[3,32,128]{2,1,0:T(8,128)}) custom-call(s32[3,256]{1,0:T(4,128)} %cells.1, s32[256]{0:T(256)} %burgers_index.1, s32[256]{0:T(256)} %habit_index.1, f32[256]{0:T(256)} %radius.1, s32[32,128]{1,0:T(8,128)} %bitcast.61), custom_call_target="tpu_custom_call" | custom-call | flops 57671680 | bytes 114688 | tf_op jit(solution)/shard_map/pallas_call | solution.py:214
  10.3 1.4 %copy.27 = f32[3,16,2,128]{3,2,0,1:T(2,128)} copy(f32[3,16,2,128]{3,2,1,0:T(2,128)} %bitcast.59) | data formatting | bytes 98304 | tf_op jit(solution)/shard_map/reshape | solution.py:230
  11.7 8.7 %all-to-all-start = ((f32[3,16,2,128]{3,2,0,1:T(2,128)}), f32[3,16,2,128]{3,2,0,1:T(2,128)S(1)}, u32[]{:S(2)}, u32[]{:S(2)}) async-start(f32[3,16,2,128]{3,2,0,1:T(2,128)} %copy.27), calls=%async_computation | async-start | bytes 98304 | tf_op jit(solution)/shard_map/all_to_all | solution.py:229
  20.5 0.7 compare_select_fusion.1
  21.2 0.6 gather_fusion
  21.8 0.6 gather_fusion.1
  22.5 0.7 and_select_fusion.1
  23.1 0.1 slice.65
  23.2 4.6 %all-to-all-done = f32[3,16,2,128]{3,2,0,1:T(2,128)S(1)} async-done(((f32[3,16,2,128]{3,2,0,1:T(2,128)}), f32[3,16,2,128]{3,2,0,1:T(2,128)S(1)}, u32[]{:S(2)}, u32[]{:S(2)}) %all-to-all-start) | async-done | bytes 49184 | tf_op jit(solution)/shard_map/all_to_all | solution.py:229
  27.8 0.6 broadcast_in_dim.4
  28.5 3.5 %all-to-all-start.1 = ((f32[3,16,2,128]{3,2,0,1:T(2,128)}), f32[3,16,2,128]{3,2,0,1:T(2,128)S(1)}, u32[]{:S(2)}, u32[]{:S(2)}) async-start(f32[3,16,2,128]{3,2,0,1:T(2,128)} %broadcast_in_dim.4), calls=%async_computation.1 | async-start | bytes 98304 | tf_op jit(solution)/shard_map/all_to_all | solution.py:232
  32.0 7.3 %all-to-all-done.1 = f32[3,16,2,128]{3,2,0,1:T(2,128)S(1)} async-done(((f32[3,16,2,128]{3,2,0,1:T(2,128)}), f32[3,16,2,128]{3,2,0,1:T(2,128)S(1)}, u32[]{:S(2)}, u32[]{:S(2)}) %all-to-all-start.1) | async-done | bytes 49184 | tf_op jit(solution)/shard_map/all_to_all | solution.py:232
  39.3 0.1 reshape.596
  39.4 0.8 %bitcast_add_fusion = f32[3,4096]{1,0:T(4,128)S(1)} fusion(f32[3,4096]{1,0:T(4,128)S(1)} %reshape.596, f32[1,3,32,128]{3,2,1,0:T(8,128)} %bitcast.60), kind=kLoop, calls=%fused_computation.46 | loop fusion | flops 12288 | bytes 147456 | tf_op jit(solution)/shard_map/add | solution.py:235
  40.3 1.0 %multiply_cosine_fusion = (f32[16,4096]{1,0:T(8,128)S(1)}, f32[16,4096]{1,0:T(8,128)S(1)}) fusion(f32[4096]{0:T(1024)S(1)} %bitcast.55, f32[16]{0:T(128)S(1)} %slice_subtract_fusion.1), kind=kLoop, calls=%fused_computation.23 | loop fusion | flops 65536 | bytes 540736 | tf_op jit(solution)/shard_map/cos | solution.py:114
  41.2 0.5 multiply_cosine_fusion.5
  41.8 1.9 %multiply_cosine_fusion.3 = (f32[8,4096]{1,0:T(8,128)S(1)}, f32[8,4096]{1,0:T(8,128)S(1)}, f32[8,4096]{1,0:T(8,128)S(1)}, f32[8,4096]{1,0:T(8,128)S(1)}, f32[8,4...) fusion(f32[8]{0:T(128)S(1)} %get-tuple-element.47, ...), kind=kLoop, calls=%fused_computation.31 | loop fusion | flops 131072 | bytes 1081440 | tf_op jit(solution)/shard_map/cos | solution.py:114
  43.7 0.6 multiply_subtract_fusion.2
  44.2 0.6 subtract_bitcast_fusion.1
  44.8 2.4 %multiply_subtract_fusion.1 = (f32[64,4,1,4096]{3,0,2,1:T(8,128)S(1)}, f32[64,4,1,4096]{3,0,2,1:T(8,128)S(1)}, f32[64,4,1,4096]{3,0,2,1:T(8,128)S(1)}, f32[64,4,1,4096]{3,0,2,1:T(8,128)S(1)}) fusion(f32[64,4096]{1,0:T(8,128)S(1)} %get-tuple-element.17, f32[4,4096]{1,0:T(4,128)S(1)} %get-tuple-element.36, f32[64,4096]{1,0:T(8,128)S(1)} %get-tuple-element.16, ...), kind=kLoop, calls=%fused_computation.15 | loop fusion | flops 12582912 | bytes 21102592 | tf_op jit(solution)/shard_map/sub | solution.py:89
  47.2 3.6 %fusion.4 = f32[64,4,2,256]{3,0,1,2:T(8,128)S(1)} fusion(f32[128,4096]{1,0:T(8,128)S(1)} %bitcast.52, f32[128,4096]{1,0:T(8,128)S(1)} %bitcast.50, f32[64,4,1,4096]{3,0,2,1:T(8,128)S(1)} %get-tuple-element.24, f32[64,4,1,4096]{3,0,2,1:T(8,128)S(1)} %get-tuple-element.25), kind=kOutput, calls=%fused_computation.7 | convolution fusion | flops 3224371200 | bytes 13107200 | tf_op jit(solution)/shard_map/xzca,da->xzcd/dot_general | solution.py:95
  51.0 6.0 %collective-permute-start = (f32[64,2,4,128]{3,0,2,1:T(8,128)S(1)}, f32[64,2,4,128]{3,0,2,1:T(8,128)S(1)}, u32[]{:S(2)}, u32[]{:S(2)}) collective-permute-start(f32[64,2,4,128]{3,0,2,1:T(8,128)S(1)} %pad_maximum_fusion.4), channel_id=1, source_target_pairs={{0,16},{16,0},{1,17},{17,1},{2,18},{18,2},{3,19},{19,3},{4,20},{20... | collective-permute-start | bytes 786440 | tf_op jit(solution)/shard_map/ppermute | solution.py:255
  57.0 3.6 %fusion = f32[64,4,2,256]{3,0,2,1:T(8,128)S(1)} fusion(f32[64,4,1,4096]{3,0,2,1:T(8,128)S(1)} %get-tuple-element.11, f32[64,4,1,4096]{3,0,2,1:T(8,128)S(1)} %get-tuple-element.10, f32[128,4096]{1,0:T(8,128)S(1)} %bitcast.53, f32[128,4096]{1,0:T(8,128)S(1)} %bitcast.51), kind=kOutput, calls=%fused_computation.2 | convolution fusion | flops 3224371200 | bytes 13107200 | tf_op jit(solution)/shard_map/xzca,da->xzcd/dot_general | solution.py:95
  60.7 0.0 collective-permute-done
  60.8 0.1 copy.35
  60.8 21.9 %all_to_all.15 = f32[16,4,2,4,128]{4,1,3,2,0:T(4,128)S(1)} all-to-all(f32[16,4,2,4,128]{4,1,3,2,0:T(4,128)S(1)} %copy.35), channel_id=1, replica_groups=mesh['atom_pairs'=16,'atom_core'=2,'loops'=16] {'atom_pairs'}, dimensions={0} | all-to-all | bytes 524288 | tf_op jit(solution)/shard_map/all_to_all | solution.py:259
  82.8 0.1 reduce_sum.19
  82.8 0.6 fusion.16
  (12 shorter events, 0.3 us)
Async XLA Ops:
  11.7 16.1 %all-to-all-start = ((f32[3,16,2,128]{3,2,0,1:T(2,128)}), f32[3,16,2,128]{3,2,0,1:T(2,128)S(1)}, u32[]{:S(2)}, u32[]{:S(2)}) async-start(f32[3,16,2,128]{3,2,0,1:T(2,128)} %copy.27), calls=%async_computation | async-start | bytes 98304 | tf_op jit(solution)/shard_map/all_to_all | solution.py:229
  28.5 10.8 %all-to-all-start.1 = ((f32[3,16,2,128]{3,2,0,1:T(2,128)}), f32[3,16,2,128]{3,2,0,1:T(2,128)S(1)}, u32[]{:S(2)}, u32[]{:S(2)}) async-start(f32[3,16,2,128]{3,2,0,1:T(2,128)} %broadcast_in_dim.4), calls=%async_computation.1 | async-start | bytes 98304 | tf_op jit(solution)/shard_map/all_to_all | solution.py:232
  51.0 9.8 %collective-permute-start = (f32[64,2,4,128]{3,0,2,1:T(8,128)S(1)}, f32[64,2,4,128]{3,0,2,1:T(8,128)S(1)}, u32[]{:S(2)}, u32[]{:S(2)}) collective-permute-start(f32[64,2,4,128]{3,0,2,1:T(8,128)S(1)} %pad_maximum_fusion.4), channel_id=1, source_target_pairs={{0,16},{16,0},{1,17},{17,1},{2,18},{18,2},{3,19},{19,3},{4,20},{20... | collective-permute-start | bytes 786440 | tf_op jit(solution)/shard_map/ppermute | solution.py:255

commit v10 on v9

--- a/solution.py
+++ b/solution.py
@@ -84,23 +84,22 @@
 
 
 def factor_block(xcosines, xsines, zcosines, zsines, ytable):
-    ywidth = ytable.shape[0] // 2
     left_real = (
         zcosines[None, :, :] * xcosines[:, None, :] - zsines[None, :, :] * xsines[:, None, :]
     )
     left_imag = (
         zcosines[None, :, :] * xsines[:, None, :] + zsines[None, :, :] * xcosines[:, None, :]
     )
-    left_pair = jnp.stack([left_real, left_imag], axis=2)
+    left_three = jnp.stack([left_real + left_imag, left_real, left_imag])
     product = jnp.einsum(
-        "xzca,da->xzcd",
-        left_pair,
+        "gxza,gda->gxzd",
+        left_three,
         ytable,
         precision=lax.Precision.HIGH,
         preferred_element_type=jnp.float32,
     )
-    real_part = product[:, :, 0, :ywidth] - product[:, :, 1, ywidth:]
-    imag_part = product[:, :, 0, ywidth:] + product[:, :, 1, :ywidth]
+    real_part = product[0] - product[2]
+    imag_part = product[0] + product[1]
     return jnp.stack([real_part, imag_part], axis=1)
 
 
@@ -128,7 +127,7 @@
 def phase_tables(position, ywaves, zwaves):
     ycosines, ysines = sincos_rows(*steps_of(ywaves), position[1])
     zangle = zwaves[:, None] * position[2][None, :]
-    ytable = jnp.concatenate([ycosines, ysines], axis=0)
+    ytable = jnp.stack([ycosines, ysines - ycosines, ycosines + ysines])
     return jnp.cos(zangle), jnp.sin(zangle), ytable
 
 

time: 83.9 us -> 106 us (1.26)
  matrix products: 7.29 us -> 21 us
  other arithmetic: 10 us -> 18.9 us
    dot_general x2, matrix products: 7.29 us -> 21 us  [factor_block(): jnp.einsum('gxza,gda->gxzd', left_three, ytable, precision=lax.Precision....]
    add x1, other arithmetic: 0.02 us -> 7.43 us  [factor_block(): left_three = jnp.stack([left_real + left_imag, left_real, left_imag])]
  transfers between devices with their start and end apart: 3 -> 3, of which waited for: 2 -> 2; matrix products, arithmetic and copies ran while one was open for 8% -> 12% of each run, Pallas kernels for 0% -> 0%
where the time goes in v10:
time: 106 us
  blocking collectives  22 us (21%)
  matrix products  21 us (20%)
  other arithmetic  18.9 us (18%)
  starting transfers between devices  18.2 us (17%)
  waiting for transfers between devices  11.9 us (11%)
  Pallas kernels  10.3 us (10%)
  local copies, waits for them, and re-layouts  3.6 us (3%)
    all_to_all x1, blocking collectives, body(): summed = lax.all_to_all(blocks, ATOM_OUTER, 0, 0, tiled=True).sum(axis=0)  22 us
    dot_general x2, matrix products, factor_block(): jnp.einsum('gxza,gda->gxzd', left_three, ytable, precision=lax.Precision....  21 us
    pallas_call x1, Pallas kernels, anchor_and_field(): pl.pallas_call(field_kernel, in_specs=[smem, smem, smem, smem, vmem], out...  10.3 us
    all_to_all x1, starting transfers between devices, body(): lax.all_to_all(field.reshape(3, loop_groups, rows, field.shape[2]), 'loop...  8.68 us
    add x1, other arithmetic, factor_block(): left_three = jnp.stack([left_real + left_imag, left_real, left_imag])  7.43 us
    all_to_all x1, waiting for transfers between devices, body(): lax.all_to_all(jnp.broadcast_to(owned[:, None], (3, loop_groups, *owned.s...  7.31 us
    ppermute x1, starting transfers between devices, body(): arrived = lax.ppermute(sent, ATOM_CORE, [(0, 1), (1, 0)])  6.03 us
    all_to_all x1, waiting for transfers between devices, body(): lax.all_to_all(field.reshape(3, loop_groups, rows, field.shape[2]), 'loop...  4.57 us
  transfers between devices with their start and end apart: 3, of which 2 were waited for; matrix products, arithmetic and copies ran while one was open for 12% of the time, Pallas kernels for 0%

profile of v10, /device:TPU:1, one launch (start us, length us, event | category | flops | bytes accessed | tf_op | source)
XLA Modules:
  0.0 106.0 jit_solution(12805426270054813112)
XLA Ops:
  0.0 10.3 %shard_map.64 = (f32[3,32,128]{2,1,0:T(8,128)}, f32[3,32,128]{2,1,0:T(8,128)}) custom-call(s32[3,256]{1,0:T(4,128)} %cells.1, s32[256]{0:T(256)} %burgers_index.1, s32[256]{0:T(256)} %habit_index.1, f32[256]{0:T(256)} %radius.1, s32[32,128]{1,0:T(8,128)} %bitcast.56), custom_call_target="tpu_custom_call" | custom-call | flops 57671680 | bytes 114688 | tf_op jit(solution)/shard_map/pallas_call | solution.py:213
  10.3 1.4 %copy.9 = f32[3,16,2,128]{3,2,0,1:T(2,128)} copy(f32[3,16,2,128]{3,2,1,0:T(2,128)} %bitcast.54) | data formatting | bytes 98304 | tf_op jit(solution)/shard_map/reshape | solution.py:229
  11.7 8.7 %all-to-all-start = ((f32[3,16,2,128]{3,2,0,1:T(2,128)}), f32[3,16,2,128]{3,2,0,1:T(2,128)S(1)}, u32[]{:S(2)}, u32[]{:S(2)}) async-start(f32[3,16,2,128]{3,2,0,1:T(2,128)} %copy.9), calls=%async_computation | async-start | bytes 98304 | tf_op jit(solution)/shard_map/all_to_all | solution.py:228
  20.5 0.7 compare_select_fusion.1
  21.2 0.6 gather_fusion.1
  21.8 0.6 gather_fusion
  22.5 0.7 and_select_fusion.1
  23.1 0.1 slice.61
  23.2 4.6 %all-to-all-done = f32[3,16,2,128]{3,2,0,1:T(2,128)S(1)} async-done(((f32[3,16,2,128]{3,2,0,1:T(2,128)}), f32[3,16,2,128]{3,2,0,1:T(2,128)S(1)}, u32[]{:S(2)}, u32[]{:S(2)}) %all-to-all-start) | async-done | bytes 49184 | tf_op jit(solution)/shard_map/all_to_all | solution.py:228
  27.8 0.6 broadcast_in_dim.4
  28.4 3.5 %all-to-all-start.1 = ((f32[3,16,2,128]{3,2,0,1:T(2,128)}), f32[3,16,2,128]{3,2,0,1:T(2,128)S(1)}, u32[]{:S(2)}, u32[]{:S(2)}) async-start(f32[3,16,2,128]{3,2,0,1:T(2,128)} %broadcast_in_dim.4), calls=%async_computation.1 | async-start | bytes 98304 | tf_op jit(solution)/shard_map/all_to_all | solution.py:231
  32.0 7.3 %all-to-all-done.1 = f32[3,16,2,128]{3,2,0,1:T(2,128)S(1)} async-done(((f32[3,16,2,128]{3,2,0,1:T(2,128)}), f32[3,16,2,128]{3,2,0,1:T(2,128)S(1)}, u32[]{:S(2)}, u32[]{:S(2)}) %all-to-all-start.1) | async-done | bytes 49184 | tf_op jit(solution)/shard_map/all_to_all | solution.py:231
  39.3 0.1 reshape.738
  39.3 0.8 bitcast_add_fusion.1
  40.2 1.0 multiply_cosine_fusion
  41.2 0.5 multiply_cosine_fusion.5
  41.8 1.9 %multiply_cosine_fusion.3 = (f32[8,4096]{1,0:T(8,128)S(1)}, f32[8,4096]{1,0:T(8,128)S(1)}, f32[8,4096]{1,0:T(8,128)S(1)}, f32[8,4096]{1,0:T(8,128)S(1)}, f32[8,4...) fusion(f32[8]{0:T(128)S(1)} %get-tuple-element.54, ...), kind=kLoop, calls=%fused_computation.36 | loop fusion | flops 131072 | bytes 1081440 | tf_op jit(solution)/shard_map/cos | solution.py:113
  43.7 0.4 multiply_subtract_fusion.2
  44.1 2.3 %bitcast_subtract_fusion = (f32[1,128,4096]{2,1,0:T(8,128)}, f32[1,128,4096]{2,1,0:T(8,128)}) fusion(f32[1,128,4096]{2,1,0:T(8,128)S(1)} %bitcast.48, f32[1,128,4096]{2,1,0:T(8,128)S(1)} %bitcast.45), kind=kLoop, calls=%fused_computation.20 | loop fusion | flops 1048576 | bytes 8388608 | tf_op jit(solution)/shard_map/sub | solution.py:130
  46.4 0.6 subtract_bitcast_fusion.1
  46.9 7.4 %fusion.22 = (f32[1,64,4,4096]{3,1,2,0:T(8,128)S(1)}, f32[1,64,4,4096]{3,1,2,0:T(8,128)}, f32[1,64,4,4096]{3,1,2,0:T(8,128)}, f32[1,64,4,4096]{3,1,2,0:T(8,128)}...) fusion(f32[64,4096]{1,0:T(8,128)S(1)} %get-tuple-element.21, f32[4,4096]{1,0:T(4,128)S(1)} %get-tuple-element.43, ...), kind=kLoop, calls=%fused_computation.67 | loop fusion | flops 14680064 | bytes 29491200 | tf_op jit(solution)/shard_map/add | solution.py:93
  54.4 11.1 %fusion.6 = f32[3,64,4,128]{3,1,2,0:T(8,128)S(1)} fusion(f32[1,64,4,4096]{3,1,2,0:T(8,128)} %get-tuple-element.31, f32[1,64,4,4096]{3,1,2,0:T(8,128)} %get-tuple-element.30, f32[1,64,4,4096]{3,1,2,0:T(8,128)} %get-tuple-element.32, f32[1,128,4096]{2,1,0:T(8,128)} %get-tuple-element.11, f32[1,128,4096]{2,1,0:T(8,128)} %get-tuple-element.10, ...), kind=kOutput, calls=%fused_computation.8 | convolution fusion | flops 2425356288 | bytes 19267584 | tf_op jit(solution)/shard_map/gxza,gda->gxzd/dot_general | solution.py:94
  65.5 0.7 pad_maximum_fusion
  66.3 6.0 %collective-permute-start = (f32[64,2,4,128]{3,0,2,1:T(8,128)}, f32[64,2,4,128]{3,0,2,1:T(8,128)}, u32[]{:S(2)}, u32[]{:S(2)}) collective-permute-start(f32[64,2,4,128]{3,0,2,1:T(8,128)} %pad_maximum_fusion), channel_id=1, source_target_pairs={{0,16},{16,0},{1,17},{17,1},{2,18},{18,2},{3,19},{19,3},{4,20},{20... | collective-permute-start | bytes 786440 | tf_op jit(solution)/shard_map/ppermute | solution.py:254
  72.3 9.9 %fusion = f32[3,64,4,128]{3,1,2,0:T(8,128)S(1)} fusion(f32[1,64,4,4096]{3,1,2,0:T(8,128)} %get-tuple-element.13, f32[1,64,4,4096]{3,1,2,0:T(8,128)} %get-tuple-element.14, f32[1,64,4,4096]{3,1,2,0:T(8,128)S(1)} %get-tuple-element.12, f32[1,128,4096]{2,1,0:T(8,128)} %get-tuple-element.11, f32[1,128,4096]{2,1,0:T(8,128)} %get-tuple-element.10, ...), kind=kOutput, calls=%fused_computation.2 | convolution fusion | flops 2425356288 | bytes 19267584 | tf_op jit(solution)/shard_map/gxza,gda->gxzd/dot_general | solution.py:94
  82.3 0.0 collective-permute-done
  82.3 1.0 maximum_add_fusion
  83.3 0.1 copy.11
  83.3 22.0 %all_to_all.15 = f32[16,4,2,4,128]{4,1,3,2,0:T(4,128)S(1)} all-to-all(f32[16,4,2,4,128]{4,1,3,2,0:T(4,128)S(1)} %copy.11), channel_id=1, replica_groups=mesh['atom_pairs'=16,'atom_core'=2,'loops'=16] {'atom_pairs'}, dimensions={0} | all-to-all | bytes 524288 | tf_op jit(solution)/shard_map/all_to_all | solution.py:258
  105.3 0.1 reduce_sum.19
  105.3 0.6 fusion.19
  (9 shorter events, 0.2 us)
Async XLA Ops:
  11.7 16.1 %all-to-all-start = ((f32[3,16,2,128]{3,2,0,1:T(2,128)}), f32[3,16,2,128]{3,2,0,1:T(2,128)S(1)}, u32[]{:S(2)}, u32[]{:S(2)}) async-start(f32[3,16,2,128]{3,2,0,1:T(2,128)} %copy.9), calls=%async_computation | async-start | bytes 98304 | tf_op jit(solution)/shard_map/all_to_all | solution.py:228
  28.4 10.8 %all-to-all-start.1 = ((f32[3,16,2,128]{3,2,0,1:T(2,128)}), f32[3,16,2,128]{3,2,0,1:T(2,128)S(1)}, u32[]{:S(2)}, u32[]{:S(2)}) async-start(f32[3,16,2,128]{3,2,0,1:T(2,128)} %broadcast_in_dim.4), calls=%async_computation.1 | async-start | bytes 98304 | tf_op jit(solution)/shard_map/all_to_all | solution.py:231
  66.3 16.0 %collective-permute-start = (f32[64,2,4,128]{3,0,2,1:T(8,128)}, f32[64,2,4,128]{3,0,2,1:T(8,128)}, u32[]{:S(2)}, u32[]{:S(2)}) collective-permute-start(f32[64,2,4,128]{3,0,2,1:T(8,128)} %pad_maximum_fusion), channel_id=1, source_target_pairs={{0,16},{16,0},{1,17},{17,1},{2,18},{18,2},{3,19},{19,3},{4,20},{20... | collective-permute-start | bytes 786440 | tf_op jit(solution)/shard_map/ppermute | solution.py:254

commit v11 on v9

--- a/solution.py
+++ b/solution.py
@@ -137,6 +137,7 @@
 STRENGTH_SCALE = 1.0 / (8.0 * (1.0 - POISSON))
 FIELD_SPLIT = 2
 FIELD_UNROLL = 2
+FIELD_SLOTS = 8
 
 
 def field_kernel(cells, burgers_index, habit_index, radius, site, anchor_out, field_out):
@@ -199,9 +200,13 @@
     zero = jnp.zeros((rows, whole.shape[1]), jnp.float32)
     start = tuple((zero, zero, zero) for _ in range(FIELD_SPLIT))
     totals = lax.fori_loop(0, radius.shape[0], one_loop, start, unroll=FIELD_UNROLL)
+    slots = field_out.shape[0] // rows
     for p in range(FIELD_SPLIT):
         for axis in range(3):
-            field_out[axis, p * rows : (p + 1) * rows] = totals[p][axis]
+            field_out[pl.ds(axis * FIELD_SPLIT + p, rows, stride=slots), :] = totals[p][axis]
+    spare = jnp.zeros((rows, whole.shape[1]), jnp.float32)
+    for slot in range(3 * FIELD_SPLIT, slots):
+        field_out[pl.ds(slot, rows, stride=slots), :] = spare
 
 
 def anchor_and_field(atom_site, loop_cells, loop_burgers, loop_habit, loop_radius):
@@ -211,11 +216,13 @@
     smem = pl.BlockSpec(memory_space=pltpu.SMEM)
     vmem = pl.BlockSpec(memory_space=pltpu.VMEM)
     shape = jax.ShapeDtypeStruct((3, *tiled.shape), jnp.float32)
+    rows = tiled.shape[0] // FIELD_SPLIT
+    chunked = jax.ShapeDtypeStruct((rows * FIELD_SLOTS, 128), jnp.float32)
     anchor, field = pl.pallas_call(
         field_kernel,
         in_specs=[smem, smem, smem, smem, vmem],
         out_specs=[vmem, vmem],
-        out_shape=[shape, shape],
+        out_shape=[shape, chunked],
         cost_estimate=pl.CostEstimate(
             flops=55 * atoms * loops, transcendentals=atoms * loops, bytes_accessed=28 * atoms
         ),
@@ -225,13 +232,13 @@
 def body(atom_site, loop_cells, loop_burgers, loop_habit, loop_radius):
     anchor, field = anchor_and_field(atom_site, loop_cells, loop_burgers, loop_habit, loop_radius)
     loop_groups = lax.axis_size("loops")
-    rows = field.shape[1] // loop_groups
-    owned = lax.all_to_all(
-        field.reshape(3, loop_groups, rows, field.shape[2]), "loops", 1, 1, tiled=True
-    ).sum(axis=1)
-    displacement = lax.all_to_all(
-        jnp.broadcast_to(owned[:, None], (3, loop_groups, *owned.shape[1:])), "loops", 1, 1, tiled=True
-    ).reshape(3, -1)
+    chunks = field.reshape(loop_groups, FIELD_SLOTS, field.shape[1])
+    owned = lax.all_to_all(chunks, "loops", 0, 0, tiled=True).sum(axis=0)
+    gathered = lax.all_to_all(
+        jnp.broadcast_to(owned[None], chunks.shape), "loops", 0, 0, tiled=True
+    )
+    used = gathered[:, : 3 * FIELD_SPLIT].reshape(loop_groups, 3, FIELD_SPLIT, field.shape[1])
+    displacement = used.transpose(1, 2, 0, 3).reshape(3, -1)
     position = anchor + displacement
     group_count = lax.axis_size((ATOM_OUTER, ATOM_CORE))
     zrows = QZ // lax.axis_size("loops")

time: 83.9 us -> 82.3 us (0.981)
  local copies, waits for them, and re-layouts: 3.61 us -> 2.12 us
    reshape x2 -> x0, local copies, waits for them, and re-layouts: 1.48 us -> none  [the longest x1 1.43 us: body(): field.reshape(3, loop_groups, rows, field.shape[2])]
where the time goes in v11:
time: 82.3 us; the launch traced here: 81.9 us
  blocking collectives  22 us (27%)
  starting transfers between devices  18.2 us (22%)
  waiting for transfers between devices  11.9 us (14%)
  Pallas kernels  10.3 us (13%)
  other arithmetic  9.92 us (12%)
  matrix products  7.29 us (9%)
  local copies, waits for them, and re-layouts  2.12 us (3%)
    all_to_all x1, blocking collectives, body(): summed = lax.all_to_all(blocks, ATOM_OUTER, 0, 0, tiled=True).sum(axis=0)  22 us
    pallas_call x1, Pallas kernels, anchor_and_field(): pl.pallas_call(field_kernel, in_specs=[smem, smem, smem, smem, vmem], out...  10.3 us
    all_to_all x1, starting transfers between devices, body(): owned = lax.all_to_all(chunks, 'loops', 0, 0, tiled=True).sum(axis=0)  8.68 us
    dot_general x2, matrix products, factor_block(): jnp.einsum('xzca,da->xzcd', left_pair, ytable, precision=lax.Precision.HI...  7.29 us
    all_to_all x1, waiting for transfers between devices, body(): lax.all_to_all(jnp.broadcast_to(owned[None], chunks.shape), 'loops', 0, 0...  6.56 us
    ppermute x1, starting transfers between devices, body(): arrived = lax.ppermute(sent, ATOM_CORE, [(0, 1), (1, 0)])  6.03 us
    all_to_all x1, waiting for transfers between devices, body(): owned = lax.all_to_all(chunks, 'loops', 0, 0, tiled=True).sum(axis=0)  5.33 us
    all_to_all x1, starting transfers between devices, body(): lax.all_to_all(jnp.broadcast_to(owned[None], chunks.shape), 'loops', 0, 0...  3.49 us
  transfers between devices with their start and end apart: 3, of which 2 were waited for; matrix products, arithmetic and copies ran while one was open for 8% of the time, Pallas kernels for 0%

profile of v11, /device:TPU:1, one launch (start us, length us, event | category | flops | bytes accessed | tf_op | source)
XLA Modules:
  0.0 81.9 jit_solution(8623505358321973952)
XLA Ops:
  0.0 10.3 %shard_map.64 = (f32[3,32,128]{2,1,0:T(8,128)}, f32[128,128]{1,0:T(8,128)}) custom-call(s32[3,256]{1,0:T(4,128)} %cells.1, s32[256]{0:T(256)} %burgers_index.1, s32[256]{0:T(256)} %habit_index.1, f32[256]{0:T(256)} %radius.1, s32[32,128]{1,0:T(8,128)} %bitcast.71), custom_call_target="tpu_custom_call" | custom-call | flops 57671680 | bytes 114688 | tf_op jit(solution)/shard_map/pallas_call | solution.py:221
  10.3 8.7 %all-to-all-start = ((f32[16,8,128]{2,1,0:T(8,128)}), f32[16,8,128]{2,1,0:T(8,128)S(1)}, u32[]{:S(2)}, u32[]{:S(2)}) async-start(f32[16,8,128]{2,1,0:T(8,128)} %bitcast.68), calls=%async_computation | async-start | bytes 131072 | tf_op jit(solution)/shard_map/all_to_all | solution.py:236
  19.0 0.7 compare_select_fusion.1
  19.8 0.6 gather_fusion
  20.4 0.6 gather_fusion.1
  21.0 5.3 %all-to-all-done = f32[16,8,128]{2,1,0:T(8,128)S(1)} async-done(((f32[16,8,128]{2,1,0:T(8,128)}), f32[16,8,128]{2,1,0:T(8,128)S(1)}, u32[]{:S(2)}, u32[]{:S(2)}) %all-to-all-start) | async-done | bytes 65568 | tf_op jit(solution)/shard_map/all_to_all | solution.py:236
  26.4 0.6 broadcast_in_dim.4
  27.0 3.5 %all-to-all-start.1 = ((f32[16,8,128]{2,1,0:T(8,128)}), f32[16,8,128]{2,1,0:T(8,128)S(1)}, u32[]{:S(2)}, u32[]{:S(2)}) async-start(f32[16,8,128]{2,1,0:T(8,128)} %broadcast_in_dim.4), calls=%async_computation.1 | async-start | bytes 131072 | tf_op jit(solution)/shard_map/all_to_all | solution.py:237
  30.5 0.7 and_select_fusion.1
  31.2 0.1 slice.69
  31.3 6.6 %all-to-all-done.1 = f32[16,8,128]{2,1,0:T(8,128)S(1)} async-done(((f32[16,8,128]{2,1,0:T(8,128)}), f32[16,8,128]{2,1,0:T(8,128)S(1)}, u32[]{:S(2)}, u32[]{:S(2)}) %all-to-all-start.1) | async-done | bytes 65568 | tf_op jit(solution)/shard_map/all_to_all | solution.py:237
  37.9 0.9 %bitcast_add_fusion = f32[3,4096]{1,0:T(4,128)S(1)} fusion(f32[1,3,32,128]{3,2,1,0:T(8,128)S(1)} %bitcast.64, f32[1,3,32,128]{3,2,1,0:T(8,128)} %bitcast.70), kind=kLoop, calls=%fused_computation.46 | loop fusion | flops 12288 | bytes 147456 | tf_op jit(solution)/shard_map/add | solution.py:242
  38.8 1.0 %multiply_cosine_fusion = (f32[16,4096]{1,0:T(8,128)S(1)}, f32[16,4096]{1,0:T(8,128)S(1)}) fusion(f32[4096]{0:T(1024)S(1)} %bitcast.65, f32[16]{0:T(128)S(1)} %slice_subtract_fusion.1), kind=kLoop, calls=%fused_computation.23 | loop fusion | flops 65536 | bytes 540736 | tf_op jit(solution)/shard_map/cos | solution.py:114
  39.8 0.5 multiply_cosine_fusion.5
  40.3 1.9 %multiply_cosine_fusion.3 = (f32[8,4096]{1,0:T(8,128)S(1)}, f32[8,4096]{1,0:T(8,128)S(1)}, f32[8,4096]{1,0:T(8,128)S(1)}, f32[8,4096]{1,0:T(8,128)S(1)}, f32[8,4...) fusion(f32[8]{0:T(128)S(1)} %get-tuple-element.47, ...), kind=kLoop, calls=%fused_computation.31 | loop fusion | flops 131072 | bytes 1081440 | tf_op jit(solution)/shard_map/cos | solution.py:114
  42.2 0.6 multiply_subtract_fusion.2
  42.8 0.4 subtract_bitcast_fusion.1
  43.2 2.5 %multiply_subtract_fusion.1 = (f32[64,4,1,4096]{3,0,2,1:T(8,128)S(1)}, f32[64,4,1,4096]{3,0,2,1:T(8,128)S(1)}, f32[64,4,1,4096]{3,0,2,1:T(8,128)S(1)}, f32[64,4,1,4096]{3,0,2,1:T(8,128)S(1)}) fusion(f32[64,4096]{1,0:T(8,128)S(1)} %get-tuple-element.17, f32[4,4096]{1,0:T(4,128)S(1)} %get-tuple-element.36, f32[64,4096]{1,0:T(8,128)S(1)} %get-tuple-element.16, ...), kind=kLoop, calls=%fused_computation.15 | loop fusion | flops 12582912 | bytes 21102592 | tf_op jit(solution)/shard_map/sub | solution.py:89
  45.7 3.6 %fusion.4 = f32[64,4,2,256]{3,0,1,2:T(8,128)S(1)} fusion(f32[128,4096]{1,0:T(8,128)S(1)} %bitcast.60, f32[128,4096]{1,0:T(8,128)S(1)} %bitcast.58, f32[64,4,1,4096]{3,0,2,1:T(8,128)S(1)} %get-tuple-element.24, f32[64,4,1,4096]{3,0,2,1:T(8,128)S(1)} %get-tuple-element.25), kind=kOutput, calls=%fused_computation.7 | convolution fusion | flops 3224371200 | bytes 13107200 | tf_op jit(solution)/shard_map/xzca,da->xzcd/dot_general | solution.py:95
  49.4 6.0 %collective-permute-start = (f32[64,2,4,128]{3,0,2,1:T(8,128)S(1)}, f32[64,2,4,128]{3,0,2,1:T(8,128)S(1)}, u32[]{:S(2)}, u32[]{:S(2)}) collective-permute-start(f32[64,2,4,128]{3,0,2,1:T(8,128)S(1)} %pad_maximum_fusion.4), channel_id=1, source_target_pairs={{0,16},{16,0},{1,17},{17,1},{2,18},{18,2},{3,19},{19,3},{4,20},{20... | collective-permute-start | bytes 786440 | tf_op jit(solution)/shard_map/ppermute | solution.py:262
  55.4 3.6 %fusion = f32[64,4,2,256]{3,0,2,1:T(8,128)S(1)} fusion(f32[64,4,1,4096]{3,0,2,1:T(8,128)S(1)} %get-tuple-element.11, f32[64,4,1,4096]{3,0,2,1:T(8,128)S(1)} %get-tuple-element.10, f32[128,4096]{1,0:T(8,128)S(1)} %bitcast.61, f32[128,4096]{1,0:T(8,128)S(1)} %bitcast.59), kind=kOutput, calls=%fused_computation.2 | convolution fusion | flops 3224371200 | bytes 13107200 | tf_op jit(solution)/shard_map/xzca,da->xzcd/dot_general | solution.py:95
  59.1 0.0 collective-permute-done
  59.2 0.1 copy.34
  59.3 22.0 %all_to_all.15 = f32[16,4,2,4,128]{4,1,3,2,0:T(4,128)S(1)} all-to-all(f32[16,4,2,4,128]{4,1,3,2,0:T(4,128)S(1)} %copy.34), channel_id=1, replica_groups=mesh['atom_pairs'=16,'atom_core'=2,'loops'=16] {'atom_pairs'}, dimensions={0} | all-to-all | bytes 524288 | tf_op jit(solution)/shard_map/all_to_all | solution.py:266
  81.2 0.1 reduce_sum.19
  81.3 0.6 fusion.16
  (12 shorter events, 0.2 us)
Async XLA Ops:
  10.3 16.1 %all-to-all-start = ((f32[16,8,128]{2,1,0:T(8,128)}), f32[16,8,128]{2,1,0:T(8,128)S(1)}, u32[]{:S(2)}, u32[]{:S(2)}) async-start(f32[16,8,128]{2,1,0:T(8,128)} %bitcast.68), calls=%async_computation | async-start | bytes 131072 | tf_op jit(solution)/shard_map/all_to_all | solution.py:236
  27.0 10.8 %all-to-all-start.1 = ((f32[16,8,128]{2,1,0:T(8,128)}), f32[16,8,128]{2,1,0:T(8,128)S(1)}, u32[]{:S(2)}, u32[]{:S(2)}) async-start(f32[16,8,128]{2,1,0:T(8,128)} %broadcast_in_dim.4), calls=%async_computation.1 | async-start | bytes 131072 | tf_op jit(solution)/shard_map/all_to_all | solution.py:237
  49.4 9.7 %collective-permute-start = (f32[64,2,4,128]{3,0,2,1:T(8,128)S(1)}, f32[64,2,4,128]{3,0,2,1:T(8,128)S(1)}, u32[]{:S(2)}, u32[]{:S(2)}) collective-permute-start(f32[64,2,4,128]{3,0,2,1:T(8,128)S(1)} %pad_maximum_fusion.4), channel_id=1, source_target_pairs={{0,16},{16,0},{1,17},{17,1},{2,18},{18,2},{3,19},{19,3},{4,20},{20... | collective-permute-start | bytes 786440 | tf_op jit(solution)/shard_map/ppermute | solution.py:262

commit v12 on v11

--- a/solution.py
+++ b/solution.py
@@ -149,9 +149,15 @@
     third = jnp.right_shift(cell, 10)
     half = 0.5 * basis.astype(jnp.float32)
     coords = [LATTICE * (c.astype(jnp.float32) + half) for c in (first, second, third)]
-    for axis in range(3):
-        anchor_out[axis] = coords[axis]
     rows = whole.shape[0] // FIELD_SPLIT
+    slots = field_out.shape[0] // rows
+    spare = jnp.zeros((rows, whole.shape[1]), jnp.float32)
+    for p in range(FIELD_SPLIT):
+        for axis in range(3):
+            piece = coords[axis][p * rows : (p + 1) * rows]
+            anchor_out[pl.ds(axis * FIELD_SPLIT + p, rows, stride=slots), :] = piece
+    for slot in range(3 * FIELD_SPLIT, slots):
+        anchor_out[pl.ds(slot, rows, stride=slots), :] = spare
     pieces = [[c[p * rows : (p + 1) * rows] for c in coords] for p in range(FIELD_SPLIT)]
 
     def one_loop(number, running):
@@ -200,11 +206,9 @@
     zero = jnp.zeros((rows, whole.shape[1]), jnp.float32)
     start = tuple((zero, zero, zero) for _ in range(FIELD_SPLIT))
     totals = lax.fori_loop(0, radius.shape[0], one_loop, start, unroll=FIELD_UNROLL)
-    slots = field_out.shape[0] // rows
     for p in range(FIELD_SPLIT):
         for axis in range(3):
             field_out[pl.ds(axis * FIELD_SPLIT + p, rows, stride=slots), :] = totals[p][axis]
-    spare = jnp.zeros((rows, whole.shape[1]), jnp.float32)
     for slot in range(3 * FIELD_SPLIT, slots):
         field_out[pl.ds(slot, rows, stride=slots), :] = spare
 
@@ -215,34 +219,36 @@
     tiled = atom_site.reshape(atoms // 128, 128)
     smem = pl.BlockSpec(memory_space=pltpu.SMEM)
     vmem = pl.BlockSpec(memory_space=pltpu.VMEM)
-    shape = jax.ShapeDtypeStruct((3, *tiled.shape), jnp.float32)
     rows = tiled.shape[0] // FIELD_SPLIT
     chunked = jax.ShapeDtypeStruct((rows * FIELD_SLOTS, 128), jnp.float32)
     anchor, field = pl.pallas_call(
         field_kernel,
         in_specs=[smem, smem, smem, smem, vmem],
         out_specs=[vmem, vmem],
-        out_shape=[shape, chunked],
+        out_shape=[chunked, chunked],
         cost_estimate=pl.CostEstimate(
             flops=55 * atoms * loops, transcendentals=atoms * loops, bytes_accessed=28 * atoms
         ),
     )(loop_cells, loop_burgers, loop_habit, loop_radius, tiled)
-    return anchor.reshape(3, atoms), field
+    return anchor, field
 
 def body(atom_site, loop_cells, loop_burgers, loop_habit, loop_radius):
     anchor, field = anchor_and_field(atom_site, loop_cells, loop_burgers, loop_habit, loop_radius)
     loop_groups = lax.axis_size("loops")
     chunks = field.reshape(loop_groups, FIELD_SLOTS, field.shape[1])
-    owned = lax.all_to_all(chunks, "loops", 0, 0, tiled=True).sum(axis=0)
+    own_anchor = lax.dynamic_index_in_dim(
+        anchor.reshape(chunks.shape), lax.axis_index("loops"), axis=0, keepdims=False
+    )
+    owned = lax.all_to_all(chunks, "loops", 0, 0, tiled=True).sum(axis=0) + own_anchor
     gathered = lax.all_to_all(
         jnp.broadcast_to(owned[None], chunks.shape), "loops", 0, 0, tiled=True
     )
-    used = gathered[:, : 3 * FIELD_SPLIT].reshape(loop_groups, 3, FIELD_SPLIT, field.shape[1])
-    displacement = used.transpose(1, 2, 0, 3).reshape(3, -1)
-    position = anchor + displacement
+    position = [
+        gathered[:, axis * FIELD_SPLIT : (axis + 1) * FIELD_SPLIT].reshape(-1) for axis in range(3)
+    ]
     group_count = lax.axis_size((ATOM_OUTER, ATOM_CORE))
     zrows = QZ // lax.axis_size("loops")
-    atom_total = position.shape[1] * group_count
+    atom_total = position[0].shape[0] * group_count
     zfirst = (lax.axis_index("loops") * zrows).astype(jnp.float32)
     zwaves = waves(zfirst, zrows, QZ, 0.0)
     ywaves = waves(jnp.float32(0.0), QY, QY, 1.0)

time: 82.3 us -> 82.1 us (level)
    add x1 -> x0, other arithmetic: 0.86 us -> none  [body(): position = anchor + displacement]
where the time goes in v12:
time: 82.1 us; the launch traced here: 81.7 us
  blocking collectives  22 us (27%)
  starting transfers between devices  18.2 us (22%)
  waiting for transfers between devices  11.9 us (14%)
  Pallas kernels  10.3 us (13%)
  other arithmetic  9.74 us (12%)
  matrix products  7.3 us (9%)
  local copies, waits for them, and re-layouts  2.09 us (3%)
    all_to_all x1, blocking collectives, body(): summed = lax.all_to_all(blocks, ATOM_OUTER, 0, 0, tiled=True).sum(axis=0)  22 us
    pallas_call x1, Pallas kernels, anchor_and_field(): pl.pallas_call(field_kernel, in_specs=[smem, smem, smem, smem, vmem], out...  10.3 us
    all_to_all x1, starting transfers between devices, body(): lax.all_to_all(chunks, 'loops', 0, 0, tiled=True).sum(axis=0) + own_anchor  8.68 us
    dot_general x2, matrix products, factor_block(): jnp.einsum('xzca,da->xzcd', left_pair, ytable, precision=lax.Precision.HI...  7.3 us
    all_to_all x1, waiting for transfers between devices, body(): lax.all_to_all(jnp.broadcast_to(owned[None], chunks.shape), 'loops', 0, 0...  6.56 us
    ppermute x1, starting transfers between devices, body(): arrived = lax.ppermute(sent, ATOM_CORE, [(0, 1), (1, 0)])  6.03 us
    all_to_all x1, waiting for transfers between devices, body(): lax.all_to_all(chunks, 'loops', 0, 0, tiled=True).sum(axis=0) + own_anchor  5.33 us
    all_to_all x1, starting transfers between devices, body(): lax.all_to_all(jnp.broadcast_to(owned[None], chunks.shape), 'loops', 0, 0...  3.49 us
  transfers between devices with their start and end apart: 3, of which 2 were waited for; matrix products, arithmetic and copies ran while one was open for 8% of the time, Pallas kernels for 0%

profile of v12, /device:TPU:1, one launch (start us, length us, event | category | flops | bytes accessed | tf_op | source)
XLA Modules:
  0.0 81.7 jit_solution(3831572482375221709)
XLA Ops:
  0.0 10.3 %shard_map.64 = (f32[128,128]{1,0:T(8,128)}, f32[128,128]{1,0:T(8,128)}) custom-call(s32[3,256]{1,0:T(4,128)} %cells.1, s32[256]{0:T(256)} %burgers_index.1, s32[256]{0:T(256)} %habit_index.1, f32[256]{0:T(256)} %radius.1, s32[32,128]{1,0:T(8,128)} %bitcast.65), custom_call_target="tpu_custom_call" | custom-call | flops 57671680 | bytes 114688 | tf_op jit(solution)/shard_map/pallas_call | solution.py:224
  10.3 8.7 %all-to-all-start = ((f32[16,8,128]{2,1,0:T(8,128)}), f32[16,8,128]{2,1,0:T(8,128)S(1)}, u32[]{:S(2)}, u32[]{:S(2)}) async-start(f32[16,8,128]{2,1,0:T(8,128)} %bitcast.62), calls=%async_computation | async-start | bytes 131072 | tf_op jit(solution)/shard_map/all_to_all | solution.py:242
  19.0 0.7 compare_select_fusion.1
  19.8 0.6 gather_fusion
  20.4 0.6 gather_fusion.1
  21.1 5.3 %all-to-all-done = f32[16,8,128]{2,1,0:T(8,128)S(1)} async-done(((f32[16,8,128]{2,1,0:T(8,128)}), f32[16,8,128]{2,1,0:T(8,128)S(1)}, u32[]{:S(2)}, u32[]{:S(2)}) %all-to-all-start) | async-done | bytes 65568 | tf_op jit(solution)/shard_map/all_to_all | solution.py:242
  26.4 0.7 fusion.17
  27.1 0.6 broadcast_in_dim.7
  27.7 3.5 %all-to-all-start.1 = ((f32[16,8,128]{2,1,0:T(8,128)}), f32[16,8,128]{2,1,0:T(8,128)S(1)}, u32[]{:S(2)}, u32[]{:S(2)}) async-start(f32[16,8,128]{2,1,0:T(8,128)} %broadcast_in_dim.7), calls=%async_computation.1 | async-start | bytes 131072 | tf_op jit(solution)/shard_map/all_to_all | solution.py:243
  31.2 0.7 and_select_fusion.1
  31.9 0.1 slice.61
  32.0 6.6 %all-to-all-done.1 = f32[16,8,128]{2,1,0:T(8,128)S(1)} async-done(((f32[16,8,128]{2,1,0:T(8,128)}), f32[16,8,128]{2,1,0:T(8,128)S(1)}, u32[]{:S(2)}, u32[]{:S(2)}) %all-to-all-start.1) | async-done | bytes 65568 | tf_op jit(solution)/shard_map/all_to_all | solution.py:243
  38.6 1.0 %multiply_cosine_fusion = (f32[16,4096]{1,0:T(8,128)S(1)}, f32[16,4096]{1,0:T(8,128)S(1)}) fusion(f32[4096]{0:T(1024)S(1)} %bitcast.59, f32[16]{0:T(128)S(1)} %slice_subtract_fusion.1), kind=kLoop, calls=%fused_computation.23 | loop fusion | flops 65536 | bytes 540736 | tf_op jit(solution)/shard_map/cos | solution.py:114
  39.5 0.5 multiply_cosine_fusion.5
  40.1 1.9 %multiply_cosine_fusion.3 = (f32[8,4096]{1,0:T(8,128)S(1)}, f32[8,4096]{1,0:T(8,128)S(1)}, f32[8,4096]{1,0:T(8,128)S(1)}, f32[8,4096]{1,0:T(8,128)S(1)}, f32[8,4...) fusion(f32[8]{0:T(128)S(1)} %get-tuple-element.47, ...), kind=kLoop, calls=%fused_computation.31 | loop fusion | flops 131072 | bytes 1081440 | tf_op jit(solution)/shard_map/cos | solution.py:114
  42.0 0.6 multiply_subtract_fusion.2
  42.6 0.4 subtract_bitcast_fusion.1
  43.0 2.5 %multiply_subtract_fusion.1 = (f32[64,4,1,4096]{3,0,2,1:T(8,128)S(1)}, f32[64,4,1,4096]{3,0,2,1:T(8,128)S(1)}, f32[64,4,1,4096]{3,0,2,1:T(8,128)S(1)}, f32[64,4,1,4096]{3,0,2,1:T(8,128)S(1)}) fusion(f32[64,4096]{1,0:T(8,128)S(1)} %get-tuple-element.17, f32[4,4096]{1,0:T(4,128)S(1)} %get-tuple-element.36, f32[64,4096]{1,0:T(8,128)S(1)} %get-tuple-element.16, ...), kind=kLoop, calls=%fused_computation.15 | loop fusion | flops 12582912 | bytes 21102592 | tf_op jit(solution)/shard_map/sub | solution.py:89
  45.5 3.6 %fusion.4 = f32[64,4,2,256]{3,0,1,2:T(8,128)S(1)} fusion(f32[128,4096]{1,0:T(8,128)S(1)} %bitcast.56, f32[128,4096]{1,0:T(8,128)S(1)} %bitcast.54, f32[64,4,1,4096]{3,0,2,1:T(8,128)S(1)} %get-tuple-element.24, f32[64,4,1,4096]{3,0,2,1:T(8,128)S(1)} %get-tuple-element.25), kind=kOutput, calls=%fused_computation.7 | convolution fusion | flops 3224371200 | bytes 13107200 | tf_op jit(solution)/shard_map/xzca,da->xzcd/dot_general | solution.py:95
  49.2 6.0 %collective-permute-start = (f32[64,2,4,128]{3,0,2,1:T(8,128)S(1)}, f32[64,2,4,128]{3,0,2,1:T(8,128)S(1)}, u32[]{:S(2)}, u32[]{:S(2)}) collective-permute-start(f32[64,2,4,128]{3,0,2,1:T(8,128)S(1)} %pad_maximum_fusion.4), channel_id=1, source_target_pairs={{0,16},{16,0},{1,17},{17,1},{2,18},{18,2},{3,19},{19,3},{4,20},{20... | collective-permute-start | bytes 786440 | tf_op jit(solution)/shard_map/ppermute | solution.py:268
  55.2 3.6 %fusion = f32[64,4,2,256]{3,0,2,1:T(8,128)S(1)} fusion(f32[64,4,1,4096]{3,0,2,1:T(8,128)S(1)} %get-tuple-element.11, f32[64,4,1,4096]{3,0,2,1:T(8,128)S(1)} %get-tuple-element.10, f32[128,4096]{1,0:T(8,128)S(1)} %bitcast.57, f32[128,4096]{1,0:T(8,128)S(1)} %bitcast.55), kind=kOutput, calls=%fused_computation.2 | convolution fusion | flops 3224371200 | bytes 13107200 | tf_op jit(solution)/shard_map/xzca,da->xzcd/dot_general | solution.py:95
  58.9 0.0 collective-permute-done
  59.0 0.1 copy.25
  59.0 22.0 %all_to_all.15 = f32[16,4,2,4,128]{4,1,3,2,0:T(4,128)S(1)} all-to-all(f32[16,4,2,4,128]{4,1,3,2,0:T(4,128)S(1)} %copy.25), channel_id=1, replica_groups=mesh['atom_pairs'=16,'atom_core'=2,'loops'=16] {'atom_pairs'}, dimensions={0} | all-to-all | bytes 524288 | tf_op jit(solution)/shard_map/all_to_all | solution.py:272
  81.0 0.1 reduce_sum.22
  81.1 0.6 fusion.16
  (11 shorter events, 0.2 us)
Async XLA Ops:
  10.3 16.1 %all-to-all-start = ((f32[16,8,128]{2,1,0:T(8,128)}), f32[16,8,128]{2,1,0:T(8,128)S(1)}, u32[]{:S(2)}, u32[]{:S(2)}) async-start(f32[16,8,128]{2,1,0:T(8,128)} %bitcast.62), calls=%async_computation | async-start | bytes 131072 | tf_op jit(solution)/shard_map/all_to_all | solution.py:242
  27.7 10.8 %all-to-all-start.1 = ((f32[16,8,128]{2,1,0:T(8,128)}), f32[16,8,128]{2,1,0:T(8,128)S(1)}, u32[]{:S(2)}, u32[]{:S(2)}) async-start(f32[16,8,128]{2,1,0:T(8,128)} %broadcast_in_dim.7), calls=%async_computation.1 | async-start | bytes 131072 | tf_op jit(solution)/shard_map/all_to_all | solution.py:243
  49.2 9.7 %collective-permute-start = (f32[64,2,4,128]{3,0,2,1:T(8,128)S(1)}, f32[64,2,4,128]{3,0,2,1:T(8,128)S(1)}, u32[]{:S(2)}, u32[]{:S(2)}) collective-permute-start(f32[64,2,4,128]{3,0,2,1:T(8,128)S(1)} %pad_maximum_fusion.4), channel_id=1, source_target_pairs={{0,16},{16,0},{1,17},{17,1},{2,18},{18,2},{3,19},{19,3},{4,20},{20... | collective-permute-start | bytes 786440 | tf_op jit(solution)/shard_map/ppermute | solution.py:268

commit v13 on v12

--- a/solution.py
+++ b/solution.py
@@ -246,7 +246,7 @@
     position = [
         gathered[:, axis * FIELD_SPLIT : (axis + 1) * FIELD_SPLIT].reshape(-1) for axis in range(3)
     ]
-    group_count = lax.axis_size((ATOM_OUTER, ATOM_CORE))
+    group_count = lax.axis_size((ATOM_HALF, ATOM_INNER))
     zrows = QZ // lax.axis_size("loops")
     atom_total = position[0].shape[0] * group_count
     zfirst = (lax.axis_index("loops") * zrows).astype(jnp.float32)
@@ -254,37 +254,35 @@
     ywaves = waves(jnp.float32(0.0), QY, QY, 1.0)
     xwaves = waves(jnp.float32(0.0), QX, QX, 1.0)
     zcosines, zsines, ytable = phase_tables(position, ywaves, zwaves)
-    outer = lax.axis_size(ATOM_OUTER)
-    core = lax.axis_index(ATOM_CORE)
-    block = QX // (2 * outer)
-    lanes = np.arange(FINE_STEPS)
-    first_side = jnp.asarray(lanes[(lanes // block) % 2 == 0], jnp.int32)
-
-    def half(side):
-        xcosines, xsines = sincos_rows(*steps_of(xwaves, first_side + block * side), position[0])
+    inner = lax.axis_size(ATOM_INNER)
+    side = lax.axis_index(ATOM_HALF)
+    xcoarse, xfine = steps_of(xwaves)
+    width = xcoarse.shape[0] // 2
+
+    def half(part):
+        coarse = lax.dynamic_slice_in_dim(xcoarse, part * width, width)
+        xcosines, xsines = sincos_rows(coarse, xfine, position[0])
         return factor_block(xcosines, xsines, zcosines, zsines, ytable)
 
-    sent = half(1 - core)
-    arrived = lax.ppermute(sent, ATOM_CORE, [(0, 1), (1, 0)])
-    kept = half(core)
+    sent = half(1 - side)
+    arrived = lax.ppermute(sent, ATOM_HALF, [(0, 1), (1, 0)])
+    kept = half(side)
     partial = kept + arrived
-    blocks = partial.reshape(outer, -1, *partial.shape[1:])
-    summed = lax.all_to_all(blocks, ATOM_OUTER, 0, 0, tiled=True).sum(axis=0)
+    blocks = partial.reshape(inner, -1, *partial.shape[1:])
+    summed = lax.all_to_all(blocks, ATOM_INNER, 0, 0, tiled=True).sum(axis=0)
     power = summed[:, 0] ** 2 + summed[:, 1] ** 2
     return jnp.log1p(jnp.transpose(power, (1, 0, 2)) / atom_total)
 
 
-ATOM_OUTER = "atom_pairs"
-ATOM_CORE = "atom_core"
+ATOM_HALF = "atom_half"
+ATOM_INNER = "atom_inner"
 
 
 def solution(mesh):
     groups, loop_groups = mesh.devices.shape
-    paired = Mesh(
-        mesh.devices.reshape(groups // 2, 2, loop_groups), (ATOM_OUTER, ATOM_CORE, "loops")
-    )
-    atoms = (ATOM_OUTER, ATOM_CORE)
+    halves = Mesh(mesh.devices.reshape(2, groups // 2, loop_groups), (ATOM_HALF, ATOM_INNER, "loops"))
+    atoms = (ATOM_HALF, ATOM_INNER)
     placed = (P(atoms), P(None, "loops"), P("loops"), P("loops"), P("loops"))
     return jax.shard_map(
-        body, mesh=paired, in_specs=placed, out_specs=P("loops", atoms, None), check_vma=False
-    )
+        body, mesh=halves, in_specs=placed, out_specs=P("loops", atoms, None), check_vma=False
+    )

time: 82.1 us -> 85.9 us (1.046)
  blocking collectives: 22 us -> 26.2 us
  waiting for transfers between devices: 11.9 us -> 14.7 us
  starting transfers between devices: 18.2 us -> 16.8 us
  local copies, waits for them, and re-layouts: 2.09 us -> 0.88 us
    all_to_all x1, blocking collectives: 22 us -> 26.2 us  [body(): summed = lax.all_to_all(blocks, ATOM_INNER, 0, 0, tiled=True).sum(axis=0)]
    all_to_all x1, waiting for transfers between devices: 5.33 us -> 7.31 us  [body(): lax.all_to_all(chunks, 'loops', 0, 0, tiled=True).sum(axis=0) + own_anchor]
    cos x0 -> x2, other arithmetic: none -> 1.64 us  [sincos_rows(): cc, sc = (jnp.cos(coarse_angle), jnp.sin(coarse_angle))]
    ppermute x1, starting transfers between devices: 6.03 us -> 4.63 us  [body(): arrived = lax.ppermute(sent, ATOM_HALF, [(0, 1), (1, 0)])]
    select_n x2 -> x0, other arithmetic: 1.33 us -> none  [steps_of(): fine = jnp.take(fine, picked)]
    gather x2 -> x0, local copies, waits for them, and re-layouts: 1.29 us -> none  [steps_of(): fine = jnp.take(fine, picked)]
    cos x2 -> x1, other arithmetic: 2.87 us -> 1.89 us  [sincos_rows(): cf, sf = (jnp.cos(fine_angle), jnp.sin(fine_angle))]
  transfers between devices with their start and end apart: 3 -> 3, of which waited for: 2 -> 3; matrix products, arithmetic and copies ran while one was open for 8% -> 5% of each run, Pallas kernels for 0% -> 0%
where the time goes in v13:
time: 85.9 us; the launch traced here: 85.5 us
  blocking collectives  26.2 us (31%)
  starting transfers between devices  16.8 us (20%)
  waiting for transfers between devices  14.7 us (17%)
  Pallas kernels  10.3 us (12%)
  other arithmetic  9.06 us (11%)
  matrix products  7.29 us (8%)
  local copies, waits for them, and re-layouts  0.88 us (1%)
    all_to_all x1, blocking collectives, body(): summed = lax.all_to_all(blocks, ATOM_INNER, 0, 0, tiled=True).sum(axis=0)  26.2 us
    pallas_call x1, Pallas kernels, anchor_and_field(): pl.pallas_call(field_kernel, in_specs=[smem, smem, smem, smem, vmem], out...  10.3 us
    all_to_all x1, starting transfers between devices, body(): lax.all_to_all(chunks, 'loops', 0, 0, tiled=True).sum(axis=0) + own_anchor  8.68 us
    all_to_all x1, waiting for transfers between devices, body(): lax.all_to_all(chunks, 'loops', 0, 0, tiled=True).sum(axis=0) + own_anchor  7.31 us
    dot_general x2, matrix products, factor_block(): jnp.einsum('xzca,da->xzcd', left_pair, ytable, precision=lax.Precision.HI...  7.29 us
    all_to_all x1, waiting for transfers between devices, body(): lax.all_to_all(jnp.broadcast_to(owned[None], chunks.shape), 'loops', 0, 0...  7.14 us
    ppermute x1, starting transfers between devices, body(): arrived = lax.ppermute(sent, ATOM_HALF, [(0, 1), (1, 0)])  4.63 us
    all_to_all x1, starting transfers between devices, body(): lax.all_to_all(jnp.broadcast_to(owned[None], chunks.shape), 'loops', 0, 0...  3.49 us
  transfers between devices with their start and end apart: 3, of which 3 were waited for; matrix products, arithmetic and copies ran while one was open for 5% of the time, Pallas kernels for 0%

profile of v13, /device:TPU:1, one launch (start us, length us, event | category | flops | bytes accessed | tf_op | source)
XLA Modules:
  0.0 85.5 jit_solution(983295188451351097)
XLA Ops:
  0.0 10.3 %shard_map.55 = (f32[128,128]{1,0:T(8,128)}, f32[128,128]{1,0:T(8,128)}) custom-call(s32[3,256]{1,0:T(4,128)} %cells.1, s32[256]{0:T(256)} %burgers_index.1, s32[256]{0:T(256)} %habit_index.1, f32[256]{0:T(256)} %radius.1, s32[32,128]{1,0:T(8,128)} %bitcast.66), custom_call_target="tpu_custom_call" | custom-call | flops 57671680 | bytes 114688 | tf_op jit(solution)/shard_map/pallas_call | solution.py:224
  10.3 8.7 %all-to-all-start = ((f32[16,8,128]{2,1,0:T(8,128)}), f32[16,8,128]{2,1,0:T(8,128)S(1)}, u32[]{:S(2)}, u32[]{:S(2)}) async-start(f32[16,8,128]{2,1,0:T(8,128)} %bitcast.63), calls=%async_computation | async-start | bytes 131072 | tf_op jit(solution)/shard_map/all_to_all | solution.py:242
  19.1 7.3 %all-to-all-done = f32[16,8,128]{2,1,0:T(8,128)S(1)} async-done(((f32[16,8,128]{2,1,0:T(8,128)}), f32[16,8,128]{2,1,0:T(8,128)S(1)}, u32[]{:S(2)}, u32[]{:S(2)}) %all-to-all-start) | async-done | bytes 65568 | tf_op jit(solution)/shard_map/all_to_all | solution.py:242
  26.4 0.7 fusion.17
  27.1 0.6 broadcast_in_dim.5
  27.7 3.5 %all-to-all-start.1 = ((f32[16,8,128]{2,1,0:T(8,128)}), f32[16,8,128]{2,1,0:T(8,128)S(1)}, u32[]{:S(2)}, u32[]{:S(2)}) async-start(f32[16,8,128]{2,1,0:T(8,128)} %broadcast_in_dim.5), calls=%async_computation.1 | async-start | bytes 131072 | tf_op jit(solution)/shard_map/all_to_all | solution.py:243
  31.3 0.1 slice.58
  31.3 0.1 fusion.21
  31.4 7.1 %all-to-all-done.1 = f32[16,8,128]{2,1,0:T(8,128)S(1)} async-done(((f32[16,8,128]{2,1,0:T(8,128)}), f32[16,8,128]{2,1,0:T(8,128)S(1)}, u32[]{:S(2)}, u32[]{:S(2)}) %all-to-all-start.1) | async-done | bytes 65568 | tf_op jit(solution)/shard_map/all_to_all | solution.py:243
  38.6 0.5 multiply_cosine_fusion.2
  39.1 1.9 %multiply_cosine_fusion = (f32[16,4096]{1,0:T(8,128)S(1)}, f32[16,4096]{1,0:T(8,128)S(1)}, f32[16,4096]{1,0:T(8,128)S(1)}, f32[16,4096]{1,0:T(8,128)S(1)}) fusion(f32[4096]{0:T(1024)S(1)} %bitcast.62, f32[16]{0:T(128)S(1)} %slice_subtract_fusion.1, f32[4096]{0:T(1024)S(1)} %bitcast.59), kind=kLoop, calls=%fused_computation.21 | loop fusion | flops 131072 | bytes 1081408 | tf_op jit(solution)/shard_map/cos | solution.py:114
  41.0 1.1 %multiply_cosine_fusion.4 = (f32[4,4096]{1,0:T(4,128)S(1)}, f32[4,4096]{1,0:T(4,128)S(1)}, f32[4,4096]{1,0:T(4,128)S(1)}, f32[4,4096]{1,0:T(4,128)S(1)}) fusion(f32[4096]{0:T(1024)S(1)} %bitcast.60, f32[4]{0:T(128)S(1)} %get-tuple-element.42, f32[4]{0:T(128)S(1)} %get-tuple-element.43), kind=kLoop, calls=%fused_computation.41 | loop fusion | flops 32768 | bytes 278560 | tf_op jit(solution)/shard_map/cos | solution.py:113
  42.1 0.5 multiply_cosine_fusion.5
  42.7 0.6 multiply_subtract_fusion.2
  43.2 0.4 multiply_subtract_fusion.4
  43.7 2.5 %multiply_subtract_fusion.1 = (f32[64,4,1,4096]{3,0,2,1:T(8,128)S(1)}, f32[64,4,1,4096]{3,0,2,1:T(8,128)S(1)}, f32[64,4,1,4096]{3,0,2,1:T(8,128)S(1)}, f32[64,4,1,4096]{3,0,2,1:T(8,128)S(1)}) fusion(f32[64,4096]{1,0:T(8,128)S(1)} %bitcast.51, f32[4,4096]{1,0:T(4,128)S(1)} %get-tuple-element.35, f32[64,4096]{1,0:T(8,128)S(1)} %bitcast.50, ...), kind=kLoop, calls=%fused_computation.13 | loop fusion | flops 12582912 | bytes 21102592 | tf_op jit(solution)/shard_map/sub | solution.py:89
  46.1 3.6 %fusion.4 = f32[64,4,2,256]{3,0,1,2:T(8,128)S(1)} fusion(f32[128,4096]{1,0:T(8,128)S(1)} %bitcast.56, f32[128,4096]{1,0:T(8,128)S(1)} %bitcast.54, f32[64,4,1,4096]{3,0,2,1:T(8,128)S(1)} %get-tuple-element.23, f32[64,4,1,4096]{3,0,2,1:T(8,128)S(1)} %get-tuple-element.24), kind=kOutput, calls=%fused_computation.5 | convolution fusion | flops 3224371200 | bytes 13107200 | tf_op jit(solution)/shard_map/xzca,da->xzcd/dot_general | solution.py:95
  49.9 4.6 %collective-permute-start = (f32[64,2,4,128]{3,0,2,1:T(8,128)S(1)}, f32[64,2,4,128]{3,0,2,1:T(8,128)S(1)}, u32[]{:S(2)}, u32[]{:S(2)}) collective-permute-start(f32[64,2,4,128]{3,0,2,1:T(8,128)S(1)} %pad_maximum_fusion.4), channel_id=1, source_target_pairs={{0,256},{256,0},{1,257},{257,1},{2,258},{258,2},{3,259},{259,3},{4... | collective-permute-start | bytes 786440 | tf_op jit(solution)/shard_map/ppermute | solution.py:268
  54.5 3.6 %fusion = f32[64,4,2,256]{3,0,2,1:T(8,128)S(1)} fusion(f32[64,4,1,4096]{3,0,2,1:T(8,128)S(1)} %get-tuple-element.10, f32[64,4,1,4096]{3,0,2,1:T(8,128)S(1)} %get-tuple-element.9, f32[128,4096]{1,0:T(8,128)S(1)} %bitcast.57, f32[128,4096]{1,0:T(8,128)S(1)} %bitcast.55), kind=kOutput, calls=%fused_computation | convolution fusion | flops 3224371200 | bytes 13107200 | tf_op jit(solution)/shard_map/xzca,da->xzcd/dot_general | solution.py:95
  58.2 0.3 collective-permute-done
  58.5 0.1 copy.18
  58.6 26.2 %all_to_all.15 = f32[16,4,2,4,128]{4,1,3,2,0:T(4,128)S(1)} all-to-all(f32[16,4,2,4,128]{4,1,3,2,0:T(4,128)S(1)} %copy.18), channel_id=1, replica_groups=mesh['atom_half'=2,'atom_inner'=16,'loops'=16] {'atom_inner'}, dimensions={0} | all-to-all | bytes 524288 | tf_op jit(solution)/shard_map/all_to_all | solution.py:272
  84.8 0.1 reduce_sum.22
  84.9 0.6 fusion.16
  (10 shorter events, 0.2 us)
Async XLA Ops:
  10.3 16.1 %all-to-all-start = ((f32[16,8,128]{2,1,0:T(8,128)}), f32[16,8,128]{2,1,0:T(8,128)S(1)}, u32[]{:S(2)}, u32[]{:S(2)}) async-start(f32[16,8,128]{2,1,0:T(8,128)} %bitcast.63), calls=%async_computation | async-start | bytes 131072 | tf_op jit(solution)/shard_map/all_to_all | solution.py:242
  27.7 10.8 %all-to-all-start.1 = ((f32[16,8,128]{2,1,0:T(8,128)}), f32[16,8,128]{2,1,0:T(8,128)S(1)}, u32[]{:S(2)}, u32[]{:S(2)}) async-start(f32[16,8,128]{2,1,0:T(8,128)} %broadcast_in_dim.5), calls=%async_computation.1 | async-start | bytes 131072 | tf_op jit(solution)/shard_map/all_to_all | solution.py:243
  49.9 8.6 %collective-permute-start = (f32[64,2,4,128]{3,0,2,1:T(8,128)S(1)}, f32[64,2,4,128]{3,0,2,1:T(8,128)S(1)}, u32[]{:S(2)}, u32[]{:S(2)}) collective-permute-start(f32[64,2,4,128]{3,0,2,1:T(8,128)S(1)} %pad_maximum_fusion.4), channel_id=1, source_target_pairs={{0,256},{256,0},{1,257},{257,1},{2,258},{258,2},{3,259},{259,3},{4... | collective-permute-start | bytes 786440 | tf_op jit(solution)/shard_map/ppermute | solution.py:268

commit v14 on v12

--- a/solution.py
+++ b/solution.py
@@ -140,7 +140,7 @@
 FIELD_SLOTS = 8
 
 
-def field_kernel(cells, burgers_index, habit_index, radius, site, anchor_out, field_out):
+def field_kernel(owner, cells, burgers_index, habit_index, radius, site, field_out):
     whole = site[...]
     basis = jnp.bitwise_and(whole, 1)
     cell = jnp.right_shift(whole, 1)
@@ -152,12 +152,6 @@
     rows = whole.shape[0] // FIELD_SPLIT
     slots = field_out.shape[0] // rows
     spare = jnp.zeros((rows, whole.shape[1]), jnp.float32)
-    for p in range(FIELD_SPLIT):
-        for axis in range(3):
-            piece = coords[axis][p * rows : (p + 1) * rows]
-            anchor_out[pl.ds(axis * FIELD_SPLIT + p, rows, stride=slots), :] = piece
-    for slot in range(3 * FIELD_SPLIT, slots):
-        anchor_out[pl.ds(slot, rows, stride=slots), :] = spare
     pieces = [[c[p * rows : (p + 1) * rows] for c in coords] for p in range(FIELD_SPLIT)]
 
     def one_loop(number, running):
@@ -206,9 +200,11 @@
     zero = jnp.zeros((rows, whole.shape[1]), jnp.float32)
     start = tuple((zero, zero, zero) for _ in range(FIELD_SPLIT))
     totals = lax.fori_loop(0, radius.shape[0], one_loop, start, unroll=FIELD_UNROLL)
+    mine = lax.broadcasted_iota(jnp.int32, spare.shape, 0) == owner[0]
     for p in range(FIELD_SPLIT):
         for axis in range(3):
-            field_out[pl.ds(axis * FIELD_SPLIT + p, rows, stride=slots), :] = totals[p][axis]
+            total = totals[p][axis] + jnp.where(mine, pieces[p][axis], spare)
+            field_out[pl.ds(axis * FIELD_SPLIT + p, rows, stride=slots), :] = total
     for slot in range(3 * FIELD_SPLIT, slots):
         field_out[pl.ds(slot, rows, stride=slots), :] = spare
 
@@ -221,25 +217,23 @@
     vmem = pl.BlockSpec(memory_space=pltpu.VMEM)
     rows = tiled.shape[0] // FIELD_SPLIT
     chunked = jax.ShapeDtypeStruct((rows * FIELD_SLOTS, 128), jnp.float32)
-    anchor, field = pl.pallas_call(
+    owner = lax.axis_index("loops").astype(jnp.int32).reshape(1)
+    field = pl.pallas_call(
         field_kernel,
-        in_specs=[smem, smem, smem, smem, vmem],
-        out_specs=[vmem, vmem],
-        out_shape=[chunked, chunked],
+        in_specs=[smem, smem, smem, smem, smem, vmem],
+        out_specs=vmem,
+        out_shape=chunked,
         cost_estimate=pl.CostEstimate(
             flops=55 * atoms * loops, transcendentals=atoms * loops, bytes_accessed=28 * atoms
         ),
-    )(loop_cells, loop_burgers, loop_habit, loop_radius, tiled)
-    return anchor, field
+    )(owner, loop_cells, loop_burgers, loop_habit, loop_radius, tiled)
+    return field
 
 def body(atom_site, loop_cells, loop_burgers, loop_habit, loop_radius):
-    anchor, field = anchor_and_field(atom_site, loop_cells, loop_burgers, loop_habit, loop_radius)
+    field = anchor_and_field(atom_site, loop_cells, loop_burgers, loop_habit, loop_radius)
     loop_groups = lax.axis_size("loops")
     chunks = field.reshape(loop_groups, FIELD_SLOTS, field.shape[1])
-    own_anchor = lax.dynamic_index_in_dim(
-        anchor.reshape(chunks.shape), lax.axis_index("loops"), axis=0, keepdims=False
-    )
-    owned = lax.all_to_all(chunks, "loops", 0, 0, tiled=True).sum(axis=0) + own_anchor
+    owned = lax.all_to_all(chunks, "loops", 0, 0, tiled=True).sum(axis=0)
     gathered = lax.all_to_all(
         jnp.broadcast_to(owned[None], chunks.shape), "loops", 0, 0, tiled=True
     )

time: 82.1 us -> 81.5 us (level)
  no operation moved by 1% of the time
where the time goes in v14:
time: 81.5 us; the launch traced here: 81.1 us
  blocking collectives  21.9 us (27%)
  starting transfers between devices  18.3 us (22%)
  waiting for transfers between devices  11.9 us (15%)
  Pallas kernels  10.4 us (13%)
  other arithmetic  9.06 us (11%)
  matrix products  7.29 us (9%)
  local copies, waits for them, and re-layouts  2.1 us (3%)
    all_to_all x1, blocking collectives, body(): summed = lax.all_to_all(blocks, ATOM_OUTER, 0, 0, tiled=True).sum(axis=0)  21.9 us
    pallas_call x1, Pallas kernels, anchor_and_field(): pl.pallas_call(field_kernel, in_specs=[smem, smem, smem, smem, smem, vmem...  10.4 us
    all_to_all x1, starting transfers between devices, body(): owned = lax.all_to_all(chunks, 'loops', 0, 0, tiled=True).sum(axis=0)  8.68 us
    dot_general x2, matrix products, factor_block(): jnp.einsum('xzca,da->xzcd', left_pair, ytable, precision=lax.Precision.HI...  7.29 us
    all_to_all x1, waiting for transfers between devices, body(): lax.all_to_all(jnp.broadcast_to(owned[None], chunks.shape), 'loops', 0, 0...  6.56 us
    ppermute x1, starting transfers between devices, body(): arrived = lax.ppermute(sent, ATOM_CORE, [(0, 1), (1, 0)])  6.08 us
    all_to_all x1, waiting for transfers between devices, body(): owned = lax.all_to_all(chunks, 'loops', 0, 0, tiled=True).sum(axis=0)  5.34 us
    all_to_all x1, starting transfers between devices, body(): lax.all_to_all(jnp.broadcast_to(owned[None], chunks.shape), 'loops', 0, 0...  3.49 us
  transfers between devices with their start and end apart: 3, of which 2 were waited for; matrix products, arithmetic and copies ran while one was open for 8% of the time, Pallas kernels for 0%

profile of v14, /device:TPU:1, one launch (start us, length us, event | category | flops | bytes accessed | tf_op | source)
XLA Modules:
  0.0 81.1 jit_solution(11117385285133386234)
XLA Ops:
  0.0 10.4 %shard_map.64 = f32[128,128]{1,0:T(8,128)} custom-call(s32[1]{0:T(128)} %bitcast.owner, s32[3,256]{1,0:T(4,128)} %cells.1, s32[256]{0:T(256)} %burgers_index.1, s32[256]{0:T(256)} %habit_index.1, f32[256]{0:T(256)} %radius.1, s32[32,128]{1,0:T(8,128)} %bitcast.58), custom_call_target="tpu_custom_call" | custom-call | flops 57671680 | bytes 114688 | tf_op jit(solution)/shard_map/pallas_call | solution.py:221
  10.4 8.7 %all-to-all-start = ((f32[16,8,128]{2,1,0:T(8,128)}), f32[16,8,128]{2,1,0:T(8,128)S(1)}, u32[]{:S(2)}, u32[]{:S(2)}) async-start(f32[16,8,128]{2,1,0:T(8,128)} %bitcast.56), calls=%async_computation | async-start | bytes 131072 | tf_op jit(solution)/shard_map/all_to_all | solution.py:236
  19.1 0.7 compare_select_fusion.1
  19.8 0.6 gather_fusion
  20.5 0.6 gather_fusion.1
  21.1 5.3 %all-to-all-done = f32[16,8,128]{2,1,0:T(8,128)S(1)} async-done(((f32[16,8,128]{2,1,0:T(8,128)}), f32[16,8,128]{2,1,0:T(8,128)S(1)}, u32[]{:S(2)}, u32[]{:S(2)}) %all-to-all-start) | async-done | bytes 65568 | tf_op jit(solution)/shard_map/all_to_all | solution.py:236
  26.5 0.6 broadcast_in_dim.4
  27.1 3.5 %all-to-all-start.1 = ((f32[16,8,128]{2,1,0:T(8,128)}), f32[16,8,128]{2,1,0:T(8,128)S(1)}, u32[]{:S(2)}, u32[]{:S(2)}) async-start(f32[16,8,128]{2,1,0:T(8,128)} %broadcast_in_dim.4), calls=%async_computation.1 | async-start | bytes 131072 | tf_op jit(solution)/shard_map/all_to_all | solution.py:237
  30.6 0.7 and_select_fusion.1
  31.3 0.1 slice.61
  31.4 6.6 %all-to-all-done.1 = f32[16,8,128]{2,1,0:T(8,128)S(1)} async-done(((f32[16,8,128]{2,1,0:T(8,128)}), f32[16,8,128]{2,1,0:T(8,128)S(1)}, u32[]{:S(2)}, u32[]{:S(2)}) %all-to-all-start.1) | async-done | bytes 65568 | tf_op jit(solution)/shard_map/all_to_all | solution.py:237
  38.0 1.0 %multiply_cosine_fusion = (f32[16,4096]{1,0:T(8,128)S(1)}, f32[16,4096]{1,0:T(8,128)S(1)}) fusion(f32[4096]{0:T(1024)S(1)} %bitcast.53, f32[16]{0:T(128)S(1)} %slice_subtract_fusion.1), kind=kLoop, calls=%fused_computation.23 | loop fusion | flops 65536 | bytes 540736 | tf_op jit(solution)/shard_map/cos | solution.py:114
  39.0 0.5 multiply_cosine_fusion.5
  39.5 1.9 %multiply_cosine_fusion.3 = (f32[8,4096]{1,0:T(8,128)S(1)}, f32[8,4096]{1,0:T(8,128)S(1)}, f32[8,4096]{1,0:T(8,128)S(1)}, f32[8,4096]{1,0:T(8,128)S(1)}, f32[8,4...) fusion(f32[8]{0:T(128)S(1)} %get-tuple-element.43, ...), kind=kLoop, calls=%fused_computation.31 | loop fusion | flops 131072 | bytes 1081440 | tf_op jit(solution)/shard_map/cos | solution.py:114
  41.4 0.6 multiply_subtract_fusion.2
  42.0 0.4 subtract_bitcast_fusion.1
  42.4 2.5 %multiply_subtract_fusion.1 = (f32[64,4,1,4096]{3,0,2,1:T(8,128)S(1)}, f32[64,4,1,4096]{3,0,2,1:T(8,128)S(1)}, f32[64,4,1,4096]{3,0,2,1:T(8,128)S(1)}, f32[64,4,1,4096]{3,0,2,1:T(8,128)S(1)}) fusion(f32[64,4096]{1,0:T(8,128)S(1)} %get-tuple-element.13, f32[4,4096]{1,0:T(4,128)S(1)} %get-tuple-element.32, f32[64,4096]{1,0:T(8,128)S(1)} %get-tuple-element.12, ...), kind=kLoop, calls=%fused_computation.15 | loop fusion | flops 12582912 | bytes 21102592 | tf_op jit(solution)/shard_map/sub | solution.py:89
  44.9 3.6 %fusion.4 = f32[64,4,2,256]{3,0,1,2:T(8,128)S(1)} fusion(f32[128,4096]{1,0:T(8,128)S(1)} %bitcast.50, f32[128,4096]{1,0:T(8,128)S(1)} %bitcast.48, f32[64,4,1,4096]{3,0,2,1:T(8,128)S(1)} %get-tuple-element.20, f32[64,4,1,4096]{3,0,2,1:T(8,128)S(1)} %get-tuple-element.21), kind=kOutput, calls=%fused_computation.7 | convolution fusion | flops 3224371200 | bytes 13107200 | tf_op jit(solution)/shard_map/xzca,da->xzcd/dot_general | solution.py:95
  48.6 6.1 %collective-permute-start = (f32[64,2,4,128]{3,0,2,1:T(8,128)S(1)}, f32[64,2,4,128]{3,0,2,1:T(8,128)S(1)}, u32[]{:S(2)}, u32[]{:S(2)}) collective-permute-start(f32[64,2,4,128]{3,0,2,1:T(8,128)S(1)} %pad_maximum_fusion.4), channel_id=1, source_target_pairs={{0,16},{16,0},{1,17},{17,1},{2,18},{18,2},{3,19},{19,3},{4,20},{20... | collective-permute-start | bytes 786440 | tf_op jit(solution)/shard_map/ppermute | solution.py:262
  54.7 3.6 %fusion = f32[64,4,2,256]{3,0,2,1:T(8,128)S(1)} fusion(f32[64,4,1,4096]{3,0,2,1:T(8,128)S(1)} %get-tuple-element.7, f32[64,4,1,4096]{3,0,2,1:T(8,128)S(1)} %get-tuple-element.6, f32[128,4096]{1,0:T(8,128)S(1)} %bitcast.51, f32[128,4096]{1,0:T(8,128)S(1)} %bitcast.49), kind=kOutput, calls=%fused_computation.2 | convolution fusion | flops 3224371200 | bytes 13107200 | tf_op jit(solution)/shard_map/xzca,da->xzcd/dot_general | solution.py:95
  58.4 0.0 collective-permute-done
  58.4 0.1 copy.25
  58.5 21.9 %all_to_all.15 = f32[16,4,2,4,128]{4,1,3,2,0:T(4,128)S(1)} all-to-all(f32[16,4,2,4,128]{4,1,3,2,0:T(4,128)S(1)} %copy.25), channel_id=1, replica_groups=mesh['atom_pairs'=16,'atom_core'=2,'loops'=16] {'atom_pairs'}, dimensions={0} | all-to-all | bytes 524288 | tf_op jit(solution)/shard_map/all_to_all | solution.py:266
  80.4 0.1 reduce_sum.19
  80.5 0.6 fusion.16
  (11 shorter events, 0.2 us)
Async XLA Ops:
  10.4 16.1 %all-to-all-start = ((f32[16,8,128]{2,1,0:T(8,128)}), f32[16,8,128]{2,1,0:T(8,128)S(1)}, u32[]{:S(2)}, u32[]{:S(2)}) async-start(f32[16,8,128]{2,1,0:T(8,128)} %bitcast.56), calls=%async_computation | async-start | bytes 131072 | tf_op jit(solution)/shard_map/all_to_all | solution.py:236
  27.1 10.8 %all-to-all-start.1 = ((f32[16,8,128]{2,1,0:T(8,128)}), f32[16,8,128]{2,1,0:T(8,128)S(1)}, u32[]{:S(2)}, u32[]{:S(2)}) async-start(f32[16,8,128]{2,1,0:T(8,128)} %broadcast_in_dim.4), calls=%async_computation.1 | async-start | bytes 131072 | tf_op jit(solution)/shard_map/all_to_all | solution.py:237
  48.6 9.8 %collective-permute-start = (f32[64,2,4,128]{3,0,2,1:T(8,128)S(1)}, f32[64,2,4,128]{3,0,2,1:T(8,128)S(1)}, u32[]{:S(2)}, u32[]{:S(2)}) collective-permute-start(f32[64,2,4,128]{3,0,2,1:T(8,128)S(1)} %pad_maximum_fusion.4), channel_id=1, source_target_pairs={{0,16},{16,0},{1,17},{17,1},{2,18},{18,2},{3,19},{19,3},{4,20},{20... | collective-permute-start | bytes 786440 | tf_op jit(solution)/shard_map/ppermute | solution.py:262
